TPU v7x, 32 devices: a whole 2x2x4 slice. The times are simulated.
32 devices in a mesh: gx: 2 (over core), gy: 2 (over x), gz: 8 (over z, y).
Axes of the slice: x: 2, y: 2, z: 4, core: 2. Of those that a mesh axis runs over, the one named last changes fastest.
Arguments:
- phase_field: float32 [256, 128, 256], P('gz', 'gx', 'gy'), may hold values from -3 to 3
- centres: float32 [4], replicated, may hold values from -0.8 to 0.8
- widths: float32 [4], replicated, may hold values from 0.15 to 0.5
- densities: float32 [4], replicated, may hold values from 0.5 to 3
- colours: float32 [3, 4], replicated, may hold values from 0 to 1
Outputs:
- picture: float32 [4, 128, 256], P(None, ('gx', 'gz'), 'gy')
All inputs are finite; a program needn't handle non-finite values.
Results may differ from a plain program's by a relative error of at most 0.0003.
Values sent between devices are 32-bit elements; how exact they have to be, the bound alone decides.
No kernel may reach another device: no remote copies, remote signals or barrier semaphores. Data moves between devices by JAX's collectives and lax.ppermute only.
A program may use at most 64 MiB of HBM per device.

v0:
```python
import jax
import jax.numpy as jnp
from jax import lax
from jax.sharding import PartitionSpec as P

STEPS = 4
MATERIALS = 4


KAPPA = 0.5
RATE_DEPTH = 0.3
RATE_PLANE = 0.09


def with_halo(x, sides, width):
    for axis, dim in sides:
        size, length = (lax.axis_size(axis), x.shape[dim])
        up = [(i, (i + 1) % size) for i in range(size - 1)]
        down = [(j, i) for i, j in up]
        last = lax.slice_in_dim(x, length - width, length, axis=dim)
        first = lax.slice_in_dim(x, 0, width, axis=dim)
        before = lax.ppermute(last, axis, up)
        after = lax.ppermute(first, axis, down)
        x = jnp.concatenate([before, x, after], axis=dim)
    return x


def swapped(x, axis, bit):
    return lax.ppermute(x, axis, [(i, i ^ 1 << bit) for i in range(lax.axis_size(axis))])


def neighbour_flux(padded, centre, dim_index, shift_by, weight):
    selector = [slice(1, -1), slice(1, -1), slice(1, -1)]
    selector[dim_index] = slice(shift_by, padded.shape[dim_index] - 2 + shift_by)
    differ = padded[tuple(selector)] - centre
    return weight * differ / (1.0 + (differ / KAPPA) ** 2)


def smooth_valid(padded):
    centre = padded[1:-1, 1:-1, 1:-1]
    updated = centre
    for dim_index, weight in ((0, RATE_DEPTH), (1, RATE_PLANE), (2, RATE_PLANE)):
        for shift_by in (0, 2):
            updated = updated + neighbour_flux(padded, centre, dim_index, shift_by, weight)
    return updated


def edge_ones(first_cell, length, upper_limit):
    coords = first_cell + jnp.arange(length, dtype=jnp.int32)
    return ((coords >= 0) & (coords < upper_limit)).astype(jnp.float32)


def inside_mask(depth_cells, row_cells, col_cells, margin):
    along_depth = edge_ones(
        lax.axis_index("gz") * depth_cells - margin,
        depth_cells + 2 * margin,
        depth_cells * lax.axis_size("gz"),
    )
    along_rows = edge_ones(
        lax.axis_index("gx") * row_cells - margin,
        row_cells + 2 * margin,
        row_cells * lax.axis_size("gx"),
    )
    along_cols = edge_ones(
        lax.axis_index("gy") * col_cells - margin,
        col_cells + 2 * margin,
        col_cells * lax.axis_size("gy"),
    )
    return along_depth[:, None, None] * along_rows[None, :, None] * along_cols[None, None, :]


def optics(values, centres, widths, densities, colours):
    bump_list = [
        densities[material] * jnp.exp(-(((values - centres[material]) / widths[material]) ** 2))
        for material in range(MATERIALS)
    ]
    extinct = sum(bump_list)
    emitted = jnp.stack(
        [
            sum((colours[channel, material] * bump_list[material] for material in range(MATERIALS)))
            for channel in range(3)
        ]
    )
    return (extinct, emitted)


def composite_over(nearer, farther, chan_axis):
    near_rad = lax.slice_in_dim(nearer, 0, 3, axis=chan_axis)
    near_through = lax.slice_in_dim(nearer, 3, 4, axis=chan_axis)
    far_rad = lax.slice_in_dim(farther, 0, 3, axis=chan_axis)
    far_through = lax.slice_in_dim(farther, 3, 4, axis=chan_axis)
    return jnp.concatenate(
        [near_rad + near_through * far_rad, near_through * far_through], axis=chan_axis
    )


def shards(phase_field, centres, widths, densities, colours):
    depth_cells, row_cells, col_cells = phase_field.shape
    padded = with_halo(phase_field, (("gx", 1), ("gy", 2), ("gz", 0)), STEPS)
    for repeat in range(STEPS):
        margin = STEPS - repeat - 1
        padded = smooth_valid(padded) * inside_mask(depth_cells, row_cells, col_cells, margin)
    extinct, emitted = optics(padded, centres, widths, densities, colours)
    step_len = 1.0 / (depth_cells * lax.axis_size("gz"))
    positions = jnp.arange(depth_cells, dtype=jnp.int32)
    strictly_lower = (positions[:, None] > positions[None, :]).astype(jnp.float32)
    running = jnp.einsum("ab,bxy->axy", strictly_lower, extinct, precision=lax.Precision.HIGHEST)
    through = jnp.exp(-step_len * running)
    radiance = step_len * jnp.sum(through[None] * emitted, axis=1)
    seg_through = jnp.exp(-step_len * jnp.sum(extinct, axis=0))
    segment = jnp.concatenate([radiance, seg_through[None]], axis=0)
    depth_count = lax.axis_size("gz")
    rows_part = row_cells // depth_count
    levels = depth_count.bit_length() - 1
    partial_value = segment.reshape((4,) + (2,) * levels + (rows_part, col_cells))
    for bit_level in range(levels):
        dim_at = levels - bit_level
        lower_half = jnp.take(partial_value, 0, axis=dim_at)
        upper_half = jnp.take(partial_value, 1, axis=dim_at)
        is_behind = jnp.bitwise_and(jnp.right_shift(lax.axis_index("gz"), bit_level), 1) == 1
        kept_half = jnp.where(is_behind, upper_half, lower_half)
        sent_half = jnp.where(is_behind, lower_half, upper_half)
        arrived = swapped(sent_half, "gz", bit_level)
        partial_value = composite_over(
            jnp.where(is_behind, arrived, kept_half), jnp.where(is_behind, kept_half, arrived), 0
        )
    return jnp.concatenate([partial_value[:3], 1.0 - partial_value[3:4]], axis=0)


def solution(mesh):
    placed = (P("gz", "gx", "gy"), P(), P(), P(), P())
    return jax.shard_map(
        shards, mesh=mesh, in_specs=placed, out_specs=P(None, ("gx", "gz"), "gy"), check_vma=False
    )
```

profile of v0, /device:TPU:0, one launch (start us, length us, event | category | flops | bytes accessed | tf_op | source)
XLA Modules:
  0.0 124.2 jit_solution(7431676522352942093)
XLA Ops:
  1.0 2.4 %collective-permute-start = (f32[32,4,128]{2,0,1:T(8,128)S(1)}, f32[32,4,128]{2,0,1:T(8,128)S(1)}, u32[]{:S(2)}, u32[]{:S(2)}) collective-permute-start(f32[32,4,128]{2,0,1:T(8,128)S(1)} %copy.60), channel_id=1, source_target_pairs={{0,16},{1,17},{2,18},{3,19},{4,20},{5,21},{6,22},{7,23},{8,24},{9,... | collective-permute-start | bytes 196616 | tf_op jit(solution)/shard_map/ppermute | solution.py:22
  3.4 1.3 %collective-permute-start.1 = (f32[32,4,128]{2,0,1:T(8,128)S(1)}, f32[32,4,128]{2,0,1:T(8,128)S(1)}, u32[]{:S(2)}, u32[]{:S(2)}) collective-permute-start(f32[32,4,128]{2,0,1:T(8,128)S(1)} %copy.61), channel_id=1, source_target_pairs={{16,0},{17,1},{18,2},{19,3},{20,4},{21,5},{22,6},{23,7},{24,8},{25... | collective-permute-start | bytes 196616 | tf_op jit(solution)/shard_map/ppermute | solution.py:23
  5.4 1.5 %fusion.22 = (f32[1]{0:T(128)}, f32[1]{0:T(128)}, f32[1]{0:T(128)}, f32[1]{0:T(128)}) fusion(f32[4]{0:T(128)} %param.20), kind=kLoop, calls=%fused_computation.116 | loop fusion | bytes 32 | tf_op jit(solution)/shard_map/slice | solution.py:74
  6.9 1.5 %fusion.23 = (f32[1]{0:T(128)}, f32[1]{0:T(128)}, f32[1]{0:T(128)}, f32[1]{0:T(128)}) fusion(f32[4]{0:T(128)} %param.18), kind=kLoop, calls=%fused_computation.117 | loop fusion | bytes 32 | tf_op jit(solution)/shard_map/slice | solution.py:74
  8.3 1.5 %fusion.24 = (f32[1]{0:T(128)}, f32[1]{0:T(128)}, f32[1]{0:T(128)}, f32[1]{0:T(128)}) fusion(f32[4]{0:T(128)} %param.19), kind=kLoop, calls=%fused_computation.118 | loop fusion | bytes 32 | tf_op jit(solution)/shard_map/slice | solution.py:74
  12.6 1.3 %pad_maximum_fusion.1 = f32[32,72,128]{2,1,0:T(8,128)S(1)} fusion(f32[32,4,128]{2,1,0:T(4,128)S(1)} %copy.40, f32[32,64,128]{2,1,0:T(8,128)} %param.17, f32[32,4,128]{2,1,0:T(4,128)S(1)} %copy.39), kind=kLoop, calls=%fused_computation.26 | loop fusion | flops 589824 | bytes 2359296 | tf_op jit(solution)/shard_map/concatenate | solution.py:24
  15.4 4.2 %collective-permute-start.2 = (f32[32,72,4]{1,0,2:T(8,128)}, f32[32,72,4]{1,0,2:T(8,128)S(1)}, u32[]{:S(2)}, u32[]{:S(2)}) collective-permute-start(f32[32,72,4]{1,0,2:T(8,128)} %copy.41), channel_id=1, source_target_pairs={{0,8},{1,9},{2,10},{3,11},{4,12},{5,13},{6,14},{7,15},{16,24},{17,... | collective-permute-start | bytes 110600 | tf_op jit(solution)/shard_map/ppermute | solution.py:22
  20.0 1.3 %collective-permute-start.3 = (f32[32,72,4]{1,0,2:T(8,128)S(1)}, f32[32,72,4]{1,0,2:T(8,128)}, u32[]{:S(2)}, u32[]{:S(2)}) collective-permute-start(f32[32,72,4]{1,0,2:T(8,128)S(1)} %copy.42), channel_id=1, source_target_pairs={{8,0},{9,1},{10,2},{11,3},{12,4},{13,5},{14,6},{15,7},{24,16},{25,... | collective-permute-start | bytes 110600 | tf_op jit(solution)/shard_map/ppermute | solution.py:23
  22.6 4.2 %collective-permute-done.3 = f32[32,72,4]{1,0,2:T(8,128)} collective-permute-done((f32[32,72,4]{1,0,2:T(8,128)S(1)}, f32[32,72,4]{1,0,2:T(8,128)}, u32[]{:S(2)}, u32[]{:S(2)}) %collective-permute-start.3) | collective-permute-done | bytes 36896 | tf_op jit(solution)/shard_map/ppermute | solution.py:23
  26.8 1.3 %copy.44 = f32[32,72,4]{2,1,0:T(8,128)S(1)} copy(f32[32,72,4]{1,0,2:T(8,128)} %collective-permute-done.3) | data formatting | bytes 73728 | tf_op jit(solution)/shard_map/ppermute | solution.py:23
  29.3 1.8 %copy.45 = f32[4,72,136]{1,2,0:T(8,128)} copy(f32[4,72,136]{2,1,0:T(8,128)} %get-tuple-element.81) | data formatting | bytes 313344 | tf_op jit(solution)/shard_map/slice | solution.py:20
  31.1 4.1 %collective-permute-start.4 = (f32[4,72,136]{1,2,0:T(8,128)}, f32[4,72,136]{1,2,0:T(8,128)}, u32[]{:S(2)}, u32[]{:S(2)}) collective-permute-start(f32[4,72,136]{1,2,0:T(8,128)} %copy.45), channel_id=1, source_target_pairs={{0,1},{1,2},{2,3},{3,4},{4,5},{5,6},{6,7},{8,9},{9,10},{10,11},{11... | collective-permute-start | bytes 470024 | tf_op jit(solution)/shard_map/ppermute | solution.py:22
  35.3 1.9 %copy.46 = f32[4,72,136]{1,2,0:T(8,128)} copy(f32[4,72,136]{2,1,0:T(8,128)} %get-tuple-element.82) | data formatting | bytes 313344 | tf_op jit(solution)/shard_map/slice | solution.py:21
  37.1 1.5 %collective-permute-start.5 = (f32[4,72,136]{1,2,0:T(8,128)}, f32[4,72,136]{1,2,0:T(8,128)}, u32[]{:S(2)}, u32[]{:S(2)}) collective-permute-start(f32[4,72,136]{1,2,0:T(8,128)} %copy.46), channel_id=1, source_target_pairs={{1,0},{2,1},{3,2},{4,3},{5,4},{6,5},{7,6},{9,8},{10,9},{11,10},{12... | collective-permute-start | bytes 470024 | tf_op jit(solution)/shard_map/ppermute | solution.py:23
  39.1 1.8 %fusion.21 = (f32[1,1]{1,0:T(1,128)}, f32[1,1]{1,0:T(1,128)}, f32[1,1]{1,0:T(1,128)}, f32[1,1]{1,0:T(1,128)}, f32[1,1]{1,0:T(1,128)}, /*index=5*/f32[1,1]{1,0:T(...) fusion(f32[3,4]{1,0:T(4,128)} %param.21), kind=kLoop, calls=%fused_computation.115 | loop fusion | bytes 96 | tf_op jit(solution)/shard_map/slice | solution.py:80
  41.1 1.9 %copy.47 = f32[4,72,136]{2,1,0:T(8,128)} copy(f32[4,72,136]{1,2,0:T(8,128)} %collective-permute-done.4) | data formatting | bytes 313344 | tf_op jit(solution)/shard_map/ppermute | solution.py:22
  42.9 4.6 %collective-permute-done.5 = f32[4,72,136]{1,2,0:T(8,128)} collective-permute-done((f32[4,72,136]{1,2,0:T(8,128)}, f32[4,72,136]{1,2,0:T(8,128)}, u32[]{:S(2)}, u32[]{:S(2)}) %collective-permute-start.5) | collective-permute-done | bytes 156704 | tf_op jit(solution)/shard_map/ppermute | solution.py:23
  47.6 1.9 %copy.48 = f32[4,72,136]{2,1,0:T(8,128)} copy(f32[4,72,136]{1,2,0:T(8,128)} %collective-permute-done.5) | data formatting | bytes 313344 | tf_op jit(solution)/shard_map/ppermute | solution.py:23
  49.4 2.2 %pad_maximum_fusion = f32[40,72,136]{2,1,0:T(8,128)S(1)} fusion(f32[4,72,136]{2,1,0:T(8,128)} %copy.48, f32[32,72,4]{2,1,0:T(8,128)S(1)} %copy.44, f32[32,4,128]{2,1,0:T(4,128)S(1)} %copy.40, f32[32,64,128]{2,1,0:T(8,128)S(1)} %copy-done, f32[32,4,128]{2,1,0:T(4,128)S(1)} %copy.39, f32[32,72,4]{2,1,0:T(8,128)S(1)} %copy.43, f32[4,72,136]{2,1,0:T(8,128)} %copy.47), kind=kLoop, calls=%fused_computation.2 | loop fusion | flops 2350080 | bytes 3133440 | tf_op jit(solution)/shard_map/concatenate | solution.py:24
  51.7 6.5 %multiply_multiply_fusion = f32[38,70,134]{2,1,0:T(8,128)S(1)} fusion(f32[40,72,136]{2,1,0:T(8,128)S(1)} %pad_maximum_fusion, f32[134]{0:T(256)S(1)} %copy-done.4, f32[38,70]{1,0:T(8,128)S(1)} %copy-done.3), kind=kLoop, calls=%fused_computation.9 | loop fusion | flops 15683360 | bytes 11417256 | tf_op jit(solution)/shard_map/mul | solution.py:102
  58.2 6.2 %multiply_multiply_fusion.1 = f32[36,68,132]{2,1,0:T(8,128)S(1)} fusion(f32[38,70,134]{2,1,0:T(8,128)S(1)} %multiply_multiply_fusion, f32[132]{0:T(256)S(1)} %copy-done.5, f32[36,68]{1,0:T(8,128)S(1)} %copy-done.1), kind=kLoop, calls=%fused_computation.16 | loop fusion | flops 14217984 | bytes 10350672 | tf_op jit(solution)/shard_map/mul | solution.py:102
  64.4 6.1 %multiply_multiply_fusion.2 = f32[34,66,130]{2,1,0:T(8,128)S(1)} fusion(f32[36,68,132]{2,1,0:T(8,128)S(1)} %multiply_multiply_fusion.1, f32[130]{0:T(256)S(1)} %copy-done.6, f32[34,66]{1,0:T(8,128)S(1)} %copy-done.2), kind=kLoop, calls=%fused_computation.23 | loop fusion | flops 12835680 | bytes 9344536 | tf_op jit(solution)/shard_map/mul | solution.py:102
  70.5 14.3 %add_bitcast_fusion.2 = (f32[1,32,64,128]{3,2,1,0:T(8,128)S(1)}, f32[32,64,128]{2,1,0:T(8,128)S(1)}) fusion(f32[]{:T(128)} %bitcast.16, f32[]{:T(128)} %bitcast.15, f32[]{:T(128)} %bitcast.14, f32[]{:T(128)} %bitcast.13, f32[]{:T(128)} %bitcast.3, f32[]{:T(128)} %bitcast.2, f32[]{:T(128)} %bitcast.1, f32[]{:T(128)} %bitcast.6, f32[]{:T(128)} %bitcast.5, ...), kind=kLoop, calls=%fused_computation.36 | loop fusion | flops 18612224 | bytes 9445952 | tf_op jit(solution)/shard_map/stack | solution.py:78
  84.8 11.2 %fusion.18 = (f32[64,128]{1,0:T(8,128)S(1)}, f32[32,64,128]{2,1,0:T(8,128)S(1)}, f32[1,32,64,128]{3,2,1,0:T(8,128)S(1)}) fusion(f32[]{:T(128)} %bitcast.12, f32[32,64,128]{2,1,0:T(8,128)S(1)} %get-tuple-element.78, f32[]{:T(128)} %bitcast.11, f32[]{:T(128)} %bitcast.10, f32[]{:T(128)} %bitcast.9, f32[]{:T(128)} %bitcast.8, f32[]{:T(128)} %bitcast.7, ...), kind=kLoop, calls=%fused_computation.112 | loop fusion | flops 8118272 | bytes 3178560 | tf_op jit(solution)/shard_map/reduce_sum | solution.py:110
  96.0 1.3 %fusion.1 = f32[32,64,128]{2,0,1:T(8,128)S(1)} fusion(f32[32,64,128]{2,1,0:T(8,128)S(1)} %get-tuple-element.80), kind=kOutput, calls=%fused_computation.25 | convolution fusion | flops 100926464 | bytes 2097152 | tf_op jit(solution)/shard_map/ab,bxy->axy/dot_general | solution.py:107
  98.0 11.1 %add_bitcast_fusion = f32[1,32,64,128]{3,2,1,0:T(8,128)S(1)} fusion(f32[]{:T(128)} %bitcast.26, f32[]{:T(128)} %bitcast.25, f32[]{:T(128)} %bitcast.24, f32[]{:T(128)} %bitcast.23, f32[]{:T(128)} %bitcast.3, f32[32,64,128]{2,1,0:T(8,128)S(1)} %get-tuple-element.78, f32[]{:T(128)} %bitcast.2, f32[]{:T(128)} %bitcast.1, f32[]{:T(128)} %bitcast.6, f32[]{:T(128)} %bitcast.5, ...), kind=kLoop, calls=%fused_computation.34 | loop fusion | flops 7077888 | bytes 2097216 | tf_op jit(solution)/shard_map/stack | solution.py:78
  109.6 1.8 %collective-permute-start.6 = (f32[4,2,2,8,128]{4,3,2,1,0:T(8,128)S(1)}, f32[4,2,2,8,128]{4,3,2,1,0:T(8,128)S(1)}, u32[]{:S(2)}, u32[]{:S(2)}) collective-permute-start(f32[4,2,2,8,128]{4,3,2,1,0:T(8,128)S(1)} %broadcast_select_fusion.3), channel_id=1, source_target_pairs={{0,1},{1,0},{2,3},{3,2},{4,5},{5,4},{6,7},{7,6},{8,9},{9,8},{10,11... | collective-permute-start | bytes 196616 | tf_op jit(solution)/shard_map/ppermute | solution.py:29
  111.4 2.5 %collective-permute-done.6 = f32[4,2,2,8,128]{4,3,2,1,0:T(8,128)S(1)} collective-permute-done((f32[4,2,2,8,128]{4,3,2,1,0:T(8,128)S(1)}, f32[4,2,2,8,128]{4,3,2,1,0:T(8,128)S(1)}, u32[]{:S(2)}, u32[]{:S(2)}) %collective-permute-start.6) | collective-permute-done | bytes 65568 | tf_op jit(solution)/shard_map/ppermute | solution.py:29
  114.0 2.8 %collective-permute-start.7 = (f32[4,2,8,128]{3,2,1,0:T(8,128)S(1)}, f32[4,2,8,128]{3,2,1,0:T(8,128)S(1)}, u32[]{:S(2)}, u32[]{:S(2)}) collective-permute-start(f32[4,2,8,128]{3,2,1,0:T(8,128)S(1)} %broadcast_select_fusion.7), channel_id=1, source_target_pairs={{0,2},{1,3},{2,0},{3,1},{4,6},{5,7},{6,4},{7,5},{8,10},{9,11},{10,... | collective-permute-start | bytes 98312 | tf_op jit(solution)/shard_map/ppermute | solution.py:29
  116.8 1.9 %collective-permute-done.7 = f32[4,2,8,128]{3,2,1,0:T(8,128)S(1)} collective-permute-done((f32[4,2,8,128]{3,2,1,0:T(8,128)S(1)}, f32[4,2,8,128]{3,2,1,0:T(8,128)S(1)}, u32[]{:S(2)}, u32[]{:S(2)}) %collective-permute-start.7) | collective-permute-done | bytes 32800 | tf_op jit(solution)/shard_map/ppermute | solution.py:29
  118.7 3.1 %collective-permute-start.8 = (f32[4,8,128]{2,1,0:T(8,128)S(1)}, f32[4,8,128]{2,1,0:T(8,128)S(1)}, u32[]{:S(2)}, u32[]{:S(2)}) collective-permute-start(f32[4,8,128]{2,1,0:T(8,128)S(1)} %broadcast_select_fusion.11), channel_id=1, source_target_pairs={{0,4},{1,5},{2,6},{3,7},{4,0},{5,1},{6,2},{7,3},{8,12},{9,13},{10,... | collective-permute-start | bytes 49160 | tf_op jit(solution)/shard_map/ppermute | solution.py:29
  121.8 1.7 %collective-permute-done.8 = f32[4,8,128]{2,1,0:T(8,128)S(1)} collective-permute-done((f32[4,8,128]{2,1,0:T(8,128)S(1)}, f32[4,8,128]{2,1,0:T(8,128)S(1)}, u32[]{:S(2)}, u32[]{:S(2)}) %collective-permute-start.8) | collective-permute-done | bytes 16416 | tf_op jit(solution)/shard_map/ppermute | solution.py:29
  (63 shorter events, 11.2 us)
Async XLA Ops:
  1.0 11.5 %collective-permute-start = (f32[32,4,128]{2,0,1:T(8,128)S(1)}, f32[32,4,128]{2,0,1:T(8,128)S(1)}, u32[]{:S(2)}, u32[]{:S(2)}) collective-permute-start(f32[32,4,128]{2,0,1:T(8,128)S(1)} %copy.60), channel_id=1, source_target_pairs={{0,16},{1,17},{2,18},{3,19},{4,20},{5,21},{6,22},{7,23},{8,24},{9,... | collective-permute-start | bytes 196616 | tf_op jit(solution)/shard_map/ppermute | solution.py:22
  3.4 9.1 %collective-permute-start.1 = (f32[32,4,128]{2,0,1:T(8,128)S(1)}, f32[32,4,128]{2,0,1:T(8,128)S(1)}, u32[]{:S(2)}, u32[]{:S(2)}) collective-permute-start(f32[32,4,128]{2,0,1:T(8,128)S(1)} %copy.61), channel_id=1, source_target_pairs={{16,0},{17,1},{18,2},{19,3},{20,4},{21,5},{22,6},{23,7},{24,8},{25... | collective-permute-start | bytes 196616 | tf_op jit(solution)/shard_map/ppermute | solution.py:23
  14.3 13.8 %copy-start = (f32[32,64,128]{2,1,0:T(8,128)S(1)}, f32[32,64,128]{2,1,0:T(8,128)}, u32[]{:S(2)}) copy-start(f32[32,64,128]{2,1,0:T(8,128)} %param.17) | copy-start | bytes 3145732
  15.4 6.8 %collective-permute-start.2 = (f32[32,72,4]{1,0,2:T(8,128)}, f32[32,72,4]{1,0,2:T(8,128)S(1)}, u32[]{:S(2)}, u32[]{:S(2)}) collective-permute-start(f32[32,72,4]{1,0,2:T(8,128)} %copy.41), channel_id=1, source_target_pairs={{0,8},{1,9},{2,10},{3,11},{4,12},{5,13},{6,14},{7,15},{16,24},{17,... | collective-permute-start | bytes 110600 | tf_op jit(solution)/shard_map/ppermute | solution.py:22
  20.0 6.8 %collective-permute-start.3 = (f32[32,72,4]{1,0,2:T(8,128)S(1)}, f32[32,72,4]{1,0,2:T(8,128)}, u32[]{:S(2)}, u32[]{:S(2)}) collective-permute-start(f32[32,72,4]{1,0,2:T(8,128)S(1)} %copy.42), channel_id=1, source_target_pairs={{8,0},{9,1},{10,2},{11,3},{12,4},{13,5},{14,6},{15,7},{24,16},{25,... | collective-permute-start | bytes 110600 | tf_op jit(solution)/shard_map/ppermute | solution.py:23
  31.1 9.9 %collective-permute-start.4 = (f32[4,72,136]{1,2,0:T(8,128)}, f32[4,72,136]{1,2,0:T(8,128)}, u32[]{:S(2)}, u32[]{:S(2)}) collective-permute-start(f32[4,72,136]{1,2,0:T(8,128)} %copy.45), channel_id=1, source_target_pairs={{0,1},{1,2},{2,3},{3,4},{4,5},{5,6},{6,7},{8,9},{9,10},{10,11},{11... | collective-permute-start | bytes 470024 | tf_op jit(solution)/shard_map/ppermute | solution.py:22
  37.1 10.5 %collective-permute-start.5 = (f32[4,72,136]{1,2,0:T(8,128)}, f32[4,72,136]{1,2,0:T(8,128)}, u32[]{:S(2)}, u32[]{:S(2)}) collective-permute-start(f32[4,72,136]{1,2,0:T(8,128)} %copy.46), channel_id=1, source_target_pairs={{1,0},{2,1},{3,2},{4,3},{5,4},{6,5},{7,6},{9,8},{10,9},{11,10},{12... | collective-permute-start | bytes 470024 | tf_op jit(solution)/shard_map/ppermute | solution.py:23
  49.4 2.2 %copy-start.3 = (f32[38,70]{1,0:T(8,128)S(1)}, f32[38,70]{1,0:T(8,128)}, u32[]{:S(2)}) copy-start(f32[38,70]{1,0:T(8,128)} %broadcast_multiply_fusion.3) | copy-start | bytes 31924
  49.4 2.2 %copy-start.4 = (f32[134]{0:T(256)S(1)}, f32[134]{0:T(256)}, u32[]{:S(2)}) copy-start(f32[134]{0:T(256)} %and_convert_fusion.9) | copy-start | bytes 1612
  51.7 6.5 %copy-start.1 = (f32[36,68]{1,0:T(8,128)S(1)}, f32[36,68]{1,0:T(8,128)}, u32[]{:S(2)}) copy-start(f32[36,68]{1,0:T(8,128)} %broadcast_multiply_fusion.2) | copy-start | bytes 29380
  51.7 6.5 %copy-start.5 = (f32[132]{0:T(256)S(1)}, f32[132]{0:T(256)}, u32[]{:S(2)}) copy-start(f32[132]{0:T(256)} %and_convert_fusion.6) | copy-start | bytes 1588
  58.2 6.2 %copy-start.2 = (f32[34,66]{1,0:T(8,128)S(1)}, f32[34,66]{1,0:T(8,128)}, u32[]{:S(2)}) copy-start(f32[34,66]{1,0:T(8,128)} %broadcast_multiply_fusion.1) | copy-start | bytes 26932
  58.2 6.2 %copy-start.6 = (f32[130]{0:T(256)S(1)}, f32[130]{0:T(256)}, u32[]{:S(2)}) copy-start(f32[130]{0:T(256)} %and_convert_fusion.3) | copy-start | bytes 1564
  64.4 6.1 %copy-start.7 = (f32[128]{0:T(128)S(1)}, f32[128]{0:T(128)}, u32[]{:S(2)}) copy-start(f32[128]{0:T(128)} %and_convert_fusion) | copy-start | bytes 1540
  109.6 4.3 %collective-permute-start.6 = (f32[4,2,2,8,128]{4,3,2,1,0:T(8,128)S(1)}, f32[4,2,2,8,128]{4,3,2,1,0:T(8,128)S(1)}, u32[]{:S(2)}, u32[]{:S(2)}) collective-permute-start(f32[4,2,2,8,128]{4,3,2,1,0:T(8,128)S(1)} %broadcast_select_fusion.3), channel_id=1, source_target_pairs={{0,1},{1,0},{2,3},{3,2},{4,5},{5,4},{6,7},{7,6},{8,9},{9,8},{10,11... | collective-permute-start | bytes 196616 | tf_op jit(solution)/shard_map/ppermute | solution.py:29
  114.0 4.7 %collective-permute-start.7 = (f32[4,2,8,128]{3,2,1,0:T(8,128)S(1)}, f32[4,2,8,128]{3,2,1,0:T(8,128)S(1)}, u32[]{:S(2)}, u32[]{:S(2)}) collective-permute-start(f32[4,2,8,128]{3,2,1,0:T(8,128)S(1)} %broadcast_select_fusion.7), channel_id=1, source_target_pairs={{0,2},{1,3},{2,0},{3,1},{4,6},{5,7},{6,4},{7,5},{8,10},{9,11},{10,... | collective-permute-start | bytes 98312 | tf_op jit(solution)/shard_map/ppermute | solution.py:29
  118.7 4.8 %collective-permute-start.8 = (f32[4,8,128]{2,1,0:T(8,128)S(1)}, f32[4,8,128]{2,1,0:T(8,128)S(1)}, u32[]{:S(2)}, u32[]{:S(2)}) collective-permute-start(f32[4,8,128]{2,1,0:T(8,128)S(1)} %broadcast_select_fusion.11), channel_id=1, source_target_pairs={{0,4},{1,5},{2,6},{3,7},{4,0},{5,1},{6,2},{7,3},{8,12},{9,13},{10,... | collective-permute-start | bytes 49160 | tf_op jit(solution)/shard_map/ppermute | solution.py:29
where the time goes:
time: 125 us; the launch traced here: 124 us
  other arithmetic  65.6 us (52%)
  starting transfers between devices  22.5 us (18%)
  local copies, waits for them, and re-layouts  18.9 us (15%)
  waiting for transfers between devices  15.4 us (12%)
  matrix products  1.34 us (1%)
    another operation x2, other arithmetic, optics(): jnp.stack([sum((colours[channel, material] * bump_list[material] for mate...  25.4 us
    mul x3, other arithmetic, shards(): smooth_valid(padded)  18.7 us
    reduce_sum x1, other arithmetic, shards(): seg_through = jnp.exp(-step_len * jnp.sum(extinct, axis=0))  11.2 us
    ppermute x3, starting transfers between devices, with_halo(): before = lax.ppermute(last, axis, up)  10.7 us
    ppermute x3, waiting for transfers between devices, with_halo(): after = lax.ppermute(first, axis, down)  8.84 us
    ppermute x3, starting transfers between devices, swapped(): lax.ppermute(x, axis, [(i, i ^ 1 << bit) for i in range(lax.axis_size(axi...  7.74 us
    ppermute x3, waiting for transfers between devices, swapped(): lax.ppermute(x, axis, [(i, i ^ 1 << bit) for i in range(lax.axis_size(axi...  6.1 us
    slice x4, local copies, waits for them, and re-layouts, with_halo(): last = lax.slice_in_dim(x, length - width, length, axis=dim)  4.24 us
  transfers between devices with their start and end apart: 9, of which 7 were waited for; matrix products, arithmetic and copies ran while one was open for 12% of the time, Pallas kernels for 0%

commit v1 on v0

v1 whole, which is shorter than its diff:
```python
import functools

import jax
import jax.numpy as jnp
from jax import lax
from jax.experimental import pallas as pl
from jax.experimental.pallas import tpu as pltpu
from jax.sharding import PartitionSpec as P

STEPS = 4
MATERIALS = 4
CHANNELS = 3

KAPPA = 0.5
RATE_DEPTH = 0.3
RATE_PLANE = 0.09
LANES = 256


def with_halo(x, sides, width):
    for axis, dim in sides:
        size, length = (lax.axis_size(axis), x.shape[dim])
        up = [(i, (i + 1) % size) for i in range(size - 1)]
        down = [(j, i) for i, j in up]
        last = lax.slice_in_dim(x, length - width, length, axis=dim)
        first = lax.slice_in_dim(x, 0, width, axis=dim)
        before = lax.ppermute(last, axis, up)
        after = lax.ppermute(first, axis, down)
        pieces = [before, x, after]
        if dim == 2:
            fill = list(x.shape)
            fill[2] = LANES - length - 2 * width
            pieces.append(jnp.zeros(fill, x.dtype))
        x = jnp.concatenate(pieces, axis=dim)
    return x


def flux(d, rate):
    q = d * (1.0 / KAPPA)
    return rate * d / (1.0 + q * q)


def render_kernel(lim_ref, prm_ref, x_ref, out_ref, a_ref, b_ref, m_ref, *, interior, h):
    depth, rows, lanes = x_ref.shape
    d_in, r_in, l_in = interior
    halo = STEPS

    row = lax.broadcasted_iota(jnp.int32, (rows, lanes), 0)
    lane = lax.broadcasted_iota(jnp.int32, (rows, lanes), 1)
    ok = (row >= lim_ref[2]) & (row < lim_ref[3]) & (lane >= lim_ref[4]) & (lane < lim_ref[5])
    m_ref[...] = jnp.where(ok, 1.0, 0.0).astype(jnp.float32)

    def plane_update(src, z, g_prev):
        c = src[z]
        g = flux(src[z + 1] - c, RATE_DEPTH)
        fr = flux(pltpu.roll(c, rows - 1, 0) - c, RATE_PLANE)
        fc = flux(pltpu.roll(c, lanes - 1, 1) - c, RATE_PLANE)
        new = c + (g - g_prev) + (fr - pltpu.roll(fr, 1, 0)) + (fc - pltpu.roll(fc, 1, 1))
        return new, g

    def smooth(src, dst, s):
        z0, z1 = s + 1, depth - 1 - s
        g0 = flux(src[z0] - src[z0 - 1], RATE_DEPTH)

        def body(z, g_prev):
            new, g = plane_update(src, z, g_prev)
            inside = (z >= lim_ref[0]) & (z < lim_ref[1])
            zf = jnp.where(inside, 1.0, 0.0).astype(jnp.float32)
            dst[z] = new * (m_ref[...] * zf)
            return g

        lax.fori_loop(z0, z1, body, g0)

    smooth(x_ref, a_ref, 0)
    smooth(a_ref, b_ref, 1)
    smooth(b_ref, a_ref, 2)

    cen = [prm_ref[k] for k in range(MATERIALS)]
    wid = [prm_ref[MATERIALS + k] for k in range(MATERIALS)]
    den = [prm_ref[2 * MATERIALS + k] for k in range(MATERIALS)]
    col = [[prm_ref[3 * MATERIALS + ch * MATERIALS + k] for k in range(MATERIALS)] for ch in range(CHANNELS)]

    for ch in range(CHANNELS + 1):
        out_ref[ch] = jnp.zeros((r_in, l_in), jnp.float32)

    z0, z1 = halo, halo + d_in
    g0 = flux(a_ref[z0] - a_ref[z0 - 1], RATE_DEPTH)

    def final(z, g_prev):
        new, g = plane_update(a_ref, z, g_prev)
        v = pltpu.roll(pltpu.roll(new, rows - halo, 0), lanes - halo, 1)[:r_in, :l_in]
        bumps = [den[k] * jnp.exp(-(((v - cen[k]) / wid[k]) ** 2)) for k in range(MATERIALS)]
        ext = bumps[0] + bumps[1] + bumps[2] + bumps[3]
        run = out_ref[CHANNELS]
        through = jnp.exp(-h * run)
        for ch in range(CHANNELS):
            emit = col[ch][0] * bumps[0] + col[ch][1] * bumps[1] + col[ch][2] * bumps[2] + col[ch][3] * bumps[3]
            out_ref[ch] = out_ref[ch] + through * emit
        out_ref[CHANNELS] = run + ext
        return g

    lax.fori_loop(z0, z1, final, g0)
    for ch in range(CHANNELS):
        out_ref[ch] = h * out_ref[ch]


def render_block(padded, lim, prm, interior, h):
    depth, rows, lanes = padded.shape
    d_in, r_in, l_in = interior
    cells = depth * rows * lanes
    kernel = functools.partial(render_kernel, interior=interior, h=h)
    return pl.pallas_call(
        kernel,
        out_shape=jax.ShapeDtypeStruct((CHANNELS + 1, r_in, l_in), jnp.float32),
        in_specs=[
            pl.BlockSpec(memory_space=pltpu.SMEM),
            pl.BlockSpec(memory_space=pltpu.SMEM),
            pl.BlockSpec(memory_space=pltpu.VMEM),
        ],
        out_specs=pl.BlockSpec(memory_space=pltpu.VMEM),
        scratch_shapes=[
            pltpu.VMEM((depth, rows, lanes), jnp.float32),
            pltpu.VMEM((depth, rows, lanes), jnp.float32),
            pltpu.VMEM((rows, lanes), jnp.float32),
        ],
        compiler_params=pltpu.CompilerParams(vmem_limit_bytes=48 * 1024 * 1024),
        cost_estimate=pl.CostEstimate(
            flops=int(cells * STEPS * 40 + d_in * r_in * l_in * 60),
            transcendentals=int(d_in * r_in * l_in * (MATERIALS + 1)),
            bytes_accessed=int(cells * 4 + (CHANNELS + 1) * r_in * l_in * 4),
        ),
    )(lim, prm, padded)


def shards(phase_field, centres, widths, densities, colours):
    depth_cells, row_cells, col_cells = phase_field.shape
    groups = lax.axis_size("gz")
    h = 1.0 / (depth_cells * groups)
    padded = with_halo(phase_field, (("gx", 1), ("gy", 2), ("gz", 0)), STEPS)

    z_lo = STEPS - lax.axis_index("gz") * depth_cells
    r_lo = STEPS - lax.axis_index("gx") * row_cells
    c_lo = STEPS - lax.axis_index("gy") * col_cells
    lim = jnp.stack(
        [
            z_lo,
            z_lo + depth_cells * groups,
            r_lo,
            r_lo + row_cells * lax.axis_size("gx"),
            c_lo,
            c_lo + col_cells * lax.axis_size("gy"),
        ]
    ).astype(jnp.int32)
    prm = jnp.concatenate([centres, widths, densities, colours.reshape(-1)]).astype(jnp.float32)

    seg = render_block(padded, lim, prm, (depth_cells, row_cells, col_cells), h)

    rows_part = row_cells // groups
    parts = seg.reshape(CHANNELS + 1, groups, rows_part, col_cells)
    got = lax.all_to_all(parts, "gz", 1, 1, tiled=True)
    prefix = jnp.zeros((rows_part, col_cells), jnp.float32)
    rad = jnp.zeros((CHANNELS, rows_part, col_cells), jnp.float32)
    for g in range(groups):
        rad = rad + jnp.exp(-h * prefix)[None] * got[:CHANNELS, g]
        prefix = prefix + got[CHANNELS, g]
    alpha = 1.0 - jnp.exp(-h * prefix)
    return jnp.concatenate([rad, alpha[None]], axis=0)


def solution(mesh):
    placed = (P("gz", "gx", "gy"), P(), P(), P(), P())
    return jax.shard_map(
        shards, mesh=mesh, in_specs=placed, out_specs=P(None, ("gx", "gz"), "gy"), check_vma=False
    )
```

time: 125 us -> 86.7 us (0.69)
  other arithmetic: 65.6 us -> 7.79 us
  Pallas kernels: 0 us -> 30.8 us
  local copies, waits for them, and re-layouts: 18.9 us -> 3.93 us
  blocking collectives: 0 us -> 13.9 us
  starting transfers between devices: 22.5 us -> 14.6 us
  matrix products: 1.34 us -> 0 us
    pallas_call x0 -> x1, Pallas kernels: none -> 30.8 us  [render_block(): pl.pallas_call(kernel, out_shape=jax.ShapeDtypeStruct((CHANNELS + 1, r_in...]
    another operation x2 -> x0, other arithmetic: 25.4 us -> none  [optics(): jnp.stack([sum((colours[channel, material] * bump_list[material] for mate...]
    mul x11 -> x0, other arithmetic: 20.9 us -> none  [the longest x3 18.7 us: shards(): smooth_valid(padded)]
    all_to_all x0 -> x1, blocking collectives: none -> 13.9 us  [shards(): got = lax.all_to_all(parts, 'gz', 1, 1, tiled=True)]
    reduce_sum x2 -> x0, other arithmetic: 11.7 us -> none  [the longest x1 11.2 us: shards(): seg_through = jnp.exp(-step_len * jnp.sum(extinct, axis=0))]
    ppermute x3, waiting for transfers between devices: 0.47 us -> 9.03 us  [with_halo(): before = lax.ppermute(last, axis, up)]
    ppermute x3 -> x0, starting transfers between devices: 7.74 us -> none  [swapped(): lax.ppermute(x, axis, [(i, i ^ 1 << bit) for i in range(lax.axis_size(axi...]
    slice x4 -> x0, local copies, waits for them, and re-layouts: 6.2 us -> none  [the longest x1 1.8 us: optics(): colours[channel, material] * bump_list[material]]
  transfers between devices with their start and end apart: 9 -> 6, of which waited for: 7 -> 4; matrix products, arithmetic and copies ran while one was open for 12% -> 2% of each run, Pallas kernels for 0% -> 0%
where the time goes in v1:
time: 86.7 us; the launch traced here: 86.3 us
  Pallas kernels  30.8 us (36%)
  waiting for transfers between devices  15.1 us (17%)
  starting transfers between devices  14.6 us (17%)
  blocking collectives  13.9 us (16%)
  other arithmetic  7.79 us (9%)
  local copies, waits for them, and re-layouts  3.93 us (5%)
    pallas_call x1, Pallas kernels, render_block(): pl.pallas_call(kernel, out_shape=jax.ShapeDtypeStruct((CHANNELS + 1, r_in...  30.8 us
    all_to_all x1, blocking collectives, shards(): got = lax.all_to_all(parts, 'gz', 1, 1, tiled=True)  13.9 us
    ppermute x3, starting transfers between devices, with_halo(): before = lax.ppermute(last, axis, up)  10.7 us
    ppermute x3, waiting for transfers between devices, with_halo(): before = lax.ppermute(last, axis, up)  9.03 us
    ppermute x3, waiting for transfers between devices, with_halo(): after = lax.ppermute(first, axis, down)  6.08 us
    concatenate x2, other arithmetic, with_halo(): x = jnp.concatenate(pieces, axis=dim)  4.17 us
    ppermute x3, starting transfers between devices, with_halo(): after = lax.ppermute(first, axis, down)  3.87 us
    slice x1, other arithmetic, with_halo(): last = lax.slice_in_dim(x, length - width, length, axis=dim)  2.23 us
  transfers between devices with their start and end apart: 6, of which 4 were waited for; matrix products, arithmetic and copies ran while one was open for 2% of the time, Pallas kernels for 0%

profile of v1, /device:TPU:0, one launch (start us, length us, event | category | flops | bytes accessed | tf_op | source)
XLA Modules:
  0.0 86.3 jit_solution(1081304868424873774)
XLA Ops:
  0.0 1.0 %fusion.19 = (f32[32,4,128]{2,1,0:T(4,128)S(1)}, f32[32,4,128]{2,1,0:T(4,128)S(1)}) fusion(f32[32,64,128]{2,1,0:T(8,128)} %param.5), kind=kLoop, calls=%fused_computation.51 | loop fusion | bytes 262144 | tf_op jit(solution)/shard_map/slice | solution.py:25
  1.0 2.4 %collective-permute-start = (f32[32,4,128]{2,1,0:T(4,128)S(1)}, f32[32,4,128]{2,1,0:T(4,128)S(1)}, u32[]{:S(2)}, u32[]{:S(2)}) collective-permute-start(f32[32,4,128]{2,1,0:T(4,128)S(1)} %get-tuple-element.13), channel_id=1, source_target_pairs={{0,16},{1,17},{2,18},{3,19},{4,20},{5,21},{6,22},{7,23},{8,24},{9,... | collective-permute-start | bytes 196616 | tf_op jit(solution)/shard_map/ppermute | solution.py:27
  3.4 1.3 %collective-permute-start.1 = (f32[32,4,128]{2,1,0:T(4,128)S(1)}, f32[32,4,128]{2,1,0:T(4,128)S(1)}, u32[]{:S(2)}, u32[]{:S(2)}) collective-permute-start(f32[32,4,128]{2,1,0:T(4,128)S(1)} %get-tuple-element.14), channel_id=1, source_target_pairs={{16,0},{17,1},{18,2},{19,3},{20,4},{21,5},{22,6},{23,7},{24,8},{25... | collective-permute-start | bytes 196616 | tf_op jit(solution)/shard_map/ppermute | solution.py:28
  4.7 0.0 collective-permute-done
  4.7 1.8 %collective-permute-done.1 = f32[32,4,128]{2,1,0:T(4,128)S(1)} collective-permute-done((f32[32,4,128]{2,1,0:T(4,128)S(1)}, f32[32,4,128]{2,1,0:T(4,128)S(1)}, u32[]{:S(2)}, u32[]{:S(2)}) %collective-permute-start.1) | collective-permute-done | bytes 65568 | tf_op jit(solution)/shard_map/ppermute | solution.py:28
  6.6 0.6 copy-done.1
  7.2 1.3 %pad_maximum_fusion.1 = f32[32,72,128]{2,1,0:T(8,128)S(1)} fusion(f32[32,4,128]{2,1,0:T(4,128)S(1)} %collective-permute-done.1, f32[32,64,128]{2,1,0:T(8,128)} %param.5, f32[32,4,128]{2,1,0:T(4,128)S(1)} %collective-permute-done), kind=kLoop, calls=%fused_computation.1 | loop fusion | flops 589824 | bytes 2359296 | tf_op jit(solution)/shard_map/concatenate | solution.py:34
  8.5 0.4 fusion.18
  8.9 0.4 copy.13
  9.3 4.2 %collective-permute-start.2 = (f32[32,72,4]{1,0,2:T(8,128)S(1)}, f32[32,72,4]{1,0,2:T(8,128)S(1)}, u32[]{:S(2)}, u32[]{:S(2)}) collective-permute-start(f32[32,72,4]{1,0,2:T(8,128)S(1)} %copy.13), channel_id=1, source_target_pairs={{0,8},{1,9},{2,10},{3,11},{4,12},{5,13},{6,14},{7,15},{16,24},{17,... | collective-permute-start | bytes 110600 | tf_op jit(solution)/shard_map/ppermute | solution.py:27
  13.5 0.4 copy.14
  13.9 1.3 %collective-permute-start.3 = (f32[32,72,4]{1,0,2:T(8,128)S(1)}, f32[32,72,4]{1,0,2:T(8,128)S(1)}, u32[]{:S(2)}, u32[]{:S(2)}) collective-permute-start(f32[32,72,4]{1,0,2:T(8,128)S(1)} %copy.14), channel_id=1, source_target_pairs={{8,0},{9,1},{10,2},{11,3},{12,4},{13,5},{14,6},{15,7},{24,16},{25,... | collective-permute-start | bytes 110600 | tf_op jit(solution)/shard_map/ppermute | solution.py:28
  15.2 0.2 collective-permute-done.2
  15.4 0.4 copy.15
  15.8 4.2 %collective-permute-done.3 = f32[32,72,4]{1,0,2:T(8,128)S(1)} collective-permute-done((f32[32,72,4]{1,0,2:T(8,128)S(1)}, f32[32,72,4]{1,0,2:T(8,128)S(1)}, u32[]{:S(2)}, u32[]{:S(2)}) %collective-permute-start.3) | collective-permute-done | bytes 36896 | tf_op jit(solution)/shard_map/ppermute | solution.py:28
  20.1 0.4 copy.16
  20.5 0.1 broadcast_in_dim.2
  20.6 0.0 copy-start.2
  20.6 0.0 copy-start.3
  20.6 0.0 copy-start.4
  20.7 2.2 %pad_maximum_fusion.7 = (f32[4,72,256]{2,1,0:T(8,128)}, f32[4,72,256]{2,1,0:T(8,128)}) fusion(f32[32,72,120]{2,1,0:T(8,128)S(1)} %broadcast_in_dim.2, f32[32,72,4]{2,1,0:T(8,128)S(1)} %copy.16, f32[32,72,4]{2,1,0:T(8,128)S(1)} %copy.15, f32[32,4,128]{2,1,0:T(4,128)} %copy-done.1, f32[32,64,128]{2,1,0:T(8,128)} %param.5, f32[32,4,128]{2,1,0:T(4,128)} %copy-done), kind=kLoop, calls=%fused_computation.7 | loop fusion | flops 737280 | bytes 2949120 | tf_op jit(solution)/shard_map/slice | solution.py:25
  22.9 4.1 %collective-permute-start.4 = (f32[4,72,256]{2,1,0:T(8,128)}, f32[4,72,256]{2,1,0:T(8,128)}, u32[]{:S(2)}, u32[]{:S(2)}) collective-permute-start(f32[4,72,256]{2,1,0:T(8,128)} %get-tuple-element.9), channel_id=1, source_target_pairs={{0,1},{1,2},{2,3},{3,4},{4,5},{5,6},{6,7},{8,9},{9,10},{10,11},{11... | collective-permute-start | bytes 884744 | tf_op jit(solution)/shard_map/ppermute | solution.py:27
  27.0 1.3 %collective-permute-start.5 = (f32[4,72,256]{2,1,0:T(8,128)}, f32[4,72,256]{2,1,0:T(8,128)}, u32[]{:S(2)}, u32[]{:S(2)}) collective-permute-start(f32[4,72,256]{2,1,0:T(8,128)} %get-tuple-element.10), channel_id=1, source_target_pairs={{1,0},{2,1},{3,2},{4,3},{5,4},{6,5},{7,6},{9,8},{10,9},{11,10},{12... | collective-permute-start | bytes 884744 | tf_op jit(solution)/shard_map/ppermute | solution.py:28
  28.3 0.1 reshape.210
  28.4 0.1 stack.27.lim_ref
  28.5 0.7 pad_maximum_fusion.9.prm_ref
  29.2 8.9 %collective-permute-done.4 = f32[4,72,256]{2,1,0:T(8,128)} collective-permute-done((f32[4,72,256]{2,1,0:T(8,128)}, f32[4,72,256]{2,1,0:T(8,128)}, u32[]{:S(2)}, u32[]{:S(2)}) %collective-permute-start.4) | collective-permute-done | bytes 294944 | tf_op jit(solution)/shard_map/ppermute | solution.py:27
  38.1 0.0 collective-permute-done.5
  38.1 2.8 %pad_maximum_fusion.x_ref = f32[40,72,256]{2,1,0:T(8,128)S(1)} fusion(f32[4,72,256]{2,1,0:T(8,128)} %collective-permute-done.5, f32[32,72,120]{2,1,0:T(8,128)S(1)} %broadcast_in_dim.2, f32[32,72,4]{2,1,0:T(8,128)S(1)} %copy.16, f32[32,4,128]{2,1,0:T(4,128)} %copy-done.1, f32[32,64,128]{2,1,0:T(8,128)} %param.5, f32[32,4,128]{2,1,0:T(4,128)} %copy-done, ...), kind=kLoop, calls=%fused_computation | loop fusion | flops 5160960 | bytes 5898240 | tf_op jit(solution)/shard_map/concatenate | solution.py:34
  40.9 30.8 %shard_map.55 = f32[4,64,128]{2,1,0:T(8,128)S(1)} custom-call(s32[6]{0:T(128)S(1)} %stack.27.lim_ref, f32[24]{0:T(128)S(1)} %pad_maximum_fusion.9.prm_ref, f32[40,72,256]{2,1,0:T(8,128)S(1)} %pad_maximum_fusion.x_ref), custom_call_target="tpu_custom_call" | custom-call | flops 133693440 | bytes 3080192 | tf_op jit(solution)/shard_map/pallas_call | solution.py:112
  71.7 13.9 %all_to_all.5 = f32[4,8,8,128]{3,2,0,1:T(8,128)S(1)} all-to-all(f32[4,8,8,128]{3,2,0,1:T(8,128)S(1)} %copy.17), channel_id=1, replica_groups=mesh['gx'=2,'gy'=2,'gz'=8] {'gz'}, dimensions={1} | all-to-all | bytes 262144 | tf_op jit(solution)/shard_map/all_to_all | solution.py:160
  85.7 0.6 pad_maximum_fusion.8
  (11 shorter events, 0.1 us)
Async XLA Ops:
  1.0 3.7 %collective-permute-start = (f32[32,4,128]{2,1,0:T(4,128)S(1)}, f32[32,4,128]{2,1,0:T(4,128)S(1)}, u32[]{:S(2)}, u32[]{:S(2)}) collective-permute-start(f32[32,4,128]{2,1,0:T(4,128)S(1)} %get-tuple-element.13), channel_id=1, source_target_pairs={{0,16},{1,17},{2,18},{3,19},{4,20},{5,21},{6,22},{7,23},{8,24},{9,... | collective-permute-start | bytes 196616 | tf_op jit(solution)/shard_map/ppermute | solution.py:27
  3.4 3.1 %collective-permute-start.1 = (f32[32,4,128]{2,1,0:T(4,128)S(1)}, f32[32,4,128]{2,1,0:T(4,128)S(1)}, u32[]{:S(2)}, u32[]{:S(2)}) collective-permute-start(f32[32,4,128]{2,1,0:T(4,128)S(1)} %get-tuple-element.14), channel_id=1, source_target_pairs={{16,0},{17,1},{18,2},{19,3},{20,4},{21,5},{22,6},{23,7},{24,8},{25... | collective-permute-start | bytes 196616 | tf_op jit(solution)/shard_map/ppermute | solution.py:28
  4.7 1.8 %copy-start = (f32[32,4,128]{2,1,0:T(4,128)}, f32[32,4,128]{2,1,0:T(4,128)S(1)}, u32[]{:S(2)}) copy-start(f32[32,4,128]{2,1,0:T(4,128)S(1)} %collective-permute-done) | copy-start | bytes 196612
  6.6 0.6 copy-start.1
  9.3 6.1 %collective-permute-start.2 = (f32[32,72,4]{1,0,2:T(8,128)S(1)}, f32[32,72,4]{1,0,2:T(8,128)S(1)}, u32[]{:S(2)}, u32[]{:S(2)}) collective-permute-start(f32[32,72,4]{1,0,2:T(8,128)S(1)} %copy.13), channel_id=1, source_target_pairs={{0,8},{1,9},{2,10},{3,11},{4,12},{5,13},{6,14},{7,15},{16,24},{17,... | collective-permute-start | bytes 110600 | tf_op jit(solution)/shard_map/ppermute | solution.py:27
  13.9 6.2 %collective-permute-start.3 = (f32[32,72,4]{1,0,2:T(8,128)S(1)}, f32[32,72,4]{1,0,2:T(8,128)S(1)}, u32[]{:S(2)}, u32[]{:S(2)}) collective-permute-start(f32[32,72,4]{1,0,2:T(8,128)S(1)} %copy.14), channel_id=1, source_target_pairs={{8,0},{9,1},{10,2},{11,3},{12,4},{13,5},{14,6},{15,7},{24,16},{25,... | collective-permute-start | bytes 110600 | tf_op jit(solution)/shard_map/ppermute | solution.py:28
  20.6 7.7 %copy-start.2 = (f32[3,4]{1,0:T(4,128)S(1)}, f32[3,4]{1,0:T(4,128)}, u32[]{:S(2)}) copy-start(f32[3,4]{1,0:T(4,128)} %param.9) | copy-start | bytes 148
  20.6 7.9 %copy-start.3 = (f32[4]{0:T(128)S(1)}, f32[4]{0:T(128)}, u32[]{:S(2)}) copy-start(f32[4]{0:T(128)} %param.8) | copy-start | bytes 52
  20.6 7.8 %copy-start.4 = (f32[4]{0:T(128)S(1)}, f32[4]{0:T(128)}, u32[]{:S(2)}) copy-start(f32[4]{0:T(128)} %param.7) | copy-start | bytes 52
  22.9 15.2 %collective-permute-start.4 = (f32[4,72,256]{2,1,0:T(8,128)}, f32[4,72,256]{2,1,0:T(8,128)}, u32[]{:S(2)}, u32[]{:S(2)}) collective-permute-start(f32[4,72,256]{2,1,0:T(8,128)} %get-tuple-element.9), channel_id=1, source_target_pairs={{0,1},{1,2},{2,3},{3,4},{4,5},{5,6},{6,7},{8,9},{9,10},{10,11},{11... | collective-permute-start | bytes 884744 | tf_op jit(solution)/shard_map/ppermute | solution.py:27
  27.0 11.1 %collective-permute-start.5 = (f32[4,72,256]{2,1,0:T(8,128)}, f32[4,72,256]{2,1,0:T(8,128)}, u32[]{:S(2)}, u32[]{:S(2)}) collective-permute-start(f32[4,72,256]{2,1,0:T(8,128)} %get-tuple-element.10), channel_id=1, source_target_pairs={{1,0},{2,1},{3,2},{4,3},{5,4},{6,5},{7,6},{9,8},{10,9},{11,10},{12... | collective-permute-start | bytes 884744 | tf_op jit(solution)/shard_map/ppermute | solution.py:28

commit v2 on v1

--- a/solution.py
+++ b/solution.py
@@ -1,4 +1,5 @@
 import functools
+import itertools
 
 import jax
 import jax.numpy as jnp
@@ -17,22 +18,89 @@
 LANES = 256
 
 
-def with_halo(x, sides, width):
-    for axis, dim in sides:
-        size, length = (lax.axis_size(axis), x.shape[dim])
-        up = [(i, (i + 1) % size) for i in range(size - 1)]
-        down = [(j, i) for i, j in up]
-        last = lax.slice_in_dim(x, length - width, length, axis=dim)
-        first = lax.slice_in_dim(x, 0, width, axis=dim)
-        before = lax.ppermute(last, axis, up)
-        after = lax.ppermute(first, axis, down)
-        pieces = [before, x, after]
-        if dim == 2:
-            fill = list(x.shape)
-            fill[2] = LANES - length - 2 * width
-            pieces.append(jnp.zeros(fill, x.dtype))
-        x = jnp.concatenate(pieces, axis=dim)
-    return x
+def pick(cond, a, b):
+    if isinstance(cond, bool):
+        return a if cond else b
+    return jnp.where(cond, a, b)
+
+
+def axis_moves(axis):
+    n = lax.axis_size(axis)
+    if n == 1:
+        return []
+    if n == 2:
+        me = lax.axis_index(axis)
+        return [([(0, 1), (1, 0)], me == 0, me == 1)]
+    up = [(i, i + 1) for i in range(n - 1)]
+    down = [(i + 1, i) for i in range(n - 1)]
+    return [(up, True, True), (down, False, False)]
+
+
+def halo_stage(x, dim_axes, width):
+    dims = [d for d, _ in dim_axes]
+    axes = [a for _, a in dim_axes]
+    sizes = [lax.axis_size(a) for a in axes]
+    options = [[None] + axis_moves(a) for a in axes]
+    blocks = {}
+    for combo in itertools.product(*options):
+        if all(m is None for m in combo):
+            continue
+        piece = x
+        for d, m in zip(dims, combo):
+            if m is not None:
+                n_d = piece.shape[d]
+                lo = lax.slice_in_dim(piece, 0, width, axis=d)
+                hi = lax.slice_in_dim(piece, n_d - width, n_d, axis=d)
+                piece = pick(m[1], hi, lo)
+        used = [(a, s, m) for a, s, m in zip(axes, sizes, combo) if m is not None]
+        pairs = []
+        for parts in itertools.product(*[m[0] for _, _, m in used]):
+            src = dst = 0
+            for (_, s, _), (p, q) in zip(used, parts):
+                src, dst = src * s + p, dst * s + q
+            pairs.append((src, dst))
+        got = lax.ppermute(piece, tuple(a for a, _, _ in used), pairs)
+        landing = [(d, m[2]) for d, m in zip(dims, combo) if m is not None]
+        for sides in itertools.product(("lo", "hi"), repeat=len(landing)):
+            cond = True
+            for (d, land_lo), side in zip(landing, sides):
+                this = land_lo if side == "lo" else (not land_lo if isinstance(land_lo, bool) else ~land_lo)
+                if isinstance(cond, bool) and isinstance(this, bool):
+                    cond = cond and this
+                elif isinstance(cond, bool):
+                    cond = this if cond else False
+                elif isinstance(this, bool):
+                    cond = cond if this else False
+                else:
+                    cond = cond & this
+            if cond is False:
+                continue
+            key = [None] * len(dims)
+            for (d, _), side in zip(landing, sides):
+                key[dims.index(d)] = side
+            key = tuple(k or "mid" for k in key)
+            val = got if cond is True else jnp.where(cond, got, 0.0)
+            blocks[key] = val if key not in blocks else blocks[key] + val
+    blocks[tuple("mid" for _ in dims)] = x
+
+    def block_shape(key):
+        shape = list(x.shape)
+        for d, k in zip(dims, key):
+            if k != "mid":
+                shape[d] = width
+        return shape
+
+    def assemble(prefix):
+        level = len(prefix)
+        if level == len(dims):
+            key = tuple(prefix)
+            if key in blocks:
+                return blocks[key]
+            return jnp.zeros(block_shape(key), x.dtype)
+        parts = [assemble(prefix + [k]) for k in ("lo", "mid", "hi")]
+        return jnp.concatenate(parts, axis=dims[level])
+
+    return assemble([])
 
 
 def flux(d, rate):
@@ -136,7 +204,10 @@
     depth_cells, row_cells, col_cells = phase_field.shape
     groups = lax.axis_size("gz")
     h = 1.0 / (depth_cells * groups)
-    padded = with_halo(phase_field, (("gx", 1), ("gy", 2), ("gz", 0)), STEPS)
+    padded = halo_stage(phase_field, ((0, "gz"),), STEPS)
+    padded = halo_stage(padded, ((1, "gx"), (2, "gy")), STEPS)
+    fill = (padded.shape[0], padded.shape[1], LANES - padded.shape[2])
+    padded = jnp.concatenate([padded, jnp.zeros(fill, padded.dtype)], axis=2)
 
     z_lo = STEPS - lax.axis_index("gz") * depth_cells
     r_lo = STEPS - lax.axis_index("gx") * row_cells

time: 86.7 us -> 73.3 us (0.85)
  waiting for transfers between devices: 15.1 us -> 6.43 us
  starting transfers between devices: 14.6 us -> 8.53 us
  local copies, waits for them, and re-layouts: 3.93 us -> 8.99 us
  other arithmetic: 7.79 us -> 5.24 us
  blocking collectives: 13.9 us -> 12.9 us
    ppermute x6 -> x5, waiting for transfers between devices: 15.1 us -> 6.43 us  [halo_stage(): got = lax.ppermute(piece, tuple((a for a, _, _ in used)), pairs)]
    ppermute x6 -> x5, starting transfers between devices: 14.6 us -> 8.53 us  [halo_stage(): got = lax.ppermute(piece, tuple((a for a, _, _ in used)), pairs)]
    slice x4, local copies, waits for them, and re-layouts: 2.18 us -> 4.78 us  [the longest x3 4.3 us: halo_stage(): lo = lax.slice_in_dim(piece, 0, width, axis=d)]
    slice x1 -> x0, other arithmetic: 2.23 us -> none  [with_halo(): last = lax.slice_in_dim(x, length - width, length, axis=dim)]
    select_n x0 -> x2, local copies, waits for them, and re-layouts: none -> 2.04 us  [halo_stage(): val = got if cond is True else jnp.where(cond, got, 0.0)]
    all_to_all x1, blocking collectives: 13.9 us -> 12.9 us  [shards(): got = lax.all_to_all(parts, 'gz', 1, 1, tiled=True)]
    concatenate x2 -> x1, other arithmetic: 4.17 us -> 3.57 us  [assemble(): return jnp.concatenate(parts, axis=dims[level])]
  transfers between devices with their start and end apart: 6 -> 5, of which waited for: 4 -> 2; matrix products, arithmetic and copies ran while one was open for 2% -> 10% of each run, Pallas kernels for 0% -> 0%
where the time goes in v2:
time: 73.3 us; the launch traced here: 73 us
  Pallas kernels  30.8 us (42%)
  blocking collectives  12.9 us (18%)
  local copies, waits for them, and re-layouts  8.99 us (12%)
  starting transfers between devices  8.53 us (12%)
  waiting for transfers between devices  6.43 us (9%)
  other arithmetic  5.24 us (7%)
    pallas_call x1, Pallas kernels, render_block(): pl.pallas_call(kernel, out_shape=jax.ShapeDtypeStruct((CHANNELS + 1, r_in...  30.8 us
    all_to_all x1, blocking collectives, shards(): got = lax.all_to_all(parts, 'gz', 1, 1, tiled=True)  12.9 us
    ppermute x5, starting transfers between devices, halo_stage(): got = lax.ppermute(piece, tuple((a for a, _, _ in used)), pairs)  8.53 us
    ppermute x5, waiting for transfers between devices, halo_stage(): got = lax.ppermute(piece, tuple((a for a, _, _ in used)), pairs)  6.43 us
    slice x3, local copies, waits for them, and re-layouts, halo_stage(): lo = lax.slice_in_dim(piece, 0, width, axis=d)  4.3 us
    concatenate x1, other arithmetic, assemble(): return jnp.concatenate(parts, axis=dims[level])  3.57 us
    select_n x2, local copies, waits for them, and re-layouts, halo_stage(): val = got if cond is True else jnp.where(cond, got, 0.0)  2.04 us
  transfers between devices with their start and end apart: 5, of which 2 were waited for; matrix products, arithmetic and copies ran while one was open for 10% of the time, Pallas kernels for 0%

profile of v2, /device:TPU:0, one launch (start us, length us, event | category | flops | bytes accessed | tf_op | source)
XLA Modules:
  0.0 73.0 jit_solution(10980954431998218661)
XLA Ops:
  0.0 1.0 %fusion.21 = (f32[4,64,128]{2,1,0:T(8,128)S(1)}, f32[4,64,128]{2,1,0:T(8,128)S(1)}) fusion(f32[32,64,128]{2,1,0:T(8,128)} %param.5), kind=kLoop, calls=%fused_computation.66 | loop fusion | bytes 524288 | tf_op jit(solution)/shard_map/slice | solution.py:52
  1.0 4.9 %collective-permute-start = (f32[4,64,128]{2,1,0:T(8,128)S(1)}, f32[4,64,128]{2,1,0:T(8,128)S(1)}, u32[]{:S(2)}, u32[]{:S(2)}) collective-permute-start(f32[4,64,128]{2,1,0:T(8,128)S(1)} %get-tuple-element.12), channel_id=1, source_target_pairs={{0,1},{1,2},{2,3},{3,4},{4,5},{5,6},{6,7},{8,9},{9,10},{10,11},{11... | collective-permute-start | bytes 393224 | tf_op jit(solution)/shard_map/ppermute | solution.py:62
  5.9 1.3 %collective-permute-start.1 = (f32[4,64,128]{2,1,0:T(8,128)S(1)}, f32[4,64,128]{2,1,0:T(8,128)S(1)}, u32[]{:S(2)}, u32[]{:S(2)}) collective-permute-start(f32[4,64,128]{2,1,0:T(8,128)S(1)} %get-tuple-element.11), channel_id=1, source_target_pairs={{1,0},{2,1},{3,2},{4,3},{5,4},{6,5},{7,6},{9,8},{10,9},{11,10},{12... | collective-permute-start | bytes 393224 | tf_op jit(solution)/shard_map/ppermute | solution.py:62
  7.3 0.8 %reshape.210 = f32[12]{0:T(128)S(1)} reshape(f32[3,4]{1,0:T(4,128)} %param.9) | data formatting | bytes 96 | tf_op jit(solution)/shard_map/reshape | solution.py:225
  8.0 0.1 stack.27.lim_ref
  8.1 0.8 %pad_maximum_fusion.1.prm_ref = f32[24]{0:T(128)S(1)} fusion(f32[12]{0:T(128)S(1)} %reshape.210, f32[4]{0:T(128)} %param.8, f32[4]{0:T(128)} %param.7, f32[4]{0:T(128)} %param.6), kind=kLoop, calls=%fused_computation.64 | loop fusion | flops 72 | bytes 192 | tf_op jit(solution)/shard_map/concatenate | solution.py:225
  8.9 0.0 collective-permute-done
  8.9 1.3 %constant_dynamic-update-slice_fusion.1 = f32[40,64,128]{2,1,0:T(8,128)S(1)} fusion(f32[40,64,128]{2,1,0:T(8,128)S(1)} %constant_dynamic-update-slice_fusion.2, f32[32,64,128]{2,1,0:T(8,128)} %param.5), kind=kLoop, calls=%fused_computation.44 | loop fusion | bytes 2097152
  10.2 2.6 %collective-permute-done.1 = f32[4,64,128]{2,1,0:T(8,128)S(1)} collective-permute-done((f32[4,64,128]{2,1,0:T(8,128)S(1)}, f32[4,64,128]{2,1,0:T(8,128)S(1)}, u32[]{:S(2)}, u32[]{:S(2)}) %collective-permute-start.1) | collective-permute-done | bytes 131104 | tf_op jit(solution)/shard_map/ppermute | solution.py:62
  12.8 1.6 %fusion.20 = (f32[40,64,4]{2,1,0:T(8,128)}, f32[40,64,4]{2,1,0:T(8,128)S(1)}) fusion(f32[40,64,128]{2,1,0:T(8,128)S(1)} %constant_dynamic-update-slice_fusion), kind=kLoop, calls=%fused_computation.65 | loop fusion | bytes 163840 | tf_op jit(solution)/shard_map/slice | solution.py:52
  14.4 0.1 collective-permute-start.3
  14.4 0.1 slice_select_fusion
  14.6 1.7 %collective-permute-start.2 = (f32[40,4,4]{2,1,0:T(4,128)S(1)}, f32[40,4,4]{2,1,0:T(4,128)S(1)}, u32[]{:S(2)}, u32[]{:S(2)}) collective-permute-start(f32[40,4,4]{2,1,0:T(4,128)S(1)} %slice_select_fusion), channel_id=1, source_target_pairs={{0,24},{8,16},{16,8},{24,0},{1,25},{9,17},{17,9},{25,1},{2,26},{10... | collective-permute-start | bytes 7688 | tf_op jit(solution)/shard_map/ppermute | solution.py:62
  16.2 1.8 %copy.24 = f32[40,64,4]{1,0,2:T(8,128)S(1)} copy(f32[40,64,4]{2,1,0:T(8,128)} %get-tuple-element.9) | data formatting | bytes 81920 | tf_op jit(solution)/shard_map/slice | solution.py:52
  18.0 0.5 copy.23
  18.5 0.6 collective-permute-start.4
  19.1 0.0 collective-permute-done.2
  19.1 0.1 broadcast_select_fusion.7
  19.1 3.8 %collective-permute-done.4 = f32[40,64,4]{1,0,2:T(8,128)S(1)} collective-permute-done((f32[40,64,4]{1,0,2:T(8,128)S(1)}, f32[40,64,4]{1,0,2:T(8,128)S(1)}, u32[]{:S(2)}, u32[]{:S(2)}) %collective-permute-start.4) | collective-permute-done | bytes 40992 | tf_op jit(solution)/shard_map/ppermute | solution.py:62
  23.0 0.5 copy.25
  23.5 1.6 %copy.26 = f32[40,64,4]{2,1,0:T(8,128)} copy(f32[40,64,4]{1,0,2:T(8,128)S(1)} %get-tuple-element.26) | data formatting | bytes 81920 | tf_op jit(solution)/shard_map/jit(_where)/select_n | solution.py:82
  25.1 0.0 collective-permute-done.3
  25.1 3.6 %fusion.x_ref = f32[40,72,256]{2,1,0:T(8,128)S(1)} fusion(f32[40,4,4]{2,1,0:T(4,128)S(1)} %get-tuple-element.20, f32[40,4,128]{2,1,0:T(4,128)S(1)} %get-tuple-element.24, f32[40,4,4]{2,1,0:T(4,128)S(1)} %get-tuple-element.21, f32[40,64,4]{2,1,0:T(8,128)} %copy.26, f32[40,4,4]{2,1,0:T(4,128)S(1)} %get-tuple-element.22, ...), kind=kLoop, calls=%fused_computation.1 | loop fusion | flops 13271040 | bytes 4515840 | tf_op jit(solution)/shard_map/concatenate | solution.py:101
  28.7 30.8 %shard_map.55 = f32[4,64,128]{2,1,0:T(8,128)S(1)} custom-call(s32[6]{0:T(128)S(1)} %stack.27.lim_ref, f32[24]{0:T(128)S(1)} %pad_maximum_fusion.1.prm_ref, f32[40,72,256]{2,1,0:T(8,128)S(1)} %fusion.x_ref), custom_call_target="tpu_custom_call" | custom-call | flops 133693440 | bytes 3080192 | tf_op jit(solution)/shard_map/pallas_call | solution.py:180
  59.5 12.9 %all_to_all.5 = f32[4,8,8,128]{3,2,0,1:T(8,128)S(1)} all-to-all(f32[4,8,8,128]{3,2,0,1:T(8,128)S(1)} %copy.27), channel_id=1, replica_groups=mesh['gx'=2,'gy'=2,'gz'=8] {'gz'}, dimensions={1} | all-to-all | bytes 262144 | tf_op jit(solution)/shard_map/all_to_all | solution.py:231
  72.4 0.6 pad_maximum_fusion
  (11 shorter events, 0.2 us)
Async XLA Ops:
  1.0 7.9 %collective-permute-start = (f32[4,64,128]{2,1,0:T(8,128)S(1)}, f32[4,64,128]{2,1,0:T(8,128)S(1)}, u32[]{:S(2)}, u32[]{:S(2)}) collective-permute-start(f32[4,64,128]{2,1,0:T(8,128)S(1)} %get-tuple-element.12), channel_id=1, source_target_pairs={{0,1},{1,2},{2,3},{3,4},{4,5},{5,6},{6,7},{8,9},{9,10},{10,11},{11... | collective-permute-start | bytes 393224 | tf_op jit(solution)/shard_map/ppermute | solution.py:62
  5.9 6.9 %collective-permute-start.1 = (f32[4,64,128]{2,1,0:T(8,128)S(1)}, f32[4,64,128]{2,1,0:T(8,128)S(1)}, u32[]{:S(2)}, u32[]{:S(2)}) collective-permute-start(f32[4,64,128]{2,1,0:T(8,128)S(1)} %get-tuple-element.11), channel_id=1, source_target_pairs={{1,0},{2,1},{3,2},{4,3},{5,4},{6,5},{7,6},{9,8},{10,9},{11,10},{12... | collective-permute-start | bytes 393224 | tf_op jit(solution)/shard_map/ppermute | solution.py:62
  14.4 10.7 %collective-permute-start.3 = (f32[40,4,128]{2,1,0:T(4,128)S(1)}, f32[40,4,128]{2,1,0:T(4,128)S(1)}, u32[]{:S(2)}, u32[]{:S(2)}) collective-permute-start(f32[40,4,128]{2,1,0:T(4,128)S(1)} %slice_select_fusion.1), channel_id=1, source_target_pairs={{0,16},{16,0},{1,17},{17,1},{2,18},{18,2},{3,19},{19,3},{4,20},{20... | collective-permute-start | bytes 245768 | tf_op jit(solution)/shard_map/ppermute | solution.py:62
  14.6 4.5 %collective-permute-start.2 = (f32[40,4,4]{2,1,0:T(4,128)S(1)}, f32[40,4,4]{2,1,0:T(4,128)S(1)}, u32[]{:S(2)}, u32[]{:S(2)}) collective-permute-start(f32[40,4,4]{2,1,0:T(4,128)S(1)} %slice_select_fusion), channel_id=1, source_target_pairs={{0,24},{8,16},{16,8},{24,0},{1,25},{9,17},{17,9},{25,1},{2,26},{10... | collective-permute-start | bytes 7688 | tf_op jit(solution)/shard_map/ppermute | solution.py:62
  18.5 4.5 %collective-permute-start.4 = (f32[40,64,4]{1,0,2:T(8,128)S(1)}, f32[40,64,4]{1,0,2:T(8,128)S(1)}, u32[]{:S(2)}, u32[]{:S(2)}) collective-permute-start(f32[40,64,4]{1,0,2:T(8,128)S(1)} %broadcast_select_fusion.8), channel_id=1, source_target_pairs={{0,8},{8,0},{1,9},{9,1},{2,10},{10,2},{3,11},{11,3},{4,12},{12,4},... | collective-permute-start | bytes 122888 | tf_op jit(solution)/shard_map/ppermute | solution.py:62

commit v3 on v2

--- a/solution.py
+++ b/solution.py
@@ -83,24 +83,16 @@
             blocks[key] = val if key not in blocks else blocks[key] + val
     blocks[tuple("mid" for _ in dims)] = x
 
-    def block_shape(key):
+    def block(*key):
+        if key in blocks:
+            return blocks[key]
         shape = list(x.shape)
         for d, k in zip(dims, key):
             if k != "mid":
                 shape[d] = width
-        return shape
-
-    def assemble(prefix):
-        level = len(prefix)
-        if level == len(dims):
-            key = tuple(prefix)
-            if key in blocks:
-                return blocks[key]
-            return jnp.zeros(block_shape(key), x.dtype)
-        parts = [assemble(prefix + [k]) for k in ("lo", "mid", "hi")]
-        return jnp.concatenate(parts, axis=dims[level])
-
-    return assemble([])
+        return jnp.zeros(shape, x.dtype)
+
+    return block
 
 
 def flux(d, rate):
@@ -108,30 +100,48 @@
     return rate * d / (1.0 + q * q)
 
 
-def render_kernel(lim_ref, prm_ref, x_ref, out_ref, a_ref, b_ref, m_ref, *, interior, h):
-    depth, rows, lanes = x_ref.shape
+def render_kernel(lim_ref, prm_ref, x_hbm, zlo_hbm, zhi_hbm, rband_hbm, cband_hbm, out_ref, a_ref, b_ref, m_ref, sem,
+                  *, interior, h):
+    depth, rows, lanes = a_ref.shape
     d_in, r_in, l_in = interior
     halo = STEPS
+    copies = [
+        pltpu.make_async_copy(x_hbm, b_ref.at[halo:halo + d_in, 0:r_in, 0:l_in], sem.at[0]),
+        pltpu.make_async_copy(zlo_hbm, b_ref.at[0:halo, 0:r_in, 0:l_in], sem.at[1]),
+        pltpu.make_async_copy(zhi_hbm, b_ref.at[halo + d_in:depth, 0:r_in, 0:l_in], sem.at[2]),
+        pltpu.make_async_copy(rband_hbm, b_ref.at[:, r_in:rows, 0:l_in], sem.at[3]),
+        pltpu.make_async_copy(cband_hbm, b_ref.at[:, :, l_in:lanes], sem.at[4]),
+    ]
+    for cp in copies:
+        cp.start()
 
     row = lax.broadcasted_iota(jnp.int32, (rows, lanes), 0)
     lane = lax.broadcasted_iota(jnp.int32, (rows, lanes), 1)
-    ok = (row >= lim_ref[2]) & (row < lim_ref[3]) & (lane >= lim_ref[4]) & (lane < lim_ref[5])
+    row_at = jnp.where(row < r_in + halo, row, row - rows)
+    lane_at = jnp.where(lane < (l_in + lanes) // 2, lane, lane - lanes)
+    ok = (row_at >= lim_ref[2]) & (row_at < lim_ref[3]) & (lane_at >= lim_ref[4]) & (lane_at < lim_ref[5])
     m_ref[...] = jnp.where(ok, 1.0, 0.0).astype(jnp.float32)
 
-    def plane_update(src, z, g_prev):
-        c = src[z]
-        g = flux(src[z + 1] - c, RATE_DEPTH)
-        fr = flux(pltpu.roll(c, rows - 1, 0) - c, RATE_PLANE)
-        fc = flux(pltpu.roll(c, lanes - 1, 1) - c, RATE_PLANE)
-        new = c + (g - g_prev) + (fr - pltpu.roll(fr, 1, 0)) + (fc - pltpu.roll(fc, 1, 1))
-        return new, g
+    cen = [prm_ref[k] for k in range(MATERIALS)]
+    wid = [prm_ref[MATERIALS + k] for k in range(MATERIALS)]
+    den = [prm_ref[2 * MATERIALS + k] for k in range(MATERIALS)]
+    col = [[prm_ref[3 * MATERIALS + ch * MATERIALS + k] for k in range(MATERIALS)] for ch in range(CHANNELS)]
+    for ch in range(CHANNELS + 1):
+        out_ref[ch] = jnp.zeros((r_in, l_in), jnp.float32)
+
+    for cp in copies:
+        cp.wait()
 
     def smooth(src, dst, s):
         z0, z1 = s + 1, depth - 1 - s
         g0 = flux(src[z0] - src[z0 - 1], RATE_DEPTH)
 
         def body(z, g_prev):
-            new, g = plane_update(src, z, g_prev)
+            c = src[z]
+            g = flux(src[z + 1] - c, RATE_DEPTH)
+            fr = flux(pltpu.roll(c, rows - 1, 0) - c, RATE_PLANE)
+            fc = flux(pltpu.roll(c, lanes - 1, 1) - c, RATE_PLANE)
+            new = c + (g - g_prev) + (fr - pltpu.roll(fr, 1, 0)) + (fc - pltpu.roll(fc, 1, 1))
             inside = (z >= lim_ref[0]) & (z < lim_ref[1])
             zf = jnp.where(inside, 1.0, 0.0).astype(jnp.float32)
             dst[z] = new * (m_ref[...] * zf)
@@ -139,24 +149,21 @@
 
         lax.fori_loop(z0, z1, body, g0)
 
-    smooth(x_ref, a_ref, 0)
+    smooth(b_ref, a_ref, 0)
     smooth(a_ref, b_ref, 1)
     smooth(b_ref, a_ref, 2)
 
-    cen = [prm_ref[k] for k in range(MATERIALS)]
-    wid = [prm_ref[MATERIALS + k] for k in range(MATERIALS)]
-    den = [prm_ref[2 * MATERIALS + k] for k in range(MATERIALS)]
-    col = [[prm_ref[3 * MATERIALS + ch * MATERIALS + k] for k in range(MATERIALS)] for ch in range(CHANNELS)]
-
-    for ch in range(CHANNELS + 1):
-        out_ref[ch] = jnp.zeros((r_in, l_in), jnp.float32)
-
     z0, z1 = halo, halo + d_in
-    g0 = flux(a_ref[z0] - a_ref[z0 - 1], RATE_DEPTH)
+    g0 = flux(a_ref[z0, 0:r_in, 0:l_in] - a_ref[z0 - 1, 0:r_in, 0:l_in], RATE_DEPTH)
 
     def final(z, g_prev):
-        new, g = plane_update(a_ref, z, g_prev)
-        v = pltpu.roll(pltpu.roll(new, rows - halo, 0), lanes - halo, 1)[:r_in, :l_in]
+        ci = a_ref[z, 0:r_in, 0:l_in]
+        g = flux(a_ref[z + 1, 0:r_in, 0:l_in] - ci, RATE_DEPTH)
+        c0 = a_ref[z, :, 0:l_in]
+        fr = flux(pltpu.roll(c0, rows - 1, 0) - c0, RATE_PLANE)
+        cr = a_ref[z, 0:r_in, :]
+        fc = flux(pltpu.roll(cr, lanes - 1, 1) - cr, RATE_PLANE)
+        v = ci + (g - g_prev) + (fr - pltpu.roll(fr, 1, 0))[0:r_in] + (fc - pltpu.roll(fc, 1, 1))[:, 0:l_in]
         bumps = [den[k] * jnp.exp(-(((v - cen[k]) / wid[k]) ** 2)) for k in range(MATERIALS)]
         ext = bumps[0] + bumps[1] + bumps[2] + bumps[3]
         run = out_ref[CHANNELS]
@@ -172,24 +179,21 @@
         out_ref[ch] = h * out_ref[ch]
 
 
-def render_block(padded, lim, prm, interior, h):
-    depth, rows, lanes = padded.shape
+def render_block(pieces, lim, prm, interior, h):
     d_in, r_in, l_in = interior
+    depth, rows, lanes = d_in + 2 * STEPS, r_in + 2 * STEPS, LANES
     cells = depth * rows * lanes
     kernel = functools.partial(render_kernel, interior=interior, h=h)
     return pl.pallas_call(
         kernel,
         out_shape=jax.ShapeDtypeStruct((CHANNELS + 1, r_in, l_in), jnp.float32),
-        in_specs=[
-            pl.BlockSpec(memory_space=pltpu.SMEM),
-            pl.BlockSpec(memory_space=pltpu.SMEM),
-            pl.BlockSpec(memory_space=pltpu.VMEM),
-        ],
+        in_specs=[pl.BlockSpec(memory_space=pltpu.SMEM)] * 2 + [pl.BlockSpec(memory_space=pl.ANY)] * 5,
         out_specs=pl.BlockSpec(memory_space=pltpu.VMEM),
         scratch_shapes=[
             pltpu.VMEM((depth, rows, lanes), jnp.float32),
             pltpu.VMEM((depth, rows, lanes), jnp.float32),
             pltpu.VMEM((rows, lanes), jnp.float32),
+            pltpu.SemaphoreType.DMA((5,)),
         ],
         compiler_params=pltpu.CompilerParams(vmem_limit_bytes=48 * 1024 * 1024),
         cost_estimate=pl.CostEstimate(
@@ -197,21 +201,26 @@
             transcendentals=int(d_in * r_in * l_in * (MATERIALS + 1)),
             bytes_accessed=int(cells * 4 + (CHANNELS + 1) * r_in * l_in * 4),
         ),
-    )(lim, prm, padded)
+    )(lim, prm, *pieces)
 
 
 def shards(phase_field, centres, widths, densities, colours):
     depth_cells, row_cells, col_cells = phase_field.shape
     groups = lax.axis_size("gz")
     h = 1.0 / (depth_cells * groups)
-    padded = halo_stage(phase_field, ((0, "gz"),), STEPS)
-    padded = halo_stage(padded, ((1, "gx"), (2, "gy")), STEPS)
-    fill = (padded.shape[0], padded.shape[1], LANES - padded.shape[2])
-    padded = jnp.concatenate([padded, jnp.zeros(fill, padded.dtype)], axis=2)
+    zblock = halo_stage(phase_field, ((0, "gz"),), STEPS)
+    zlo, zhi = zblock("lo"), zblock("hi")
+    deep = jnp.concatenate([zlo, phase_field, zhi], axis=0)
+    plane = halo_stage(deep, ((1, "gx"), (2, "gy")), STEPS)
+    rband = jnp.concatenate([plane("hi", "mid"), plane("lo", "mid")], axis=1)
+    right = jnp.concatenate([plane("mid", "hi"), plane("hi", "hi"), plane("lo", "hi")], axis=1)
+    left = jnp.concatenate([plane("mid", "lo"), plane("hi", "lo"), plane("lo", "lo")], axis=1)
+    fill = jnp.zeros(right.shape[:2] + (LANES - col_cells - 2 * STEPS,), jnp.float32)
+    cband = jnp.concatenate([right, fill, left], axis=2)
 
     z_lo = STEPS - lax.axis_index("gz") * depth_cells
-    r_lo = STEPS - lax.axis_index("gx") * row_cells
-    c_lo = STEPS - lax.axis_index("gy") * col_cells
+    r_lo = -lax.axis_index("gx") * row_cells
+    c_lo = -lax.axis_index("gy") * col_cells
     lim = jnp.stack(
         [
             z_lo,
@@ -224,7 +233,7 @@
     ).astype(jnp.int32)
     prm = jnp.concatenate([centres, widths, densities, colours.reshape(-1)]).astype(jnp.float32)
 
-    seg = render_block(padded, lim, prm, (depth_cells, row_cells, col_cells), h)
+    seg = render_block((phase_field, zlo, zhi, rband, cband), lim, prm, (depth_cells, row_cells, col_cells), h)
 
     rows_part = row_cells // groups
     parts = seg.reshape(CHANNELS + 1, groups, rows_part, col_cells)

time: 73.3 us -> 65 us (0.89)
  other arithmetic: 5.24 us -> 2.21 us
  local copies, waits for them, and re-layouts: 8.99 us -> 6.2 us
  Pallas kernels: 30.8 us -> 28.3 us
    concatenate x1 -> x2, other arithmetic: 3.57 us -> 0.54 us  [the longest x1 0.5 us: shards(): cband = jnp.concatenate([right, fill, left], axis=2)]
    pallas_call x1, Pallas kernels: 30.8 us -> 28.3 us  [render_block(): pl.pallas_call(kernel, out_shape=jax.ShapeDtypeStruct((CHANNELS + 1, r_in...]
    slice x3, local copies, waits for them, and re-layouts: 4.3 us -> 1.92 us  [halo_stage(): lo = lax.slice_in_dim(piece, 0, width, axis=d)]
    select_n x2, local copies, waits for them, and re-layouts: 2.04 us -> 0.94 us  [halo_stage(): val = got if cond is True else jnp.where(cond, got, 0.0)]
    unnamed x2 -> x4, local copies, waits for them, and re-layouts: 1.31 us -> 1.93 us
  transfers between devices with their start and end apart: 5 -> 5, of which waited for: 2 -> 3; matrix products, arithmetic and copies ran while one was open for 10% -> 9% of each run, Pallas kernels for 0% -> 0%
where the time goes in v3:
time: 65 us; the launch traced here: 64.7 us
  Pallas kernels  28.3 us (44%)
  blocking collectives  12.9 us (20%)
  starting transfers between devices  8.53 us (13%)
  waiting for transfers between devices  6.35 us (10%)
  local copies, waits for them, and re-layouts  6.2 us (10%)
  other arithmetic  2.21 us (3%)
    pallas_call x1, Pallas kernels, render_block(): pl.pallas_call(kernel, out_shape=jax.ShapeDtypeStruct((CHANNELS + 1, r_in...  28.3 us
    all_to_all x1, blocking collectives, shards(): got = lax.all_to_all(parts, 'gz', 1, 1, tiled=True)  12.9 us
    ppermute x5, starting transfers between devices, halo_stage(): got = lax.ppermute(piece, tuple((a for a, _, _ in used)), pairs)  8.53 us
    ppermute x5, waiting for transfers between devices, halo_stage(): got = lax.ppermute(piece, tuple((a for a, _, _ in used)), pairs)  6.35 us
    unnamed x4, local copies, waits for them, and re-layouts  1.93 us
    slice x3, local copies, waits for them, and re-layouts, halo_stage(): lo = lax.slice_in_dim(piece, 0, width, axis=d)  1.92 us
  transfers between devices with their start and end apart: 5, of which 3 were waited for; matrix products, arithmetic and copies ran while one was open for 9% of the time, Pallas kernels for 0%

profile of v3, /device:TPU:0, one launch (start us, length us, event | category | flops | bytes accessed | tf_op | source)
XLA Modules:
  0.0 64.7 jit_solution(16686071217452914056)
XLA Ops:
  0.0 1.0 %fusion.19 = (f32[4,64,128]{2,1,0:T(8,128)S(1)}, f32[4,64,128]{2,1,0:T(8,128)S(1)}) fusion(f32[32,64,128]{2,1,0:T(8,128)} %x_hbm.1), kind=kLoop, calls=%fused_computation.59 | loop fusion | bytes 524288 | tf_op jit(solution)/shard_map/slice | solution.py:52
  1.0 4.9 %collective-permute-start = (f32[4,64,128]{2,1,0:T(8,128)S(1)}, f32[4,64,128]{2,1,0:T(8,128)S(1)}, u32[]{:S(2)}, u32[]{:S(2)}) collective-permute-start(f32[4,64,128]{2,1,0:T(8,128)S(1)} %get-tuple-element.12), channel_id=1, source_target_pairs={{0,1},{1,2},{2,3},{3,4},{4,5},{5,6},{6,7},{8,9},{9,10},{10,11},{11... | collective-permute-start | bytes 393224 | tf_op jit(solution)/shard_map/ppermute | solution.py:62
  5.9 1.3 %collective-permute-start.1 = (f32[4,64,128]{2,1,0:T(8,128)S(1)}, f32[4,64,128]{2,1,0:T(8,128)S(1)}, u32[]{:S(2)}, u32[]{:S(2)}) collective-permute-start(f32[4,64,128]{2,1,0:T(8,128)S(1)} %get-tuple-element.11), channel_id=1, source_target_pairs={{1,0},{2,1},{3,2},{4,3},{5,4},{6,5},{7,6},{9,8},{10,9},{11,10},{12... | collective-permute-start | bytes 393224 | tf_op jit(solution)/shard_map/ppermute | solution.py:62
  7.3 0.8 %reshape.210 = f32[12]{0:T(128)S(1)} reshape(f32[3,4]{1,0:T(4,128)} %param.9) | data formatting | bytes 96 | tf_op jit(solution)/shard_map/reshape | solution.py:234
  8.0 0.1 pad.5.clone
  8.1 0.1 stack.27.lim_ref
  8.2 0.8 %pad_maximum_fusion.2.prm_ref = f32[24]{0:T(128)S(1)} fusion(f32[12]{0:T(128)S(1)} %reshape.210, f32[4]{0:T(128)} %param.8, f32[4]{0:T(128)} %param.7, f32[4]{0:T(128)} %param.6), kind=kLoop, calls=%fused_computation.57 | loop fusion | flops 72 | bytes 192 | tf_op jit(solution)/shard_map/concatenate | solution.py:234
  8.9 0.0 collective-permute-done.zlo_hbm
  9.0 1.3 %constant_dynamic-update-slice_fusion.1 = f32[40,64,128]{2,1,0:T(8,128)S(1)} fusion(f32[40,64,128]{2,1,0:T(8,128)S(1)} %constant_dynamic-update-slice_fusion.2, f32[32,64,128]{2,1,0:T(8,128)} %x_hbm.1), kind=kLoop, calls=%fused_computation.37 | loop fusion | bytes 2097152
  10.3 2.5 %collective-permute-done.1.zhi_hbm = f32[4,64,128]{2,1,0:T(8,128)S(1)} collective-permute-done((f32[4,64,128]{2,1,0:T(8,128)S(1)}, f32[4,64,128]{2,1,0:T(8,128)S(1)}, u32[]{:S(2)}, u32[]{:S(2)}) %collective-permute-start.1) | collective-permute-done | bytes 131104 | tf_op jit(solution)/shard_map/ppermute | solution.py:62
  12.8 0.5 fusion.18
  13.3 0.1 collective-permute-start.2
  13.4 0.1 slice_select_fusion
  13.5 1.7 %collective-permute-start.4 = (f32[40,4,4]{2,1,0:T(4,128)S(1)}, f32[40,4,4]{2,1,0:T(4,128)S(1)}, u32[]{:S(2)}, u32[]{:S(2)}) collective-permute-start(f32[40,4,4]{2,1,0:T(4,128)S(1)} %slice_select_fusion), channel_id=1, source_target_pairs={{0,24},{8,16},{16,8},{24,0},{1,25},{9,17},{17,9},{25,1},{2,26},{10... | collective-permute-start | bytes 7688 | tf_op jit(solution)/shard_map/ppermute | solution.py:62
  15.1 0.5 copy.33
  15.6 0.5 copy.34
  16.1 0.6 collective-permute-start.3
  16.7 1.1 %collective-permute-done.4 = f32[40,4,4]{2,1,0:T(4,128)S(1)} collective-permute-done((f32[40,4,4]{2,1,0:T(4,128)S(1)}, f32[40,4,4]{2,1,0:T(4,128)S(1)}, u32[]{:S(2)}, u32[]{:S(2)}) %collective-permute-start.4) | collective-permute-done | bytes 2592 | tf_op jit(solution)/shard_map/ppermute | solution.py:62
  17.8 0.1 broadcast_select_fusion.3
  17.8 2.8 %collective-permute-done.3 = f32[40,64,4]{1,0,2:T(8,128)S(1)} collective-permute-done((f32[40,64,4]{1,0,2:T(8,128)S(1)}, f32[40,64,4]{1,0,2:T(8,128)S(1)}, u32[]{:S(2)}, u32[]{:S(2)}) %collective-permute-start.3) | collective-permute-done | bytes 40992 | tf_op jit(solution)/shard_map/ppermute | solution.py:62
  20.6 0.5 copy.35
  21.1 0.5 copy.36
  21.6 0.0 copy-start
  21.6 0.5 maximum_maximum_fusion.cband_hbm
  22.1 0.0 collective-permute-done.2
  22.2 0.6 copy-done
  22.8 28.3 %shard_map.55 = f32[4,64,128]{2,1,0:T(8,128)S(1)} custom-call(s32[6]{0:T(128)S(1)} %stack.27.lim_ref, f32[24]{0:T(128)S(1)} %pad_maximum_fusion.2.prm_ref, f32[32,64,128]{2,1,0:T(8,128)S(1)} %copy-done, f32[4,64,128]{2,1,0:T(8,128)S(1)} %collective-permute-done.zlo_hbm, f32[4,64,128]{2,1,0:T(8,128)S(1)} %collective-permute-done.1.zhi_hbm, ...), custom_call_target="tpu_custom_call" | custom-call | flops 133693440 | bytes 3080192 | tf_op jit(solution)/shard_map/pallas_call | solution.py:187
  51.2 12.9 %all_to_all.5 = f32[4,8,8,128]{3,2,0,1:T(8,128)S(1)} all-to-all(f32[4,8,8,128]{3,2,0,1:T(8,128)S(1)} %copy.37), channel_id=1, replica_groups=mesh['gx'=2,'gy'=2,'gz'=8] {'gz'}, dimensions={1} | all-to-all | bytes 262144 | tf_op jit(solution)/shard_map/all_to_all | solution.py:240
  64.1 0.6 pad_maximum_fusion.1
  (13 shorter events, 0.2 us)
Async XLA Ops:
  1.0 8.0 %collective-permute-start = (f32[4,64,128]{2,1,0:T(8,128)S(1)}, f32[4,64,128]{2,1,0:T(8,128)S(1)}, u32[]{:S(2)}, u32[]{:S(2)}) collective-permute-start(f32[4,64,128]{2,1,0:T(8,128)S(1)} %get-tuple-element.12), channel_id=1, source_target_pairs={{0,1},{1,2},{2,3},{3,4},{4,5},{5,6},{6,7},{8,9},{9,10},{10,11},{11... | collective-permute-start | bytes 393224 | tf_op jit(solution)/shard_map/ppermute | solution.py:62
  5.9 6.9 %collective-permute-start.1 = (f32[4,64,128]{2,1,0:T(8,128)S(1)}, f32[4,64,128]{2,1,0:T(8,128)S(1)}, u32[]{:S(2)}, u32[]{:S(2)}) collective-permute-start(f32[4,64,128]{2,1,0:T(8,128)S(1)} %get-tuple-element.11), channel_id=1, source_target_pairs={{1,0},{2,1},{3,2},{4,3},{5,4},{6,5},{7,6},{9,8},{10,9},{11,10},{12... | collective-permute-start | bytes 393224 | tf_op jit(solution)/shard_map/ppermute | solution.py:62
  13.3 8.8 %collective-permute-start.2 = (f32[40,4,128]{2,1,0:T(4,128)S(1)}, f32[40,4,128]{2,1,0:T(4,128)S(1)}, u32[]{:S(2)}, u32[]{:S(2)}) collective-permute-start(f32[40,4,128]{2,1,0:T(4,128)S(1)} %slice_select_fusion.1), channel_id=1, source_target_pairs={{0,16},{16,0},{1,17},{17,1},{2,18},{18,2},{3,19},{19,3},{4,20},{20... | collective-permute-start | bytes 245768 | tf_op jit(solution)/shard_map/ppermute | solution.py:62
  13.5 4.3 %collective-permute-start.4 = (f32[40,4,4]{2,1,0:T(4,128)S(1)}, f32[40,4,4]{2,1,0:T(4,128)S(1)}, u32[]{:S(2)}, u32[]{:S(2)}) collective-permute-start(f32[40,4,4]{2,1,0:T(4,128)S(1)} %slice_select_fusion), channel_id=1, source_target_pairs={{0,24},{8,16},{16,8},{24,0},{1,25},{9,17},{17,9},{25,1},{2,26},{10... | collective-permute-start | bytes 7688 | tf_op jit(solution)/shard_map/ppermute | solution.py:62
  16.1 4.5 %collective-permute-start.3 = (f32[40,64,4]{1,0,2:T(8,128)S(1)}, f32[40,64,4]{1,0,2:T(8,128)S(1)}, u32[]{:S(2)}, u32[]{:S(2)}) collective-permute-start(f32[40,64,4]{1,0,2:T(8,128)S(1)} %broadcast_select_fusion.8), channel_id=1, source_target_pairs={{0,8},{8,0},{1,9},{9,1},{2,10},{10,2},{3,11},{11,3},{4,12},{12,4},... | collective-permute-start | bytes 122888 | tf_op jit(solution)/shard_map/ppermute | solution.py:62
  21.6 1.2 %copy-start = (f32[32,64,128]{2,1,0:T(8,128)S(1)}, f32[32,64,128]{2,1,0:T(8,128)}, u32[]{:S(2)}) copy-start(f32[32,64,128]{2,1,0:T(8,128)} %x_hbm.1) | copy-start | bytes 3145732

commit v4 on v3

--- a/solution.py
+++ b/solution.py
@@ -36,7 +36,7 @@
     return [(up, True, True), (down, False, False)]
 
 
-def halo_stage(x, dim_axes, width):
+def halo_stage(x, dim_axes, width, order):
     dims = [d for d, _ in dim_axes]
     axes = [a for _, a in dim_axes]
     sizes = [lax.axis_size(a) for a in axes]
@@ -53,6 +53,7 @@
                 hi = lax.slice_in_dim(piece, n_d - width, n_d, axis=d)
                 piece = pick(m[1], hi, lo)
         used = [(a, s, m) for a, s, m in zip(axes, sizes, combo) if m is not None]
+        used.sort(key=lambda u: order.index(u[0]))
         pairs = []
         for parts in itertools.product(*[m[0] for _, _, m in used]):
             src = dst = 0
@@ -204,17 +205,20 @@
     )(lim, prm, *pieces)
 
 
-def shards(phase_field, centres, widths, densities, colours):
+def shards(phase_field, centres, widths, densities, colours, order):
     depth_cells, row_cells, col_cells = phase_field.shape
     groups = lax.axis_size("gz")
     h = 1.0 / (depth_cells * groups)
-    zblock = halo_stage(phase_field, ((0, "gz"),), STEPS)
-    zlo, zhi = zblock("lo"), zblock("hi")
-    deep = jnp.concatenate([zlo, phase_field, zhi], axis=0)
-    plane = halo_stage(deep, ((1, "gx"), (2, "gy")), STEPS)
-    rband = jnp.concatenate([plane("hi", "mid"), plane("lo", "mid")], axis=1)
-    right = jnp.concatenate([plane("mid", "hi"), plane("hi", "hi"), plane("lo", "hi")], axis=1)
-    left = jnp.concatenate([plane("mid", "lo"), plane("hi", "lo"), plane("lo", "lo")], axis=1)
+    block = halo_stage(phase_field, ((0, "gz"), (1, "gx"), (2, "gy")), STEPS, order)
+    zlo, zhi = block("lo", "mid", "mid"), block("hi", "mid", "mid")
+    sides = ("lo", "mid", "hi")
+
+    def band(parts):
+        return jnp.concatenate([jnp.concatenate([block(zs, r, c) for r, c in parts], axis=1) for zs in sides], axis=0)
+
+    rband = band((("hi", "mid"), ("lo", "mid")))
+    right = band((("mid", "hi"), ("hi", "hi"), ("lo", "hi")))
+    left = band((("mid", "lo"), ("hi", "lo"), ("lo", "lo")))
     fill = jnp.zeros(right.shape[:2] + (LANES - col_cells - 2 * STEPS,), jnp.float32)
     cband = jnp.concatenate([right, fill, left], axis=2)
 
@@ -250,5 +254,5 @@
 def solution(mesh):
     placed = (P("gz", "gx", "gy"), P(), P(), P(), P())
     return jax.shard_map(
-        shards, mesh=mesh, in_specs=placed, out_specs=P(None, ("gx", "gz"), "gy"), check_vma=False
+        functools.partial(shards, order=tuple(mesh.axis_names)), mesh=mesh, in_specs=placed, out_specs=P(None, ("gx", "gz"), "gy"), check_vma=False
     )

time: 65 us -> 102 us (1.57)
  starting transfers between devices: 8.53 us -> 29.5 us
  other arithmetic: 2.21 us -> 15.1 us
  waiting for transfers between devices: 6.35 us -> 9.15 us
    ppermute x5 -> x11, starting transfers between devices: 8.53 us -> 29.5 us  [halo_stage(): got = lax.ppermute(piece, tuple((a for a, _, _ in used)), pairs)]
    select_n x3 -> x9, other arithmetic: 0.1 us -> 7.47 us  [halo_stage(): val = got if cond is True else jnp.where(cond, got, 0.0)]
    concatenate x1, other arithmetic: 0.5 us -> 4.11 us  [shards(): cband = jnp.concatenate([right, fill, left], axis=2)]
    ppermute x5 -> x11, waiting for transfers between devices: 6.35 us -> 9.15 us  [halo_stage(): got = lax.ppermute(piece, tuple((a for a, _, _ in used)), pairs)]
    select_n x3 -> x7, other arithmetic: 0.16 us -> 2.79 us  [pick(): return jnp.where(cond, a, b)]
    unnamed x4 -> x20, local copies, waits for them, and re-layouts: 1.93 us -> 0.8 us
    slice x3 -> x2, local copies, waits for them, and re-layouts: 1.92 us -> 2.77 us  [halo_stage(): lo = lax.slice_in_dim(piece, 0, width, axis=d)]
  transfers between devices with their start and end apart: 5 -> 11, of which waited for: 3 -> 3; matrix products, arithmetic and copies ran while one was open for 9% -> 19% of each run, Pallas kernels for 0% -> 0%
where the time goes in v4:
time: 102 us
  starting transfers between devices  29.5 us (29%)
  Pallas kernels  28.3 us (28%)
  other arithmetic  15.1 us (15%)
  blocking collectives  13.2 us (13%)
  waiting for transfers between devices  9.15 us (9%)
  local copies, waits for them, and re-layouts  6.06 us (6%)
    ppermute x11, starting transfers between devices, halo_stage(): got = lax.ppermute(piece, tuple((a for a, _, _ in used)), pairs)  29.5 us
    pallas_call x1, Pallas kernels, render_block(): pl.pallas_call(kernel, out_shape=jax.ShapeDtypeStruct((CHANNELS + 1, r_in...  28.3 us
    all_to_all x1, blocking collectives, shards(): got = lax.all_to_all(parts, 'gz', 1, 1, tiled=True)  13.2 us
    ppermute x11, waiting for transfers between devices, halo_stage(): got = lax.ppermute(piece, tuple((a for a, _, _ in used)), pairs)  9.15 us
    select_n x9, other arithmetic, halo_stage(): val = got if cond is True else jnp.where(cond, got, 0.0)  7.47 us
    concatenate x1, other arithmetic, shards(): cband = jnp.concatenate([right, fill, left], axis=2)  4.11 us
    select_n x7, other arithmetic, pick(): return jnp.where(cond, a, b)  2.79 us
    slice x2, local copies, waits for them, and re-layouts, halo_stage(): lo = lax.slice_in_dim(piece, 0, width, axis=d)  2.77 us
  transfers between devices with their start and end apart: 11, of which 3 were waited for; matrix products, arithmetic and copies ran while one was open for 19% of the time, Pallas kernels for 0%

profile of v4, /device:TPU:0, one launch (start us, length us, event | category | flops | bytes accessed | tf_op | source)
XLA Modules:
  0.0 101.6 jit_solution(14520001242719441265)
XLA Ops:
  0.0 0.8 slice_select_fusion.7
  0.8 4.9 %collective-permute-start.2 = (f32[4,4,128]{2,1,0:T(4,128)S(1)}, f32[4,4,128]{2,1,0:T(4,128)}, u32[]{:S(2)}, u32[]{:S(2)}) collective-permute-start(f32[4,4,128]{2,1,0:T(4,128)S(1)} %get-tuple-element.13), channel_id=1, source_target_pairs={{0,17},{1,18},{2,19},{3,20},{4,21},{5,22},{6,23},{16,1},{17,2},{18... | collective-permute-start | bytes 24584 | tf_op jit(solution)/shard_map/ppermute | solution.py:63
  5.8 4.0 %collective-permute-start.6 = (f32[4,4,4]{2,1,0:T(4,128)S(1)}, f32[4,4,4]{2,1,0:T(4,128)S(1)}, u32[]{:S(2)}, u32[]{:S(2)}) collective-permute-start(f32[4,4,4]{2,1,0:T(4,128)S(1)} %slice_select_fusion.5), channel_id=1, source_target_pairs={{0,25},{1,26},{2,27},{3,28},{4,29},{5,30},{6,31},{8,17},{9,18},{10... | collective-permute-start | bytes 776 | tf_op jit(solution)/shard_map/ppermute | solution.py:63
  9.8 1.3 %collective-permute-start.4 = (f32[4,4,128]{2,1,0:T(4,128)S(1)}, f32[4,4,128]{2,1,0:T(4,128)}, u32[]{:S(2)}, u32[]{:S(2)}) collective-permute-start(f32[4,4,128]{2,1,0:T(4,128)S(1)} %get-tuple-element.14), channel_id=1, source_target_pairs={{1,16},{2,17},{3,18},{4,19},{5,20},{6,21},{7,22},{17,0},{18,1},{19... | collective-permute-start | bytes 24584 | tf_op jit(solution)/shard_map/ppermute | solution.py:63
  11.2 1.3 %collective-permute-start.10 = (f32[4,4,4]{2,1,0:T(4,128)S(1)}, f32[4,4,4]{2,1,0:T(4,128)S(1)}, u32[]{:S(2)}, u32[]{:S(2)}) collective-permute-start(f32[4,4,4]{2,1,0:T(4,128)S(1)} %slice_select_fusion.4), channel_id=1, source_target_pairs={{1,24},{2,25},{3,26},{4,27},{5,28},{6,29},{7,30},{9,16},{10,17},{1... | collective-permute-start | bytes 776 | tf_op jit(solution)/shard_map/ppermute | solution.py:63
  12.5 1.0 slice_select_fusion.3
  13.7 2.1 %fusion.18 = (f32[32,64,4]{2,1,0:T(8,128)S(1)}, f32[32,64,4]{2,1,0:T(8,128)S(1)}) fusion(f32[32,64,128]{2,1,0:T(8,128)} %x_hbm.1), kind=kLoop, calls=%fused_computation.77 | loop fusion | bytes 131072 | tf_op jit(solution)/shard_map/slice | solution.py:52
  15.8 0.8 slice_select_fusion.1
  16.6 0.7 fusion.19
  18.2 0.7 pad.11.clone
  19.0 0.6 collective-permute-start.8
  19.6 0.6 broadcast_select_fusion.20
  20.3 1.5 %collective-permute-start.7 = (f32[32,64,4]{1,0,2:T(8,128)S(1)}, f32[32,64,4]{1,0,2:T(8,128)S(1)}, u32[]{:S(2)}, u32[]{:S(2)}) collective-permute-start(f32[32,64,4]{1,0,2:T(8,128)S(1)} %broadcast_select_fusion.12), channel_id=1, source_target_pairs={{0,8},{8,0},{1,9},{9,1},{2,10},{10,2},{3,11},{11,3},{4,12},{12,4},... | collective-permute-start | bytes 98312 | tf_op jit(solution)/shard_map/ppermute | solution.py:63
  21.8 0.6 broadcast_select_fusion.18
  22.8 5.9 %collective-permute-start.5 = (f32[4,64,4]{2,1,0:T(8,128)}, f32[4,64,4]{2,1,0:T(8,128)S(1)}, u32[]{:S(2)}, u32[]{:S(2)}) collective-permute-start(f32[4,64,4]{2,1,0:T(8,128)} %get-tuple-element.9), channel_id=1, source_target_pairs={{0,9},{1,10},{2,11},{3,12},{4,13},{5,14},{6,15},{8,1},{9,2},{10,3}... | collective-permute-start | bytes 12296 | tf_op jit(solution)/shard_map/ppermute | solution.py:63
  28.7 0.7 broadcast_select_fusion.7
  29.4 2.6 %collective-permute-done.5 = f32[4,64,4]{2,1,0:T(8,128)S(1)} collective-permute-done((f32[4,64,4]{2,1,0:T(8,128)}, f32[4,64,4]{2,1,0:T(8,128)S(1)}, u32[]{:S(2)}, u32[]{:S(2)}) %collective-permute-start.5) | collective-permute-done | bytes 4128 | tf_op jit(solution)/shard_map/ppermute | solution.py:63
  32.1 1.3 %collective-permute-start.9 = (f32[4,64,4]{2,1,0:T(8,128)S(1)}, f32[4,64,4]{2,1,0:T(8,128)S(1)}, u32[]{:S(2)}, u32[]{:S(2)}) collective-permute-start(f32[4,64,4]{2,1,0:T(8,128)S(1)} %get-tuple-element.10), channel_id=1, source_target_pairs={{1,8},{2,9},{3,10},{4,11},{5,12},{6,13},{7,14},{9,0},{10,1},{11,2}... | collective-permute-start | bytes 12296 | tf_op jit(solution)/shard_map/ppermute | solution.py:63
  33.3 0.7 broadcast_select_fusion.3
  34.1 6.1 %collective-permute-done.9 = f32[4,64,4]{2,1,0:T(8,128)S(1)} collective-permute-done((f32[4,64,4]{2,1,0:T(8,128)S(1)}, f32[4,64,4]{2,1,0:T(8,128)S(1)}, u32[]{:S(2)}, u32[]{:S(2)}) %collective-permute-start.9) | collective-permute-done | bytes 4128 | tf_op jit(solution)/shard_map/ppermute | solution.py:63
  40.2 7.2 %collective-permute-start = (f32[4,64,128]{2,1,0:T(8,128)}, f32[4,64,128]{2,1,0:T(8,128)S(1)}, u32[]{:S(2)}, u32[]{:S(2)}) collective-permute-start(f32[4,64,128]{2,1,0:T(8,128)} %get-tuple-element.16), channel_id=1, source_target_pairs={{0,1},{1,2},{2,3},{3,4},{4,5},{5,6},{6,7},{8,9},{9,10},{10,11},{11... | collective-permute-start | bytes 393224 | tf_op jit(solution)/shard_map/ppermute | solution.py:63
  47.4 0.7 broadcast_select_fusion.2
  48.1 1.3 %collective-permute-start.1 = (f32[4,64,128]{2,1,0:T(8,128)}, f32[4,64,128]{2,1,0:T(8,128)S(1)}, u32[]{:S(2)}, u32[]{:S(2)}) collective-permute-start(f32[4,64,128]{2,1,0:T(8,128)} %get-tuple-element.15), channel_id=1, source_target_pairs={{1,0},{2,1},{3,2},{4,3},{5,4},{6,5},{7,6},{9,8},{10,9},{11,10},{12... | collective-permute-start | bytes 393224 | tf_op jit(solution)/shard_map/ppermute | solution.py:63
  49.4 1.3 %broadcast_select_fusion.24 = (f32[4,4,128]{2,1,0:T(4,128)}, f32[4,4,128]{2,1,0:T(4,128)}) fusion(f32[4,4,128]{2,1,0:T(4,128)} %collective-permute-done.2, pred[]{:T(512)S(6)} %not.4, pred[]{:T(512)S(6)} %eq.12), kind=kLoop, calls=%fused_computation.75 | loop fusion | flops 4096 | bytes 24578 | tf_op jit(solution)/shard_map/jit(_where)/select_n | solution.py:83
  50.7 1.3 %broadcast_select_fusion.22 = (f32[4,4,128]{2,1,0:T(4,128)}, f32[4,4,128]{2,1,0:T(4,128)}) fusion(f32[4,4,128]{2,1,0:T(4,128)} %collective-permute-done.4, pred[]{:T(512)S(6)} %not.4, pred[]{:T(512)S(6)} %eq.12), kind=kLoop, calls=%fused_computation.73 | loop fusion | flops 4096 | bytes 24578 | tf_op jit(solution)/shard_map/jit(_where)/select_n | solution.py:83
  52.0 0.6 broadcast_select_fusion.9
  53.0 1.2 %copy.59 = f32[32,64,4]{2,1,0:T(8,128)S(1)} copy(f32[32,64,4]{1,0,2:T(8,128)} %get-tuple-element.28) | data formatting | bytes 65536 | tf_op jit(solution)/shard_map/jit(_where)/select_n | solution.py:83
  54.3 4.1 %maximum_maximum_fusion.cband_hbm = f32[40,72,128]{2,1,0:T(8,128)S(1)} fusion(f32[4,4,4]{2,1,0:T(4,128)} %get-tuple-element.40, f32[4,4,4]{2,1,0:T(4,128)} %get-tuple-element.41, f32[4,64,4]{2,1,0:T(8,128)} %get-tuple-element.26, f32[32,4,4]{2,1,0:T(4,128)} %get-tuple-element.30, f32[32,4,4]{2,1,0:T(4,128)} %get-tuple-element.31, f32[32,64,4]{2,1,0:T(8,128)S(1)} %copy.59, ...), kind=kLoop, calls=%fused_computation | loop fusion | flops 6635520 | bytes 1567232 | tf_op jit(solution)/shard_map/concatenate | solution.py:223
  58.5 0.9 broadcast_select_fusion.11
  59.4 28.3 %shard_map.55 = f32[4,64,128]{2,1,0:T(8,128)S(1)} custom-call(s32[6]{0:T(128)S(1)} %stack.27.lim_ref, f32[24]{0:T(128)S(1)} %pad_maximum_fusion.1.prm_ref, f32[32,64,128]{2,1,0:T(8,128)S(1)} %copy-done, f32[4,64,128]{2,1,0:T(8,128)S(1)} %collective-permute-done.zlo_hbm, f32[4,64,128]{2,1,0:T(8,128)S(1)} %collective-permute-done.1.zhi_hbm, ...), custom_call_target="tpu_custom_call" | custom-call | flops 133693440 | bytes 3080192 | tf_op jit(solution)/shard_map/pallas_call | solution.py:188
  87.8 13.2 %all_to_all.5 = f32[4,8,8,128]{3,2,0,1:T(8,128)S(1)} all-to-all(f32[4,8,8,128]{3,2,0,1:T(8,128)S(1)} %copy.60), channel_id=1, replica_groups=mesh['gx'=2,'gy'=2,'gz'=8] {'gz'}, dimensions={1} | all-to-all | bytes 262144 | tf_op jit(solution)/shard_map/all_to_all | solution.py:244
  101.0 0.6 pad_maximum_fusion
  (45 shorter events, 2.3 us)
Async XLA Ops:
  0.8 47.3 %collective-permute-start.2 = (f32[4,4,128]{2,1,0:T(4,128)S(1)}, f32[4,4,128]{2,1,0:T(4,128)}, u32[]{:S(2)}, u32[]{:S(2)}) collective-permute-start(f32[4,4,128]{2,1,0:T(4,128)S(1)} %get-tuple-element.13), channel_id=1, source_target_pairs={{0,17},{1,18},{2,19},{3,20},{4,21},{5,22},{6,23},{16,1},{17,2},{18... | collective-permute-start | bytes 24584 | tf_op jit(solution)/shard_map/ppermute | solution.py:63
  5.8 13.2 %collective-permute-start.6 = (f32[4,4,4]{2,1,0:T(4,128)S(1)}, f32[4,4,4]{2,1,0:T(4,128)S(1)}, u32[]{:S(2)}, u32[]{:S(2)}) collective-permute-start(f32[4,4,4]{2,1,0:T(4,128)S(1)} %slice_select_fusion.5), channel_id=1, source_target_pairs={{0,25},{1,26},{2,27},{3,28},{4,29},{5,30},{6,31},{8,17},{9,18},{10... | collective-permute-start | bytes 776 | tf_op jit(solution)/shard_map/ppermute | solution.py:63
  9.8 40.9 %collective-permute-start.4 = (f32[4,4,128]{2,1,0:T(4,128)S(1)}, f32[4,4,128]{2,1,0:T(4,128)}, u32[]{:S(2)}, u32[]{:S(2)}) collective-permute-start(f32[4,4,128]{2,1,0:T(4,128)S(1)} %get-tuple-element.14), channel_id=1, source_target_pairs={{1,16},{2,17},{3,18},{4,19},{5,20},{6,21},{7,22},{17,0},{18,1},{19... | collective-permute-start | bytes 24584 | tf_op jit(solution)/shard_map/ppermute | solution.py:63
  11.2 9.1 %collective-permute-start.10 = (f32[4,4,4]{2,1,0:T(4,128)S(1)}, f32[4,4,4]{2,1,0:T(4,128)S(1)}, u32[]{:S(2)}, u32[]{:S(2)}) collective-permute-start(f32[4,4,4]{2,1,0:T(4,128)S(1)} %slice_select_fusion.4), channel_id=1, source_target_pairs={{1,24},{2,25},{3,26},{4,27},{5,28},{6,29},{7,30},{9,16},{10,17},{1... | collective-permute-start | bytes 776 | tf_op jit(solution)/shard_map/ppermute | solution.py:63
  13.5 45.0 %collective-permute-start.3 = (f32[32,4,128]{2,1,0:T(4,128)S(1)}, f32[32,4,128]{2,1,0:T(4,128)}, u32[]{:S(2)}, u32[]{:S(2)}) collective-permute-start(f32[32,4,128]{2,1,0:T(4,128)S(1)} %slice_select_fusion.3), channel_id=1, source_target_pairs={{0,16},{16,0},{1,17},{17,1},{2,18},{18,2},{3,19},{19,3},{4,20},{20... | collective-permute-start | bytes 196616 | tf_op jit(solution)/shard_map/ppermute | solution.py:63
  13.7 2.1 %copy-start = (f32[32,64,128]{2,1,0:T(8,128)S(1)}, f32[32,64,128]{2,1,0:T(8,128)}, u32[]{:S(2)}) copy-start(f32[32,64,128]{2,1,0:T(8,128)} %x_hbm.1) | copy-start | bytes 3145732
  16.6 1.5 %copy-start.5 = (f32[3,4]{1,0:T(4,128)S(1)}, f32[3,4]{1,0:T(4,128)}, u32[]{:S(2)}) copy-start(f32[3,4]{1,0:T(4,128)} %param.9) | copy-start | bytes 148
  16.6 2.3 %copy-start.6 = (f32[4]{0:T(128)S(1)}, f32[4]{0:T(128)}, u32[]{:S(2)}) copy-start(f32[4]{0:T(128)} %param.8) | copy-start | bytes 52
  16.6 2.3 %copy-start.7 = (f32[4]{0:T(128)S(1)}, f32[4]{0:T(128)}, u32[]{:S(2)}) copy-start(f32[4]{0:T(128)} %param.7) | copy-start | bytes 52
  16.6 2.3 %copy-start.8 = (f32[4]{0:T(128)S(1)}, f32[4]{0:T(128)}, u32[]{:S(2)}) copy-start(f32[4]{0:T(128)} %param.6) | copy-start | bytes 52
  19.0 3.8 %collective-permute-start.8 = (f32[32,4,4]{2,1,0:T(4,128)S(1)}, f32[32,4,4]{2,1,0:T(4,128)S(1)}, u32[]{:S(2)}, u32[]{:S(2)}) collective-permute-start(f32[32,4,4]{2,1,0:T(4,128)S(1)} %slice_select_fusion.2), channel_id=1, source_target_pairs={{0,24},{8,16},{16,8},{24,0},{1,25},{9,17},{17,9},{25,1},{2,26},{10... | collective-permute-start | bytes 6152 | tf_op jit(solution)/shard_map/ppermute | solution.py:63
  20.3 31.7 %collective-permute-start.7 = (f32[32,64,4]{1,0,2:T(8,128)S(1)}, f32[32,64,4]{1,0,2:T(8,128)S(1)}, u32[]{:S(2)}, u32[]{:S(2)}) collective-permute-start(f32[32,64,4]{1,0,2:T(8,128)S(1)} %broadcast_select_fusion.12), channel_id=1, source_target_pairs={{0,8},{8,0},{1,9},{9,1},{2,10},{10,2},{3,11},{11,3},{4,12},{12,4},... | collective-permute-start | bytes 98312 | tf_op jit(solution)/shard_map/ppermute | solution.py:63
  22.8 9.3 %collective-permute-start.5 = (f32[4,64,4]{2,1,0:T(8,128)}, f32[4,64,4]{2,1,0:T(8,128)S(1)}, u32[]{:S(2)}, u32[]{:S(2)}) collective-permute-start(f32[4,64,4]{2,1,0:T(8,128)} %get-tuple-element.9), channel_id=1, source_target_pairs={{0,9},{1,10},{2,11},{3,12},{4,13},{5,14},{6,15},{8,1},{9,2},{10,3}... | collective-permute-start | bytes 12296 | tf_op jit(solution)/shard_map/ppermute | solution.py:63
  32.1 8.1 %collective-permute-start.9 = (f32[4,64,4]{2,1,0:T(8,128)S(1)}, f32[4,64,4]{2,1,0:T(8,128)S(1)}, u32[]{:S(2)}, u32[]{:S(2)}) collective-permute-start(f32[4,64,4]{2,1,0:T(8,128)S(1)} %get-tuple-element.10), channel_id=1, source_target_pairs={{1,8},{2,9},{3,10},{4,11},{5,12},{6,13},{7,14},{9,0},{10,1},{11,2}... | collective-permute-start | bytes 12296 | tf_op jit(solution)/shard_map/ppermute | solution.py:63
  40.2 19.2 %collective-permute-start = (f32[4,64,128]{2,1,0:T(8,128)}, f32[4,64,128]{2,1,0:T(8,128)S(1)}, u32[]{:S(2)}, u32[]{:S(2)}) collective-permute-start(f32[4,64,128]{2,1,0:T(8,128)} %get-tuple-element.16), channel_id=1, source_target_pairs={{0,1},{1,2},{2,3},{3,4},{4,5},{5,6},{6,7},{8,9},{9,10},{10,11},{11... | collective-permute-start | bytes 393224 | tf_op jit(solution)/shard_map/ppermute | solution.py:63
  48.1 11.3 %collective-permute-start.1 = (f32[4,64,128]{2,1,0:T(8,128)}, f32[4,64,128]{2,1,0:T(8,128)S(1)}, u32[]{:S(2)}, u32[]{:S(2)}) collective-permute-start(f32[4,64,128]{2,1,0:T(8,128)} %get-tuple-element.15), channel_id=1, source_target_pairs={{1,0},{2,1},{3,2},{4,3},{5,4},{6,5},{7,6},{9,8},{10,9},{11,10},{12... | collective-permute-start | bytes 393224 | tf_op jit(solution)/shard_map/ppermute | solution.py:63
  54.3 5.0 %copy-start.1 = (f32[4,4,128]{2,1,0:T(4,128)S(1)}, f32[4,4,128]{2,1,0:T(4,128)}, u32[]{:S(2)}) copy-start(f32[4,4,128]{2,1,0:T(4,128)} %get-tuple-element.43) | copy-start | bytes 24580
  54.3 5.0 %copy-start.2 = (f32[4,4,128]{2,1,0:T(4,128)S(1)}, f32[4,4,128]{2,1,0:T(4,128)}, u32[]{:S(2)}) copy-start(f32[4,4,128]{2,1,0:T(4,128)} %get-tuple-element.44) | copy-start | bytes 24580
  54.3 5.0 %copy-start.3 = (f32[4,4,128]{2,1,0:T(4,128)S(1)}, f32[4,4,128]{2,1,0:T(4,128)}, u32[]{:S(2)}) copy-start(f32[4,4,128]{2,1,0:T(4,128)} %get-tuple-element.45) | copy-start | bytes 24580
  54.3 5.0 %copy-start.4 = (f32[4,4,128]{2,1,0:T(4,128)S(1)}, f32[4,4,128]{2,1,0:T(4,128)}, u32[]{:S(2)}) copy-start(f32[4,4,128]{2,1,0:T(4,128)} %get-tuple-element.46) | copy-start | bytes 24580

commit v5 on v3

--- a/solution.py
+++ b/solution.py
@@ -16,6 +16,7 @@
 RATE_DEPTH = 0.3
 RATE_PLANE = 0.09
 LANES = 256
+CHUNK = 8
 
 
 def pick(cond, a, b):
@@ -36,7 +37,9 @@
     return [(up, True, True), (down, False, False)]
 
 
-def halo_stage(x, dim_axes, width):
+def halo_stage(x_parts, dim_axes, width):
+    x_parts = x_parts if isinstance(x_parts, tuple) else (x_parts,)
+    x = x_parts[0] if len(x_parts) == 1 else jnp.concatenate(x_parts, axis=0)
     dims = [d for d, _ in dim_axes]
     axes = [a for _, a in dim_axes]
     sizes = [lax.axis_size(a) for a in axes]
@@ -45,13 +48,16 @@
     for combo in itertools.product(*options):
         if all(m is None for m in combo):
             continue
-        piece = x
-        for d, m in zip(dims, combo):
-            if m is not None:
-                n_d = piece.shape[d]
-                lo = lax.slice_in_dim(piece, 0, width, axis=d)
-                hi = lax.slice_in_dim(piece, n_d - width, n_d, axis=d)
-                piece = pick(m[1], hi, lo)
+        cut = []
+        for part in x_parts:
+            for d, m in zip(dims, combo):
+                if m is not None:
+                    n_d = part.shape[d]
+                    lo = lax.slice_in_dim(part, 0, width, axis=d)
+                    hi = lax.slice_in_dim(part, n_d - width, n_d, axis=d)
+                    part = pick(m[1], hi, lo)
+            cut.append(part)
+        piece = cut[0] if len(cut) == 1 else jnp.concatenate(cut, axis=0)
         used = [(a, s, m) for a, s, m in zip(axes, sizes, combo) if m is not None]
         pairs = []
         for parts in itertools.product(*[m[0] for _, _, m in used]):
@@ -105,15 +111,30 @@
     depth, rows, lanes = a_ref.shape
     d_in, r_in, l_in = interior
     halo = STEPS
-    copies = [
-        pltpu.make_async_copy(x_hbm, b_ref.at[halo:halo + d_in, 0:r_in, 0:l_in], sem.at[0]),
-        pltpu.make_async_copy(zlo_hbm, b_ref.at[0:halo, 0:r_in, 0:l_in], sem.at[1]),
-        pltpu.make_async_copy(zhi_hbm, b_ref.at[halo + d_in:depth, 0:r_in, 0:l_in], sem.at[2]),
-        pltpu.make_async_copy(rband_hbm, b_ref.at[:, r_in:rows, 0:l_in], sem.at[3]),
-        pltpu.make_async_copy(cband_hbm, b_ref.at[:, :, l_in:lanes], sem.at[4]),
-    ]
-    for cp in copies:
-        cp.start()
+    chunk = CHUNK
+    n_chunks = -(-depth // chunk)
+    chunk_copies = []
+    for k in range(n_chunks):
+        lo, hi = k * chunk, min(depth, (k + 1) * chunk)
+        jobs = [
+            (rband_hbm.at[lo:hi], b_ref.at[lo:hi, r_in:rows, 0:l_in]),
+            (cband_hbm.at[lo:hi], b_ref.at[lo:hi, :, l_in:lanes]),
+        ]
+        spans = ((0, halo, zlo_hbm, 0), (halo, halo + d_in, x_hbm, halo), (halo + d_in, depth, zhi_hbm, halo + d_in))
+        for s_lo, s_hi, ref, base in spans:
+            a, b = max(lo, s_lo), min(hi, s_hi)
+            if a < b:
+                jobs.append((ref.at[a - base:b - base], b_ref.at[a:b, 0:r_in, 0:l_in]))
+        chunk_copies.append(jobs)
+    sem_at = 0
+    for k, jobs in enumerate(chunk_copies):
+        made = []
+        for src_ref, dst_ref in jobs:
+            made.append(pltpu.make_async_copy(src_ref, dst_ref, sem.at[sem_at]))
+            sem_at += 1
+        chunk_copies[k] = made
+        for cp in made:
+            cp.start()
 
     row = lax.broadcasted_iota(jnp.int32, (rows, lanes), 0)
     lane = lax.broadcasted_iota(jnp.int32, (rows, lanes), 1)
@@ -129,11 +150,11 @@
     for ch in range(CHANNELS + 1):
         out_ref[ch] = jnp.zeros((r_in, l_in), jnp.float32)
 
-    for cp in copies:
-        cp.wait()
-
-    def smooth(src, dst, s):
+    def smooth(src, dst, s, arrived=None):
         z0, z1 = s + 1, depth - 1 - s
+        if arrived is not None:
+            arrived(0)
+            arrived(1)
         g0 = flux(src[z0] - src[z0 - 1], RATE_DEPTH)
 
         def body(z, g_prev):
@@ -147,9 +168,22 @@
             dst[z] = new * (m_ref[...] * zf)
             return g
 
-        lax.fori_loop(z0, z1, body, g0)
-
-    smooth(b_ref, a_ref, 0)
+        if arrived is None:
+            lax.fori_loop(z0, z1, body, g0)
+            return
+        g = g0
+        for k in range(n_chunks):
+            lo, hi = max(z0, k * chunk), min(z1, (k + 1) * chunk)
+            if 1 <= k and k + 1 < n_chunks:
+                arrived(k + 1)
+            if lo < hi:
+                g = lax.fori_loop(lo, hi, body, g)
+
+    def arrived(k):
+        for cp in chunk_copies[k]:
+            cp.wait()
+
+    smooth(b_ref, a_ref, 0, arrived)
     smooth(a_ref, b_ref, 1)
     smooth(b_ref, a_ref, 2)
 
@@ -184,6 +218,10 @@
     depth, rows, lanes = d_in + 2 * STEPS, r_in + 2 * STEPS, LANES
     cells = depth * rows * lanes
     kernel = functools.partial(render_kernel, interior=interior, h=h)
+    n_dma = 0
+    for k in range(-(-depth // CHUNK)):
+        lo, hi = k * CHUNK, min(depth, (k + 1) * CHUNK)
+        n_dma += 2 + sum(1 for s_lo, s_hi in ((0, STEPS), (STEPS, STEPS + d_in), (STEPS + d_in, depth)) if max(lo, s_lo) < min(hi, s_hi))
     return pl.pallas_call(
         kernel,
         out_shape=jax.ShapeDtypeStruct((CHANNELS + 1, r_in, l_in), jnp.float32),
@@ -193,7 +231,7 @@
             pltpu.VMEM((depth, rows, lanes), jnp.float32),
             pltpu.VMEM((depth, rows, lanes), jnp.float32),
             pltpu.VMEM((rows, lanes), jnp.float32),
-            pltpu.SemaphoreType.DMA((5,)),
+            pltpu.SemaphoreType.DMA((n_dma,)),
         ],
         compiler_params=pltpu.CompilerParams(vmem_limit_bytes=48 * 1024 * 1024),
         cost_estimate=pl.CostEstimate(
@@ -210,8 +248,7 @@
     h = 1.0 / (depth_cells * groups)
     zblock = halo_stage(phase_field, ((0, "gz"),), STEPS)
     zlo, zhi = zblock("lo"), zblock("hi")
-    deep = jnp.concatenate([zlo, phase_field, zhi], axis=0)
-    plane = halo_stage(deep, ((1, "gx"), (2, "gy")), STEPS)
+    plane = halo_stage((zlo, phase_field, zhi), ((1, "gx"), (2, "gy")), STEPS)
     rband = jnp.concatenate([plane("hi", "mid"), plane("lo", "mid")], axis=1)
     right = jnp.concatenate([plane("mid", "hi"), plane("hi", "hi"), plane("lo", "hi")], axis=1)
     left = jnp.concatenate([plane("mid", "lo"), plane("hi", "lo"), plane("lo", "lo")], axis=1)

time: 65 us -> 66.5 us (1.023)
  other arithmetic: 2.21 us -> 3.24 us
  waiting for transfers between devices: 6.35 us -> 5.34 us
  local copies, waits for them, and re-layouts: 6.2 us -> 7.01 us
    slice x4 -> x2, local copies, waits for them, and re-layouts: 2.38 us -> 3.74 us  [halo_stage(): lo = lax.slice_in_dim(part, 0, width, axis=d)]
    concatenate x1, other arithmetic: 0.5 us -> 1.81 us  [shards(): cband = jnp.concatenate([right, fill, left], axis=2)]
    unnamed x4 -> x12, local copies, waits for them, and re-layouts: 1.93 us -> 0.8 us
    select_n x2, local copies, waits for them, and re-layouts: 0.94 us -> 2.03 us  [halo_stage(): val = got if cond is True else jnp.where(cond, got, 0.0)]
    ppermute x5, waiting for transfers between devices: 6.35 us -> 5.34 us  [halo_stage(): got = lax.ppermute(piece, tuple((a for a, _, _ in used)), pairs)]
    concatenate x1, other arithmetic: 0.77 us -> 0.08 us  [shards(): jnp.concatenate([centres, widths, densities, colours.reshape(-1)])]
    reshape x1, local copies, waits for them, and re-layouts: 0.76 us -> 0.08 us  [shards(): colours.reshape(-1)]
  transfers between devices with their start and end apart: 5 -> 5, of which waited for: 3 -> 3; matrix products, arithmetic and copies ran while one was open for 9% -> 12% of each run, Pallas kernels for 0% -> 0%
where the time goes in v5:
time: 66.5 us; the launch traced here: 66.3 us
  Pallas kernels  28.4 us (43%)
  blocking collectives  13.1 us (20%)
  starting transfers between devices  8.81 us (13%)
  local copies, waits for them, and re-layouts  7.01 us (11%)
  waiting for transfers between devices  5.34 us (8%)
  other arithmetic  3.24 us (5%)
    pallas_call x1, Pallas kernels, render_block(): pl.pallas_call(kernel, out_shape=jax.ShapeDtypeStruct((CHANNELS + 1, r_in...  28.4 us
    all_to_all x1, blocking collectives, shards(): got = lax.all_to_all(parts, 'gz', 1, 1, tiled=True)  13.1 us
    ppermute x5, starting transfers between devices, halo_stage(): got = lax.ppermute(piece, tuple((a for a, _, _ in used)), pairs)  8.81 us
    ppermute x5, waiting for transfers between devices, halo_stage(): got = lax.ppermute(piece, tuple((a for a, _, _ in used)), pairs)  5.34 us
    slice x2, local copies, waits for them, and re-layouts, halo_stage(): lo = lax.slice_in_dim(part, 0, width, axis=d)  3.74 us
    select_n x2, local copies, waits for them, and re-layouts, halo_stage(): val = got if cond is True else jnp.where(cond, got, 0.0)  2.03 us
    concatenate x1, other arithmetic, shards(): cband = jnp.concatenate([right, fill, left], axis=2)  1.81 us
  transfers between devices with their start and end apart: 5, of which 3 were waited for; matrix products, arithmetic and copies ran while one was open for 12% of the time, Pallas kernels for 0%

profile of v5, /device:TPU:0, one launch (start us, length us, event | category | flops | bytes accessed | tf_op | source)
XLA Modules:
  0.0 66.3 jit_solution(10509370265340024275)
XLA Ops:
  0.0 1.7 %fusion.19 = (f32[4,64,128]{2,1,0:T(8,128)}, f32[4,64,128]{2,1,0:T(8,128)}) fusion(f32[32,64,128]{2,1,0:T(8,128)} %x_hbm.1), kind=kLoop, calls=%fused_computation.65 | loop fusion | bytes 524288 | tf_op jit(solution)/shard_map/slice | solution.py:56
  1.7 1.3 %collective-permute-start.1 = (f32[4,64,128]{2,1,0:T(8,128)}, f32[4,64,128]{2,1,0:T(8,128)S(1)}, u32[]{:S(2)}, u32[]{:S(2)}) collective-permute-start(f32[4,64,128]{2,1,0:T(8,128)} %get-tuple-element.11), channel_id=1, source_target_pairs={{1,0},{2,1},{3,2},{4,3},{5,4},{6,5},{7,6},{9,8},{10,9},{11,10},{12... | collective-permute-start | bytes 393224 | tf_op jit(solution)/shard_map/ppermute | solution.py:68
  3.0 5.5 %collective-permute-start = (f32[4,64,128]{2,1,0:T(8,128)}, f32[4,64,128]{2,1,0:T(8,128)S(1)}, u32[]{:S(2)}, u32[]{:S(2)}) collective-permute-start(f32[4,64,128]{2,1,0:T(8,128)} %get-tuple-element.12), channel_id=1, source_target_pairs={{0,1},{1,2},{2,3},{3,4},{4,5},{5,6},{6,7},{8,9},{9,10},{10,11},{11... | collective-permute-start | bytes 393224 | tf_op jit(solution)/shard_map/ppermute | solution.py:68
  8.5 0.0 copy-start
  8.5 2.1 %fusion.18 = (f32[32,64,4]{2,1,0:T(8,128)S(1)}, f32[32,64,4]{2,1,0:T(8,128)S(1)}) fusion(f32[32,64,128]{2,1,0:T(8,128)} %x_hbm.1), kind=kLoop, calls=%fused_computation.64 | loop fusion | bytes 131072 | tf_op jit(solution)/shard_map/slice | solution.py:56
  10.6 0.0 copy-start.2
  10.7 0.4 copy.60
  11.1 0.4 copy.61
  11.5 0.1 slice_select_fusion.2
  11.6 0.1 reshape.210
  11.7 0.1 pad.5.clone
  11.8 0.1 stack.27.lim_ref
  11.9 0.1 pad_maximum_fusion.5.prm_ref
  12.0 0.1 slice_select_fusion.4
  12.1 1.3 %collective-permute-done.zlo_hbm = f32[4,64,128]{2,1,0:T(8,128)S(1)} collective-permute-done((f32[4,64,128]{2,1,0:T(8,128)}, f32[4,64,128]{2,1,0:T(8,128)S(1)}, u32[]{:S(2)}, u32[]{:S(2)}) %collective-permute-start) | collective-permute-done | bytes 131104 | tf_op jit(solution)/shard_map/ppermute | solution.py:68
  13.3 0.1 slice_select_fusion.5
  13.5 1.2 %collective-permute-start.4 = (f32[40,4,4]{2,1,0:T(4,128)S(1)}, f32[40,4,4]{2,1,0:T(4,128)S(1)}, u32[]{:S(2)}, u32[]{:S(2)}) collective-permute-start(f32[40,4,4]{2,1,0:T(4,128)S(1)} %pad_maximum_fusion.3), channel_id=1, source_target_pairs={{0,24},{8,16},{16,8},{24,0},{1,25},{9,17},{17,9},{25,1},{2,26},{10... | collective-permute-start | bytes 7688 | tf_op jit(solution)/shard_map/ppermute | solution.py:68
  14.7 0.1 slice_select_fusion.1
  14.8 0.1 copy.55
  14.8 0.1 slice_select_fusion
  15.0 0.1 copy.56
  15.1 0.6 collective-permute-start.3
  15.7 0.2 collective-permute-start.2
  15.9 2.2 %collective-permute-done.4 = f32[40,4,4]{2,1,0:T(4,128)S(1)} collective-permute-done((f32[40,4,4]{2,1,0:T(4,128)S(1)}, f32[40,4,4]{2,1,0:T(4,128)S(1)}, u32[]{:S(2)}, u32[]{:S(2)}) %collective-permute-start.4) | collective-permute-done | bytes 2592 | tf_op jit(solution)/shard_map/ppermute | solution.py:68
  18.1 0.1 broadcast_select_fusion.3
  18.1 1.9 %collective-permute-done.3 = f32[40,64,4]{1,0,2:T(8,128)S(1)} collective-permute-done((f32[40,64,4]{1,0,2:T(8,128)S(1)}, f32[40,64,4]{1,0,2:T(8,128)S(1)}, u32[]{:S(2)}, u32[]{:S(2)}) %collective-permute-start.3) | collective-permute-done | bytes 40992 | tf_op jit(solution)/shard_map/ppermute | solution.py:68
  20.1 0.5 copy.57
  20.5 1.6 %copy.58 = f32[40,64,4]{2,1,0:T(8,128)} copy(f32[40,64,4]{1,0,2:T(8,128)S(1)} %get-tuple-element.20) | data formatting | bytes 81920 | tf_op jit(solution)/shard_map/jit(_where)/select_n | solution.py:88
  22.1 1.8 %maximum_maximum_fusion.cband_hbm = f32[40,72,128]{2,1,0:T(8,128)S(1)} fusion(f32[40,4,4]{2,1,0:T(4,128)S(1)} %get-tuple-element.22, f32[40,4,4]{2,1,0:T(4,128)S(1)} %get-tuple-element.23, f32[40,64,4]{2,1,0:T(8,128)} %copy.58, f32[40,4,4]{2,1,0:T(4,128)S(1)} %get-tuple-element.24, f32[40,4,4]{2,1,0:T(4,128)S(1)} %get-tuple-element.21, ...), kind=kLoop, calls=%fused_computation | loop fusion | flops 2211840 | bytes 1567232 | tf_op jit(solution)/shard_map/concatenate | solution.py:256
  24.0 28.4 %shard_map.55 = f32[4,64,128]{2,1,0:T(8,128)S(1)} custom-call(s32[6]{0:T(128)S(1)} %stack.27.lim_ref, f32[24]{0:T(128)S(1)} %pad_maximum_fusion.5.prm_ref, f32[32,64,128]{2,1,0:T(8,128)S(1)} %copy-done, f32[4,64,128]{2,1,0:T(8,128)S(1)} %collective-permute-done.zlo_hbm, f32[4,64,128]{2,1,0:T(8,128)S(1)} %collective-permute-done.1.zhi_hbm, ...), custom_call_target="tpu_custom_call" | custom-call | flops 133693440 | bytes 3080192 | tf_op jit(solution)/shard_map/pallas_call | solution.py:225
  52.5 13.1 %all_to_all.5 = f32[4,8,8,128]{3,2,0,1:T(8,128)S(1)} all-to-all(f32[4,8,8,128]{3,2,0,1:T(8,128)S(1)} %copy.59), channel_id=1, replica_groups=mesh['gx'=2,'gy'=2,'gz'=8] {'gz'}, dimensions={1} | all-to-all | bytes 262144 | tf_op jit(solution)/shard_map/all_to_all | solution.py:277
  65.7 0.6 pad_maximum_fusion.4
  (26 shorter events, 0.3 us)
Async XLA Ops:
  1.7 10.3 %collective-permute-start.1 = (f32[4,64,128]{2,1,0:T(8,128)}, f32[4,64,128]{2,1,0:T(8,128)S(1)}, u32[]{:S(2)}, u32[]{:S(2)}) collective-permute-start(f32[4,64,128]{2,1,0:T(8,128)} %get-tuple-element.11), channel_id=1, source_target_pairs={{1,0},{2,1},{3,2},{4,3},{5,4},{6,5},{7,6},{9,8},{10,9},{11,10},{12... | collective-permute-start | bytes 393224 | tf_op jit(solution)/shard_map/ppermute | solution.py:68
  3.0 10.4 %collective-permute-start = (f32[4,64,128]{2,1,0:T(8,128)}, f32[4,64,128]{2,1,0:T(8,128)S(1)}, u32[]{:S(2)}, u32[]{:S(2)}) collective-permute-start(f32[4,64,128]{2,1,0:T(8,128)} %get-tuple-element.12), channel_id=1, source_target_pairs={{0,1},{1,2},{2,3},{3,4},{4,5},{5,6},{6,7},{8,9},{9,10},{10,11},{11... | collective-permute-start | bytes 393224 | tf_op jit(solution)/shard_map/ppermute | solution.py:68
  8.5 2.2 %copy-start = (f32[32,64,128]{2,1,0:T(8,128)S(1)}, f32[32,64,128]{2,1,0:T(8,128)}, u32[]{:S(2)}) copy-start(f32[32,64,128]{2,1,0:T(8,128)} %x_hbm.1) | copy-start | bytes 3145732
  10.6 1.0 %copy-start.1 = (f32[3,4]{1,0:T(4,128)S(1)}, f32[3,4]{1,0:T(4,128)}, u32[]{:S(2)}) copy-start(f32[3,4]{1,0:T(4,128)} %param.9) | copy-start | bytes 148
  10.6 1.3 %copy-start.2 = (f32[4]{0:T(128)S(1)}, f32[4]{0:T(128)}, u32[]{:S(2)}) copy-start(f32[4]{0:T(128)} %param.8) | copy-start | bytes 52
  10.6 1.3 %copy-start.3 = (f32[4]{0:T(128)S(1)}, f32[4]{0:T(128)}, u32[]{:S(2)}) copy-start(f32[4]{0:T(128)} %param.7) | copy-start | bytes 52
  10.6 1.3 %copy-start.4 = (f32[4]{0:T(128)S(1)}, f32[4]{0:T(128)}, u32[]{:S(2)}) copy-start(f32[4]{0:T(128)} %param.6) | copy-start | bytes 52
  13.5 4.6 %collective-permute-start.4 = (f32[40,4,4]{2,1,0:T(4,128)S(1)}, f32[40,4,4]{2,1,0:T(4,128)S(1)}, u32[]{:S(2)}, u32[]{:S(2)}) collective-permute-start(f32[40,4,4]{2,1,0:T(4,128)S(1)} %pad_maximum_fusion.3), channel_id=1, source_target_pairs={{0,24},{8,16},{16,8},{24,0},{1,25},{9,17},{17,9},{25,1},{2,26},{10... | collective-permute-start | bytes 7688 | tf_op jit(solution)/shard_map/ppermute | solution.py:68
  15.1 4.9 %collective-permute-start.3 = (f32[40,64,4]{1,0,2:T(8,128)S(1)}, f32[40,64,4]{1,0,2:T(8,128)S(1)}, u32[]{:S(2)}, u32[]{:S(2)}) collective-permute-start(f32[40,64,4]{1,0,2:T(8,128)S(1)} %pad_maximum_fusion.2), channel_id=1, source_target_pairs={{0,8},{8,0},{1,9},{9,1},{2,10},{10,2},{3,11},{11,3},{4,12},{12,4},... | collective-permute-start | bytes 122888 | tf_op jit(solution)/shard_map/ppermute | solution.py:68
  15.7 8.2 %collective-permute-start.2 = (f32[40,4,128]{2,1,0:T(4,128)S(1)}, f32[40,4,128]{2,1,0:T(4,128)S(1)}, u32[]{:S(2)}, u32[]{:S(2)}) collective-permute-start(f32[40,4,128]{2,1,0:T(4,128)S(1)} %pad_maximum_fusion.1), channel_id=1, source_target_pairs={{0,16},{16,0},{1,17},{17,1},{2,18},{18,2},{3,19},{19,3},{4,20},{20... | collective-permute-start | bytes 245768 | tf_op jit(solution)/shard_map/ppermute | solution.py:68

commit v6 on v3

--- a/solution.py
+++ b/solution.py
@@ -95,12 +95,12 @@
     return block
 
 
-def flux(d, rate):
+def flux(d):
     q = d * (1.0 / KAPPA)
-    return rate * d / (1.0 + q * q)
-
-
-def render_kernel(lim_ref, prm_ref, x_hbm, zlo_hbm, zhi_hbm, rband_hbm, cband_hbm, out_ref, a_ref, b_ref, m_ref, sem,
+    return d / (1.0 + q * q)
+
+
+def render_kernel(lim_ref, prm_ref, x_hbm, zlo_hbm, zhi_hbm, rband_hbm, cband_hbm, out_ref, a_ref, b_ref, m_ref, acc_ref, sem,
                   *, interior, h):
     depth, rows, lanes = a_ref.shape
     d_in, r_in, l_in = interior
@@ -120,31 +120,33 @@
     row_at = jnp.where(row < r_in + halo, row, row - rows)
     lane_at = jnp.where(lane < (l_in + lanes) // 2, lane, lane - lanes)
     ok = (row_at >= lim_ref[2]) & (row_at < lim_ref[3]) & (lane_at >= lim_ref[4]) & (lane_at < lim_ref[5])
-    m_ref[...] = jnp.where(ok, 1.0, 0.0).astype(jnp.float32)
+    m_ref[0] = jnp.zeros((rows, lanes), jnp.float32)
+    m_ref[1] = jnp.where(ok, 1.0, 0.0).astype(jnp.float32)
 
     cen = [prm_ref[k] for k in range(MATERIALS)]
     wid = [prm_ref[MATERIALS + k] for k in range(MATERIALS)]
     den = [prm_ref[2 * MATERIALS + k] for k in range(MATERIALS)]
     col = [[prm_ref[3 * MATERIALS + ch * MATERIALS + k] for k in range(MATERIALS)] for ch in range(CHANNELS)]
-    for ch in range(CHANNELS + 1):
-        out_ref[ch] = jnp.zeros((r_in, l_in), jnp.float32)
+    out_ref[CHANNELS] = jnp.zeros((r_in, l_in), jnp.float32)
+    for k in range(MATERIALS):
+        acc_ref[k] = jnp.zeros((r_in, l_in), jnp.float32)
 
     for cp in copies:
         cp.wait()
 
     def smooth(src, dst, s):
         z0, z1 = s + 1, depth - 1 - s
-        g0 = flux(src[z0] - src[z0 - 1], RATE_DEPTH)
+        g0 = flux(src[z0] - src[z0 - 1])
 
         def body(z, g_prev):
             c = src[z]
-            g = flux(src[z + 1] - c, RATE_DEPTH)
-            fr = flux(pltpu.roll(c, rows - 1, 0) - c, RATE_PLANE)
-            fc = flux(pltpu.roll(c, lanes - 1, 1) - c, RATE_PLANE)
-            new = c + (g - g_prev) + (fr - pltpu.roll(fr, 1, 0)) + (fc - pltpu.roll(fc, 1, 1))
-            inside = (z >= lim_ref[0]) & (z < lim_ref[1])
-            zf = jnp.where(inside, 1.0, 0.0).astype(jnp.float32)
-            dst[z] = new * (m_ref[...] * zf)
+            g = flux(src[z + 1] - c)
+            fr = flux(pltpu.roll(c, rows - 1, 0) - c)
+            fc = flux(pltpu.roll(c, lanes - 1, 1) - c)
+            plane = (fr - pltpu.roll(fr, 1, 0)) + (fc - pltpu.roll(fc, 1, 1))
+            new = c + RATE_DEPTH * (g - g_prev) + RATE_PLANE * plane
+            inside = ((z >= lim_ref[0]) & (z < lim_ref[1])).astype(jnp.int32)
+            dst[z] = new * m_ref[inside]
             return g
 
         lax.fori_loop(z0, z1, body, g0)
@@ -154,29 +156,30 @@
     smooth(b_ref, a_ref, 2)
 
     z0, z1 = halo, halo + d_in
-    g0 = flux(a_ref[z0, 0:r_in, 0:l_in] - a_ref[z0 - 1, 0:r_in, 0:l_in], RATE_DEPTH)
+    g0 = flux(a_ref[z0, 0:r_in, 0:l_in] - a_ref[z0 - 1, 0:r_in, 0:l_in])
 
     def final(z, g_prev):
         ci = a_ref[z, 0:r_in, 0:l_in]
-        g = flux(a_ref[z + 1, 0:r_in, 0:l_in] - ci, RATE_DEPTH)
+        g = flux(a_ref[z + 1, 0:r_in, 0:l_in] - ci)
         c0 = a_ref[z, :, 0:l_in]
-        fr = flux(pltpu.roll(c0, rows - 1, 0) - c0, RATE_PLANE)
+        fr = flux(pltpu.roll(c0, rows - 1, 0) - c0)
         cr = a_ref[z, 0:r_in, :]
-        fc = flux(pltpu.roll(cr, lanes - 1, 1) - cr, RATE_PLANE)
-        v = ci + (g - g_prev) + (fr - pltpu.roll(fr, 1, 0))[0:r_in] + (fc - pltpu.roll(fc, 1, 1))[:, 0:l_in]
+        fc = flux(pltpu.roll(cr, lanes - 1, 1) - cr)
+        plane = (fr - pltpu.roll(fr, 1, 0))[0:r_in] + (fc - pltpu.roll(fc, 1, 1))[:, 0:l_in]
+        v = ci + RATE_DEPTH * (g - g_prev) + RATE_PLANE * plane
         bumps = [den[k] * jnp.exp(-(((v - cen[k]) / wid[k]) ** 2)) for k in range(MATERIALS)]
         ext = bumps[0] + bumps[1] + bumps[2] + bumps[3]
         run = out_ref[CHANNELS]
         through = jnp.exp(-h * run)
-        for ch in range(CHANNELS):
-            emit = col[ch][0] * bumps[0] + col[ch][1] * bumps[1] + col[ch][2] * bumps[2] + col[ch][3] * bumps[3]
-            out_ref[ch] = out_ref[ch] + through * emit
+        for k in range(MATERIALS):
+            acc_ref[k] = acc_ref[k] + through * bumps[k]
         out_ref[CHANNELS] = run + ext
         return g
 
     lax.fori_loop(z0, z1, final, g0)
     for ch in range(CHANNELS):
-        out_ref[ch] = h * out_ref[ch]
+        emit = col[ch][0] * acc_ref[0] + col[ch][1] * acc_ref[1] + col[ch][2] * acc_ref[2] + col[ch][3] * acc_ref[3]
+        out_ref[ch] = h * emit
 
 
 def render_block(pieces, lim, prm, interior, h):
@@ -192,7 +195,8 @@
         scratch_shapes=[
             pltpu.VMEM((depth, rows, lanes), jnp.float32),
             pltpu.VMEM((depth, rows, lanes), jnp.float32),
-            pltpu.VMEM((rows, lanes), jnp.float32),
+            pltpu.VMEM((2, rows, lanes), jnp.float32),
+            pltpu.VMEM((MATERIALS, r_in, l_in), jnp.float32),
             pltpu.SemaphoreType.DMA((5,)),
         ],
         compiler_params=pltpu.CompilerParams(vmem_limit_bytes=48 * 1024 * 1024),

time: 65 us -> 65.6 us (level)
  no operation moved by 1% of the time
where the time goes in v6:
time: 65.6 us; the launch traced here: 65.3 us
  Pallas kernels  28.9 us (44%)
  blocking collectives  12.9 us (20%)
  starting transfers between devices  8.53 us (13%)
  waiting for transfers between devices  6.35 us (10%)
  local copies, waits for them, and re-layouts  6.2 us (9%)
  other arithmetic  2.21 us (3%)
    pallas_call x1, Pallas kernels, render_block(): pl.pallas_call(kernel, out_shape=jax.ShapeDtypeStruct((CHANNELS + 1, r_in...  28.9 us
    all_to_all x1, blocking collectives, shards(): got = lax.all_to_all(parts, 'gz', 1, 1, tiled=True)  12.9 us
    ppermute x5, starting transfers between devices, halo_stage(): got = lax.ppermute(piece, tuple((a for a, _, _ in used)), pairs)  8.53 us
    ppermute x5, waiting for transfers between devices, halo_stage(): got = lax.ppermute(piece, tuple((a for a, _, _ in used)), pairs)  6.35 us
    unnamed x4, local copies, waits for them, and re-layouts  1.93 us
    slice x3, local copies, waits for them, and re-layouts, halo_stage(): lo = lax.slice_in_dim(piece, 0, width, axis=d)  1.92 us
  transfers between devices with their start and end apart: 5, of which 3 were waited for; matrix products, arithmetic and copies ran while one was open for 9% of the time, Pallas kernels for 0%

profile of v6, /device:TPU:0, one launch (start us, length us, event | category | flops | bytes accessed | tf_op | source)
XLA Modules:
  0.0 65.3 jit_solution(10231980104576453286)
XLA Ops:
  0.0 1.0 %fusion.19 = (f32[4,64,128]{2,1,0:T(8,128)S(1)}, f32[4,64,128]{2,1,0:T(8,128)S(1)}) fusion(f32[32,64,128]{2,1,0:T(8,128)} %x_hbm.1), kind=kLoop, calls=%fused_computation.59 | loop fusion | bytes 524288 | tf_op jit(solution)/shard_map/slice | solution.py:52
  1.0 4.9 %collective-permute-start = (f32[4,64,128]{2,1,0:T(8,128)S(1)}, f32[4,64,128]{2,1,0:T(8,128)S(1)}, u32[]{:S(2)}, u32[]{:S(2)}) collective-permute-start(f32[4,64,128]{2,1,0:T(8,128)S(1)} %get-tuple-element.12), channel_id=1, source_target_pairs={{0,1},{1,2},{2,3},{3,4},{4,5},{5,6},{6,7},{8,9},{9,10},{10,11},{11... | collective-permute-start | bytes 393224 | tf_op jit(solution)/shard_map/ppermute | solution.py:62
  5.9 1.3 %collective-permute-start.1 = (f32[4,64,128]{2,1,0:T(8,128)S(1)}, f32[4,64,128]{2,1,0:T(8,128)S(1)}, u32[]{:S(2)}, u32[]{:S(2)}) collective-permute-start(f32[4,64,128]{2,1,0:T(8,128)S(1)} %get-tuple-element.11), channel_id=1, source_target_pairs={{1,0},{2,1},{3,2},{4,3},{5,4},{6,5},{7,6},{9,8},{10,9},{11,10},{12... | collective-permute-start | bytes 393224 | tf_op jit(solution)/shard_map/ppermute | solution.py:62
  7.3 0.8 %reshape.210 = f32[12]{0:T(128)S(1)} reshape(f32[3,4]{1,0:T(4,128)} %param.9) | data formatting | bytes 96 | tf_op jit(solution)/shard_map/reshape | solution.py:238
  8.0 0.1 pad.5.clone
  8.1 0.1 stack.27.lim_ref
  8.2 0.8 %pad_maximum_fusion.2.prm_ref = f32[24]{0:T(128)S(1)} fusion(f32[12]{0:T(128)S(1)} %reshape.210, f32[4]{0:T(128)} %param.8, f32[4]{0:T(128)} %param.7, f32[4]{0:T(128)} %param.6), kind=kLoop, calls=%fused_computation.57 | loop fusion | flops 72 | bytes 192 | tf_op jit(solution)/shard_map/concatenate | solution.py:238
  8.9 0.0 collective-permute-done.zlo_hbm
  9.0 1.3 %constant_dynamic-update-slice_fusion.1 = f32[40,64,128]{2,1,0:T(8,128)S(1)} fusion(f32[40,64,128]{2,1,0:T(8,128)S(1)} %constant_dynamic-update-slice_fusion.2, f32[32,64,128]{2,1,0:T(8,128)} %x_hbm.1), kind=kLoop, calls=%fused_computation.37 | loop fusion | bytes 2097152
  10.3 2.5 %collective-permute-done.1.zhi_hbm = f32[4,64,128]{2,1,0:T(8,128)S(1)} collective-permute-done((f32[4,64,128]{2,1,0:T(8,128)S(1)}, f32[4,64,128]{2,1,0:T(8,128)S(1)}, u32[]{:S(2)}, u32[]{:S(2)}) %collective-permute-start.1) | collective-permute-done | bytes 131104 | tf_op jit(solution)/shard_map/ppermute | solution.py:62
  12.8 0.5 fusion.18
  13.3 0.1 collective-permute-start.2
  13.4 0.1 slice_select_fusion
  13.5 1.7 %collective-permute-start.4 = (f32[40,4,4]{2,1,0:T(4,128)S(1)}, f32[40,4,4]{2,1,0:T(4,128)S(1)}, u32[]{:S(2)}, u32[]{:S(2)}) collective-permute-start(f32[40,4,4]{2,1,0:T(4,128)S(1)} %slice_select_fusion), channel_id=1, source_target_pairs={{0,24},{8,16},{16,8},{24,0},{1,25},{9,17},{17,9},{25,1},{2,26},{10... | collective-permute-start | bytes 7688 | tf_op jit(solution)/shard_map/ppermute | solution.py:62
  15.1 0.5 copy.33
  15.6 0.5 copy.34
  16.1 0.6 collective-permute-start.3
  16.7 1.1 %collective-permute-done.4 = f32[40,4,4]{2,1,0:T(4,128)S(1)} collective-permute-done((f32[40,4,4]{2,1,0:T(4,128)S(1)}, f32[40,4,4]{2,1,0:T(4,128)S(1)}, u32[]{:S(2)}, u32[]{:S(2)}) %collective-permute-start.4) | collective-permute-done | bytes 2592 | tf_op jit(solution)/shard_map/ppermute | solution.py:62
  17.8 0.1 broadcast_select_fusion.3
  17.8 2.8 %collective-permute-done.3 = f32[40,64,4]{1,0,2:T(8,128)S(1)} collective-permute-done((f32[40,64,4]{1,0,2:T(8,128)S(1)}, f32[40,64,4]{1,0,2:T(8,128)S(1)}, u32[]{:S(2)}, u32[]{:S(2)}) %collective-permute-start.3) | collective-permute-done | bytes 40992 | tf_op jit(solution)/shard_map/ppermute | solution.py:62
  20.6 0.5 copy.35
  21.1 0.5 copy.36
  21.6 0.0 copy-start
  21.6 0.5 maximum_maximum_fusion.cband_hbm
  22.1 0.0 collective-permute-done.2
  22.2 0.6 copy-done
  22.8 28.9 %shard_map.55 = f32[4,64,128]{2,1,0:T(8,128)S(1)} custom-call(s32[6]{0:T(128)S(1)} %stack.27.lim_ref, f32[24]{0:T(128)S(1)} %pad_maximum_fusion.2.prm_ref, f32[32,64,128]{2,1,0:T(8,128)S(1)} %copy-done, f32[4,64,128]{2,1,0:T(8,128)S(1)} %collective-permute-done.zlo_hbm, f32[4,64,128]{2,1,0:T(8,128)S(1)} %collective-permute-done.1.zhi_hbm, ...), custom_call_target="tpu_custom_call" | custom-call | flops 133693440 | bytes 3080192 | tf_op jit(solution)/shard_map/pallas_call | solution.py:190
  51.8 12.9 %all_to_all.5 = f32[4,8,8,128]{3,2,0,1:T(8,128)S(1)} all-to-all(f32[4,8,8,128]{3,2,0,1:T(8,128)S(1)} %copy.37), channel_id=1, replica_groups=mesh['gx'=2,'gy'=2,'gz'=8] {'gz'}, dimensions={1} | all-to-all | bytes 262144 | tf_op jit(solution)/shard_map/all_to_all | solution.py:244
  64.7 0.6 pad_maximum_fusion.1
  (13 shorter events, 0.2 us)
Async XLA Ops:
  1.0 8.0 %collective-permute-start = (f32[4,64,128]{2,1,0:T(8,128)S(1)}, f32[4,64,128]{2,1,0:T(8,128)S(1)}, u32[]{:S(2)}, u32[]{:S(2)}) collective-permute-start(f32[4,64,128]{2,1,0:T(8,128)S(1)} %get-tuple-element.12), channel_id=1, source_target_pairs={{0,1},{1,2},{2,3},{3,4},{4,5},{5,6},{6,7},{8,9},{9,10},{10,11},{11... | collective-permute-start | bytes 393224 | tf_op jit(solution)/shard_map/ppermute | solution.py:62
  5.9 6.9 %collective-permute-start.1 = (f32[4,64,128]{2,1,0:T(8,128)S(1)}, f32[4,64,128]{2,1,0:T(8,128)S(1)}, u32[]{:S(2)}, u32[]{:S(2)}) collective-permute-start(f32[4,64,128]{2,1,0:T(8,128)S(1)} %get-tuple-element.11), channel_id=1, source_target_pairs={{1,0},{2,1},{3,2},{4,3},{5,4},{6,5},{7,6},{9,8},{10,9},{11,10},{12... | collective-permute-start | bytes 393224 | tf_op jit(solution)/shard_map/ppermute | solution.py:62
  13.3 8.8 %collective-permute-start.2 = (f32[40,4,128]{2,1,0:T(4,128)S(1)}, f32[40,4,128]{2,1,0:T(4,128)S(1)}, u32[]{:S(2)}, u32[]{:S(2)}) collective-permute-start(f32[40,4,128]{2,1,0:T(4,128)S(1)} %slice_select_fusion.1), channel_id=1, source_target_pairs={{0,16},{16,0},{1,17},{17,1},{2,18},{18,2},{3,19},{19,3},{4,20},{20... | collective-permute-start | bytes 245768 | tf_op jit(solution)/shard_map/ppermute | solution.py:62
  13.5 4.3 %collective-permute-start.4 = (f32[40,4,4]{2,1,0:T(4,128)S(1)}, f32[40,4,4]{2,1,0:T(4,128)S(1)}, u32[]{:S(2)}, u32[]{:S(2)}) collective-permute-start(f32[40,4,4]{2,1,0:T(4,128)S(1)} %slice_select_fusion), channel_id=1, source_target_pairs={{0,24},{8,16},{16,8},{24,0},{1,25},{9,17},{17,9},{25,1},{2,26},{10... | collective-permute-start | bytes 7688 | tf_op jit(solution)/shard_map/ppermute | solution.py:62
  16.1 4.5 %collective-permute-start.3 = (f32[40,64,4]{1,0,2:T(8,128)S(1)}, f32[40,64,4]{1,0,2:T(8,128)S(1)}, u32[]{:S(2)}, u32[]{:S(2)}) collective-permute-start(f32[40,64,4]{1,0,2:T(8,128)S(1)} %broadcast_select_fusion.8), channel_id=1, source_target_pairs={{0,8},{8,0},{1,9},{9,1},{2,10},{10,2},{3,11},{11,3},{4,12},{12,4},... | collective-permute-start | bytes 122888 | tf_op jit(solution)/shard_map/ppermute | solution.py:62
  21.6 1.2 %copy-start = (f32[32,64,128]{2,1,0:T(8,128)S(1)}, f32[32,64,128]{2,1,0:T(8,128)}, u32[]{:S(2)}) copy-start(f32[32,64,128]{2,1,0:T(8,128)} %x_hbm.1) | copy-start | bytes 3145732

commit v7 on v3

--- a/solution.py
+++ b/solution.py
@@ -100,7 +100,7 @@
     return rate * d / (1.0 + q * q)
 
 
-def render_kernel(lim_ref, prm_ref, x_hbm, zlo_hbm, zhi_hbm, rband_hbm, cband_hbm, out_ref, a_ref, b_ref, m_ref, sem,
+def render_kernel(lim_ref, prm_ref, x_hbm, zlo_hbm, zhi_hbm, rband_hbm, cband_hbm, out_ref, a_ref, b_ref, m_ref, acc_ref, sem,
                   *, interior, h):
     depth, rows, lanes = a_ref.shape
     d_in, r_in, l_in = interior
@@ -126,8 +126,9 @@
     wid = [prm_ref[MATERIALS + k] for k in range(MATERIALS)]
     den = [prm_ref[2 * MATERIALS + k] for k in range(MATERIALS)]
     col = [[prm_ref[3 * MATERIALS + ch * MATERIALS + k] for k in range(MATERIALS)] for ch in range(CHANNELS)]
-    for ch in range(CHANNELS + 1):
-        out_ref[ch] = jnp.zeros((r_in, l_in), jnp.float32)
+    out_ref[CHANNELS] = jnp.zeros((r_in, l_in), jnp.float32)
+    for k in range(MATERIALS):
+        acc_ref[k] = jnp.zeros((r_in, l_in), jnp.float32)
 
     for cp in copies:
         cp.wait()
@@ -168,15 +169,15 @@
         ext = bumps[0] + bumps[1] + bumps[2] + bumps[3]
         run = out_ref[CHANNELS]
         through = jnp.exp(-h * run)
-        for ch in range(CHANNELS):
-            emit = col[ch][0] * bumps[0] + col[ch][1] * bumps[1] + col[ch][2] * bumps[2] + col[ch][3] * bumps[3]
-            out_ref[ch] = out_ref[ch] + through * emit
+        for k in range(MATERIALS):
+            acc_ref[k] = acc_ref[k] + through * bumps[k]
         out_ref[CHANNELS] = run + ext
         return g
 
     lax.fori_loop(z0, z1, final, g0)
     for ch in range(CHANNELS):
-        out_ref[ch] = h * out_ref[ch]
+        emit = col[ch][0] * acc_ref[0] + col[ch][1] * acc_ref[1] + col[ch][2] * acc_ref[2] + col[ch][3] * acc_ref[3]
+        out_ref[ch] = h * emit
 
 
 def render_block(pieces, lim, prm, interior, h):
@@ -193,6 +194,7 @@
             pltpu.VMEM((depth, rows, lanes), jnp.float32),
             pltpu.VMEM((depth, rows, lanes), jnp.float32),
             pltpu.VMEM((rows, lanes), jnp.float32),
+            pltpu.VMEM((MATERIALS, r_in, l_in), jnp.float32),
             pltpu.SemaphoreType.DMA((5,)),
         ],
         compiler_params=pltpu.CompilerParams(vmem_limit_bytes=48 * 1024 * 1024),

time: 65 us -> 64.4 us (level)
  no operation moved by 1% of the time
where the time goes in v7:
time: 64.4 us; the launch traced here: 64.1 us
  Pallas kernels  27.8 us (43%)
  blocking collectives  12.9 us (20%)
  starting transfers between devices  8.53 us (13%)
  waiting for transfers between devices  6.35 us (10%)
  local copies, waits for them, and re-layouts  6.2 us (10%)
  other arithmetic  2.21 us (3%)
    pallas_call x1, Pallas kernels, render_block(): pl.pallas_call(kernel, out_shape=jax.ShapeDtypeStruct((CHANNELS + 1, r_in...  27.8 us
    all_to_all x1, blocking collectives, shards(): got = lax.all_to_all(parts, 'gz', 1, 1, tiled=True)  12.9 us
    ppermute x5, starting transfers between devices, halo_stage(): got = lax.ppermute(piece, tuple((a for a, _, _ in used)), pairs)  8.53 us
    ppermute x5, waiting for transfers between devices, halo_stage(): got = lax.ppermute(piece, tuple((a for a, _, _ in used)), pairs)  6.35 us
    unnamed x4, local copies, waits for them, and re-layouts  1.93 us
    slice x3, local copies, waits for them, and re-layouts, halo_stage(): lo = lax.slice_in_dim(piece, 0, width, axis=d)  1.92 us
  transfers between devices with their start and end apart: 5, of which 3 were waited for; matrix products, arithmetic and copies ran while one was open for 9% of the time, Pallas kernels for 0%

profile of v7, /device:TPU:0, one launch (start us, length us, event | category | flops | bytes accessed | tf_op | source)
XLA Modules:
  0.0 64.1 jit_solution(13057257104367366001)
XLA Ops:
  0.0 1.0 %fusion.19 = (f32[4,64,128]{2,1,0:T(8,128)S(1)}, f32[4,64,128]{2,1,0:T(8,128)S(1)}) fusion(f32[32,64,128]{2,1,0:T(8,128)} %x_hbm.1), kind=kLoop, calls=%fused_computation.59 | loop fusion | bytes 524288 | tf_op jit(solution)/shard_map/slice | solution.py:52
  1.0 4.9 %collective-permute-start = (f32[4,64,128]{2,1,0:T(8,128)S(1)}, f32[4,64,128]{2,1,0:T(8,128)S(1)}, u32[]{:S(2)}, u32[]{:S(2)}) collective-permute-start(f32[4,64,128]{2,1,0:T(8,128)S(1)} %get-tuple-element.12), channel_id=1, source_target_pairs={{0,1},{1,2},{2,3},{3,4},{4,5},{5,6},{6,7},{8,9},{9,10},{10,11},{11... | collective-permute-start | bytes 393224 | tf_op jit(solution)/shard_map/ppermute | solution.py:62
  5.9 1.3 %collective-permute-start.1 = (f32[4,64,128]{2,1,0:T(8,128)S(1)}, f32[4,64,128]{2,1,0:T(8,128)S(1)}, u32[]{:S(2)}, u32[]{:S(2)}) collective-permute-start(f32[4,64,128]{2,1,0:T(8,128)S(1)} %get-tuple-element.11), channel_id=1, source_target_pairs={{1,0},{2,1},{3,2},{4,3},{5,4},{6,5},{7,6},{9,8},{10,9},{11,10},{12... | collective-permute-start | bytes 393224 | tf_op jit(solution)/shard_map/ppermute | solution.py:62
  7.3 0.8 %reshape.210 = f32[12]{0:T(128)S(1)} reshape(f32[3,4]{1,0:T(4,128)} %param.9) | data formatting | bytes 96 | tf_op jit(solution)/shard_map/reshape | solution.py:236
  8.0 0.1 pad.5.clone
  8.1 0.1 stack.27.lim_ref
  8.2 0.8 %pad_maximum_fusion.2.prm_ref = f32[24]{0:T(128)S(1)} fusion(f32[12]{0:T(128)S(1)} %reshape.210, f32[4]{0:T(128)} %param.8, f32[4]{0:T(128)} %param.7, f32[4]{0:T(128)} %param.6), kind=kLoop, calls=%fused_computation.57 | loop fusion | flops 72 | bytes 192 | tf_op jit(solution)/shard_map/concatenate | solution.py:236
  8.9 0.0 collective-permute-done.zlo_hbm
  9.0 1.3 %constant_dynamic-update-slice_fusion.1 = f32[40,64,128]{2,1,0:T(8,128)S(1)} fusion(f32[40,64,128]{2,1,0:T(8,128)S(1)} %constant_dynamic-update-slice_fusion.2, f32[32,64,128]{2,1,0:T(8,128)} %x_hbm.1), kind=kLoop, calls=%fused_computation.37 | loop fusion | bytes 2097152
  10.3 2.5 %collective-permute-done.1.zhi_hbm = f32[4,64,128]{2,1,0:T(8,128)S(1)} collective-permute-done((f32[4,64,128]{2,1,0:T(8,128)S(1)}, f32[4,64,128]{2,1,0:T(8,128)S(1)}, u32[]{:S(2)}, u32[]{:S(2)}) %collective-permute-start.1) | collective-permute-done | bytes 131104 | tf_op jit(solution)/shard_map/ppermute | solution.py:62
  12.8 0.5 fusion.18
  13.3 0.1 collective-permute-start.2
  13.4 0.1 slice_select_fusion
  13.5 1.7 %collective-permute-start.4 = (f32[40,4,4]{2,1,0:T(4,128)S(1)}, f32[40,4,4]{2,1,0:T(4,128)S(1)}, u32[]{:S(2)}, u32[]{:S(2)}) collective-permute-start(f32[40,4,4]{2,1,0:T(4,128)S(1)} %slice_select_fusion), channel_id=1, source_target_pairs={{0,24},{8,16},{16,8},{24,0},{1,25},{9,17},{17,9},{25,1},{2,26},{10... | collective-permute-start | bytes 7688 | tf_op jit(solution)/shard_map/ppermute | solution.py:62
  15.1 0.5 copy.33
  15.6 0.5 copy.34
  16.1 0.6 collective-permute-start.3
  16.7 1.1 %collective-permute-done.4 = f32[40,4,4]{2,1,0:T(4,128)S(1)} collective-permute-done((f32[40,4,4]{2,1,0:T(4,128)S(1)}, f32[40,4,4]{2,1,0:T(4,128)S(1)}, u32[]{:S(2)}, u32[]{:S(2)}) %collective-permute-start.4) | collective-permute-done | bytes 2592 | tf_op jit(solution)/shard_map/ppermute | solution.py:62
  17.8 0.1 broadcast_select_fusion.3
  17.8 2.8 %collective-permute-done.3 = f32[40,64,4]{1,0,2:T(8,128)S(1)} collective-permute-done((f32[40,64,4]{1,0,2:T(8,128)S(1)}, f32[40,64,4]{1,0,2:T(8,128)S(1)}, u32[]{:S(2)}, u32[]{:S(2)}) %collective-permute-start.3) | collective-permute-done | bytes 40992 | tf_op jit(solution)/shard_map/ppermute | solution.py:62
  20.6 0.5 copy.35
  21.1 0.5 copy.36
  21.6 0.0 copy-start
  21.6 0.5 maximum_maximum_fusion.cband_hbm
  22.1 0.0 collective-permute-done.2
  22.2 0.6 copy-done
  22.8 27.8 %shard_map.55 = f32[4,64,128]{2,1,0:T(8,128)S(1)} custom-call(s32[6]{0:T(128)S(1)} %stack.27.lim_ref, f32[24]{0:T(128)S(1)} %pad_maximum_fusion.2.prm_ref, f32[32,64,128]{2,1,0:T(8,128)S(1)} %copy-done, f32[4,64,128]{2,1,0:T(8,128)S(1)} %collective-permute-done.zlo_hbm, f32[4,64,128]{2,1,0:T(8,128)S(1)} %collective-permute-done.1.zhi_hbm, ...), custom_call_target="tpu_custom_call" | custom-call | flops 133693440 | bytes 3080192 | tf_op jit(solution)/shard_map/pallas_call | solution.py:188
  50.6 12.9 %all_to_all.5 = f32[4,8,8,128]{3,2,0,1:T(8,128)S(1)} all-to-all(f32[4,8,8,128]{3,2,0,1:T(8,128)S(1)} %copy.37), channel_id=1, replica_groups=mesh['gx'=2,'gy'=2,'gz'=8] {'gz'}, dimensions={1} | all-to-all | bytes 262144 | tf_op jit(solution)/shard_map/all_to_all | solution.py:242
  63.5 0.6 pad_maximum_fusion.1
  (13 shorter events, 0.2 us)
Async XLA Ops:
  1.0 8.0 %collective-permute-start = (f32[4,64,128]{2,1,0:T(8,128)S(1)}, f32[4,64,128]{2,1,0:T(8,128)S(1)}, u32[]{:S(2)}, u32[]{:S(2)}) collective-permute-start(f32[4,64,128]{2,1,0:T(8,128)S(1)} %get-tuple-element.12), channel_id=1, source_target_pairs={{0,1},{1,2},{2,3},{3,4},{4,5},{5,6},{6,7},{8,9},{9,10},{10,11},{11... | collective-permute-start | bytes 393224 | tf_op jit(solution)/shard_map/ppermute | solution.py:62
  5.9 6.9 %collective-permute-start.1 = (f32[4,64,128]{2,1,0:T(8,128)S(1)}, f32[4,64,128]{2,1,0:T(8,128)S(1)}, u32[]{:S(2)}, u32[]{:S(2)}) collective-permute-start(f32[4,64,128]{2,1,0:T(8,128)S(1)} %get-tuple-element.11), channel_id=1, source_target_pairs={{1,0},{2,1},{3,2},{4,3},{5,4},{6,5},{7,6},{9,8},{10,9},{11,10},{12... | collective-permute-start | bytes 393224 | tf_op jit(solution)/shard_map/ppermute | solution.py:62
  13.3 8.8 %collective-permute-start.2 = (f32[40,4,128]{2,1,0:T(4,128)S(1)}, f32[40,4,128]{2,1,0:T(4,128)S(1)}, u32[]{:S(2)}, u32[]{:S(2)}) collective-permute-start(f32[40,4,128]{2,1,0:T(4,128)S(1)} %slice_select_fusion.1), channel_id=1, source_target_pairs={{0,16},{16,0},{1,17},{17,1},{2,18},{18,2},{3,19},{19,3},{4,20},{20... | collective-permute-start | bytes 245768 | tf_op jit(solution)/shard_map/ppermute | solution.py:62
  13.5 4.3 %collective-permute-start.4 = (f32[40,4,4]{2,1,0:T(4,128)S(1)}, f32[40,4,4]{2,1,0:T(4,128)S(1)}, u32[]{:S(2)}, u32[]{:S(2)}) collective-permute-start(f32[40,4,4]{2,1,0:T(4,128)S(1)} %slice_select_fusion), channel_id=1, source_target_pairs={{0,24},{8,16},{16,8},{24,0},{1,25},{9,17},{17,9},{25,1},{2,26},{10... | collective-permute-start | bytes 7688 | tf_op jit(solution)/shard_map/ppermute | solution.py:62
  16.1 4.5 %collective-permute-start.3 = (f32[40,64,4]{1,0,2:T(8,128)S(1)}, f32[40,64,4]{1,0,2:T(8,128)S(1)}, u32[]{:S(2)}, u32[]{:S(2)}) collective-permute-start(f32[40,64,4]{1,0,2:T(8,128)S(1)} %broadcast_select_fusion.8), channel_id=1, source_target_pairs={{0,8},{8,0},{1,9},{9,1},{2,10},{10,2},{3,11},{11,3},{4,12},{12,4},... | collective-permute-start | bytes 122888 | tf_op jit(solution)/shard_map/ppermute | solution.py:62
  21.6 1.2 %copy-start = (f32[32,64,128]{2,1,0:T(8,128)S(1)}, f32[32,64,128]{2,1,0:T(8,128)}, u32[]{:S(2)}) copy-start(f32[32,64,128]{2,1,0:T(8,128)} %x_hbm.1) | copy-start | bytes 3145732

commit v8 on v7

--- a/solution.py
+++ b/solution.py
@@ -100,125 +100,196 @@
     return rate * d / (1.0 + q * q)
 
 
-def render_kernel(lim_ref, prm_ref, x_hbm, zlo_hbm, zhi_hbm, rband_hbm, cband_hbm, out_ref, a_ref, b_ref, m_ref, acc_ref, sem,
-                  *, interior, h):
-    depth, rows, lanes = a_ref.shape
-    d_in, r_in, l_in = interior
-    halo = STEPS
-    copies = [
-        pltpu.make_async_copy(x_hbm, b_ref.at[halo:halo + d_in, 0:r_in, 0:l_in], sem.at[0]),
-        pltpu.make_async_copy(zlo_hbm, b_ref.at[0:halo, 0:r_in, 0:l_in], sem.at[1]),
-        pltpu.make_async_copy(zhi_hbm, b_ref.at[halo + d_in:depth, 0:r_in, 0:l_in], sem.at[2]),
-        pltpu.make_async_copy(rband_hbm, b_ref.at[:, r_in:rows, 0:l_in], sem.at[3]),
-        pltpu.make_async_copy(cband_hbm, b_ref.at[:, :, l_in:lanes], sem.at[4]),
-    ]
-    for cp in copies:
-        cp.start()
-
+def make_mask(lim_ref, m_ref, rows, lanes, r_in, l_in):
     row = lax.broadcasted_iota(jnp.int32, (rows, lanes), 0)
     lane = lax.broadcasted_iota(jnp.int32, (rows, lanes), 1)
-    row_at = jnp.where(row < r_in + halo, row, row - rows)
+    row_at = jnp.where(row < r_in + STEPS, row, row - rows)
     lane_at = jnp.where(lane < (l_in + lanes) // 2, lane, lane - lanes)
     ok = (row_at >= lim_ref[2]) & (row_at < lim_ref[3]) & (lane_at >= lim_ref[4]) & (lane_at < lim_ref[5])
     m_ref[...] = jnp.where(ok, 1.0, 0.0).astype(jnp.float32)
 
+
+def smooth_planes(lim_ref, m_ref, src, dst, z0, z1):
+    rows, lanes = m_ref.shape
+    g0 = flux(src[z0] - src[z0 - 1], RATE_DEPTH)
+
+    def body(z, g_prev):
+        c = src[z]
+        g = flux(src[z + 1] - c, RATE_DEPTH)
+        fr = flux(pltpu.roll(c, rows - 1, 0) - c, RATE_PLANE)
+        fc = flux(pltpu.roll(c, lanes - 1, 1) - c, RATE_PLANE)
+        new = c + (g - g_prev) + (fr - pltpu.roll(fr, 1, 0)) + (fc - pltpu.roll(fc, 1, 1))
+        inside = (z >= lim_ref[0]) & (z < lim_ref[1])
+        zf = jnp.where(inside, 1.0, 0.0).astype(jnp.float32)
+        dst[z] = new * (m_ref[...] * zf)
+        return g
+
+    lax.fori_loop(z0, z1, body, g0)
+
+
+def scan_planes(prm_ref, src, acc_ref, run_ref, z0, z1, h):
+    rows, lanes = src.shape[1:]
+    r_in, l_in = run_ref.shape
     cen = [prm_ref[k] for k in range(MATERIALS)]
     wid = [prm_ref[MATERIALS + k] for k in range(MATERIALS)]
     den = [prm_ref[2 * MATERIALS + k] for k in range(MATERIALS)]
-    col = [[prm_ref[3 * MATERIALS + ch * MATERIALS + k] for k in range(MATERIALS)] for ch in range(CHANNELS)]
-    out_ref[CHANNELS] = jnp.zeros((r_in, l_in), jnp.float32)
+    run_ref[...] = jnp.zeros((r_in, l_in), jnp.float32)
     for k in range(MATERIALS):
         acc_ref[k] = jnp.zeros((r_in, l_in), jnp.float32)
-
-    for cp in copies:
-        cp.wait()
-
-    def smooth(src, dst, s):
-        z0, z1 = s + 1, depth - 1 - s
-        g0 = flux(src[z0] - src[z0 - 1], RATE_DEPTH)
-
-        def body(z, g_prev):
-            c = src[z]
-            g = flux(src[z + 1] - c, RATE_DEPTH)
-            fr = flux(pltpu.roll(c, rows - 1, 0) - c, RATE_PLANE)
-            fc = flux(pltpu.roll(c, lanes - 1, 1) - c, RATE_PLANE)
-            new = c + (g - g_prev) + (fr - pltpu.roll(fr, 1, 0)) + (fc - pltpu.roll(fc, 1, 1))
-            inside = (z >= lim_ref[0]) & (z < lim_ref[1])
-            zf = jnp.where(inside, 1.0, 0.0).astype(jnp.float32)
-            dst[z] = new * (m_ref[...] * zf)
-            return g
-
-        lax.fori_loop(z0, z1, body, g0)
-
-    smooth(b_ref, a_ref, 0)
-    smooth(a_ref, b_ref, 1)
-    smooth(b_ref, a_ref, 2)
-
-    z0, z1 = halo, halo + d_in
-    g0 = flux(a_ref[z0, 0:r_in, 0:l_in] - a_ref[z0 - 1, 0:r_in, 0:l_in], RATE_DEPTH)
+    g0 = flux(src[z0, 0:r_in, 0:l_in] - src[z0 - 1, 0:r_in, 0:l_in], RATE_DEPTH)
 
     def final(z, g_prev):
-        ci = a_ref[z, 0:r_in, 0:l_in]
-        g = flux(a_ref[z + 1, 0:r_in, 0:l_in] - ci, RATE_DEPTH)
-        c0 = a_ref[z, :, 0:l_in]
+        ci = src[z, 0:r_in, 0:l_in]
+        g = flux(src[z + 1, 0:r_in, 0:l_in] - ci, RATE_DEPTH)
+        c0 = src[z, :, 0:l_in]
         fr = flux(pltpu.roll(c0, rows - 1, 0) - c0, RATE_PLANE)
-        cr = a_ref[z, 0:r_in, :]
+        cr = src[z, 0:r_in, :]
         fc = flux(pltpu.roll(cr, lanes - 1, 1) - cr, RATE_PLANE)
         v = ci + (g - g_prev) + (fr - pltpu.roll(fr, 1, 0))[0:r_in] + (fc - pltpu.roll(fc, 1, 1))[:, 0:l_in]
         bumps = [den[k] * jnp.exp(-(((v - cen[k]) / wid[k]) ** 2)) for k in range(MATERIALS)]
         ext = bumps[0] + bumps[1] + bumps[2] + bumps[3]
-        run = out_ref[CHANNELS]
+        run = run_ref[...]
         through = jnp.exp(-h * run)
         for k in range(MATERIALS):
             acc_ref[k] = acc_ref[k] + through * bumps[k]
-        out_ref[CHANNELS] = run + ext
+        run_ref[...] = run + ext
         return g
 
     lax.fori_loop(z0, z1, final, g0)
+
+
+def core_copies(x_hbm, rband_hbm, cband_hbm, b_ref, sem, lo, hi, at):
+    r_in, l_in = x_hbm.shape[1:]
+    rows, lanes = b_ref.shape[1:]
+    p0, p1 = lo + STEPS, hi + STEPS
+    return [
+        pltpu.make_async_copy(x_hbm.at[lo:hi], b_ref.at[p0:p1, 0:r_in, 0:l_in], sem.at[at]),
+        pltpu.make_async_copy(rband_hbm.at[lo:hi], b_ref.at[p0:p1, r_in:rows, 0:l_in], sem.at[at + 1]),
+        pltpu.make_async_copy(cband_hbm.at[lo:hi], b_ref.at[p0:p1, :, l_in:lanes], sem.at[at + 2]),
+    ]
+
+
+def inner_kernel(lim_ref, prm_ref, x_hbm, rband_hbm, cband_hbm, ex_ref, part_ref, a_ref, b_ref, m_ref, sem, *, h):
+    depth, rows, lanes = a_ref.shape
+    d_in, r_in, l_in = x_hbm.shape
+    copies = core_copies(x_hbm, rband_hbm, cband_hbm, b_ref, sem, 0, d_in, 0)
+    for cp in copies:
+        cp.start()
+    make_mask(lim_ref, m_ref, rows, lanes, r_in, l_in)
+    for cp in copies:
+        cp.wait()
+    e = STEPS
+    smooth_planes(lim_ref, m_ref, b_ref, a_ref, e + 1, depth - e - 1)
+    smooth_planes(lim_ref, m_ref, a_ref, b_ref, e + 2, depth - e - 2)
+    smooth_planes(lim_ref, m_ref, b_ref, a_ref, e + 3, depth - e - 3)
+    scan_planes(prm_ref, a_ref, part_ref.at[0:MATERIALS], part_ref.at[MATERIALS], e + 4, depth - e - 4, h)
+    for s, src in ((0, a_ref), (1, b_ref), (2, a_ref)):
+        for j, z in enumerate((e + 1 + s, e + 2 + s, depth - e - 3 - s, depth - e - 2 - s)):
+            ex_ref[s, j] = src[z]
+
+
+def outer_kernel(lim_ref, prm_ref, x_hbm, rband_hbm, cband_hbm, zlo_hbm, zhi_hbm, ex_hbm, part_ref,
+                 out_ref, a_ref, b_ref, m_ref, acc_ref, run_ref, sem, *, h):
+    depth, rows, lanes = a_ref.shape
+    d_in, r_in, l_in = x_hbm.shape
+    copies = core_copies(x_hbm, rband_hbm, cband_hbm, b_ref, sem, 0, 2, 0)
+    copies += core_copies(x_hbm, rband_hbm, cband_hbm, b_ref, sem, d_in - 2, d_in, 3)
+    copies.append(pltpu.make_async_copy(zlo_hbm, b_ref.at[0:STEPS], sem.at[6]))
+    copies.append(pltpu.make_async_copy(zhi_hbm, b_ref.at[depth - STEPS:depth], sem.at[7]))
+    for cp in copies:
+        cp.start()
+    make_mask(lim_ref, m_ref, rows, lanes, r_in, l_in)
+    for cp in copies:
+        cp.wait()
+    e = STEPS
+    bufs = (a_ref, b_ref, a_ref)
+    srcs = (b_ref, a_ref, b_ref)
+    for s in range(STEPS - 1):
+        smooth_planes(lim_ref, m_ref, srcs[s], bufs[s], s + 1, s + 1 + STEPS)
+        smooth_planes(lim_ref, m_ref, srcs[s], bufs[s], depth - STEPS - 1 - s, depth - 1 - s)
+        for j, z in enumerate((e + 1 + s, e + 2 + s, depth - e - 3 - s, depth - e - 2 - s)):
+            cp = pltpu.make_async_copy(ex_hbm.at[s, j], bufs[s].at[z], sem.at[8])
+            cp.start()
+            cp.wait()
+    top = STEPS
+    scan_planes(prm_ref, a_ref, acc_ref.at[0], run_ref.at[0], top, top + STEPS, h)
+    scan_planes(prm_ref, a_ref, acc_ref.at[1], run_ref.at[1], depth - 2 * STEPS, depth - STEPS, h)
+    s_lo, s_mid, s_hi = run_ref[0], part_ref[MATERIALS], run_ref[1]
+    t_lo = jnp.exp(-h * s_lo)
+    t_mid = jnp.exp(-h * (s_lo + s_mid))
+    acc = [acc_ref[0, k] + t_lo * part_ref[k] + t_mid * acc_ref[1, k] for k in range(MATERIALS)]
+    col = [[prm_ref[3 * MATERIALS + ch * MATERIALS + k] for k in range(MATERIALS)] for ch in range(CHANNELS)]
     for ch in range(CHANNELS):
-        emit = col[ch][0] * acc_ref[0] + col[ch][1] * acc_ref[1] + col[ch][2] * acc_ref[2] + col[ch][3] * acc_ref[3]
-        out_ref[ch] = h * emit
-
-
-def render_block(pieces, lim, prm, interior, h):
-    d_in, r_in, l_in = interior
+        out_ref[ch] = h * (col[ch][0] * acc[0] + col[ch][1] * acc[1] + col[ch][2] * acc[2] + col[ch][3] * acc[3])
+    out_ref[CHANNELS] = (s_lo + s_mid) + s_hi
+
+
+def render_block(x, rband, cband, zlo, zhi, lim, prm, h):
+    d_in, r_in, l_in = x.shape
     depth, rows, lanes = d_in + 2 * STEPS, r_in + 2 * STEPS, LANES
     cells = depth * rows * lanes
-    kernel = functools.partial(render_kernel, interior=interior, h=h)
+    smem = pl.BlockSpec(memory_space=pltpu.SMEM)
+    anyspace = pl.BlockSpec(memory_space=pl.ANY)
+    vmem = pl.BlockSpec(memory_space=pltpu.VMEM)
+    params = pltpu.CompilerParams(vmem_limit_bytes=48 * 1024 * 1024)
+    planes = [pltpu.VMEM((depth, rows, lanes), jnp.float32)] * 2 + [pltpu.VMEM((rows, lanes), jnp.float32)]
+    inner_frac = (d_in - 2 * STEPS) / d_in
+    ex, part = pl.pallas_call(
+        functools.partial(inner_kernel, h=h),
+        out_shape=(
+            jax.ShapeDtypeStruct((STEPS - 1, 4, rows, lanes), jnp.float32),
+            jax.ShapeDtypeStruct((MATERIALS + 1, r_in, l_in), jnp.float32),
+        ),
+        in_specs=[smem, smem, anyspace, anyspace, anyspace],
+        out_specs=(vmem, vmem),
+        scratch_shapes=planes + [pltpu.SemaphoreType.DMA((3,))],
+        compiler_params=params,
+        cost_estimate=pl.CostEstimate(
+            flops=int(inner_frac * (cells * STEPS * 40 + d_in * r_in * l_in * 60)),
+            transcendentals=int(inner_frac * d_in * r_in * l_in * (MATERIALS + 1)),
+            bytes_accessed=int(cells * 4),
+        ),
+    )(lim, prm, x, rband, cband)
     return pl.pallas_call(
-        kernel,
+        functools.partial(outer_kernel, h=h),
         out_shape=jax.ShapeDtypeStruct((CHANNELS + 1, r_in, l_in), jnp.float32),
-        in_specs=[pl.BlockSpec(memory_space=pltpu.SMEM)] * 2 + [pl.BlockSpec(memory_space=pl.ANY)] * 5,
-        out_specs=pl.BlockSpec(memory_space=pltpu.VMEM),
-        scratch_shapes=[
-            pltpu.VMEM((depth, rows, lanes), jnp.float32),
-            pltpu.VMEM((depth, rows, lanes), jnp.float32),
-            pltpu.VMEM((rows, lanes), jnp.float32),
-            pltpu.VMEM((MATERIALS, r_in, l_in), jnp.float32),
-            pltpu.SemaphoreType.DMA((5,)),
+        in_specs=[smem, smem] + [anyspace] * 6 + [vmem],
+        out_specs=vmem,
+        scratch_shapes=planes + [
+            pltpu.VMEM((2, MATERIALS, r_in, l_in), jnp.float32),
+            pltpu.VMEM((2, r_in, l_in), jnp.float32),
+            pltpu.SemaphoreType.DMA((9,)),
         ],
-        compiler_params=pltpu.CompilerParams(vmem_limit_bytes=48 * 1024 * 1024),
+        compiler_params=params,
         cost_estimate=pl.CostEstimate(
-            flops=int(cells * STEPS * 40 + d_in * r_in * l_in * 60),
-            transcendentals=int(d_in * r_in * l_in * (MATERIALS + 1)),
-            bytes_accessed=int(cells * 4 + (CHANNELS + 1) * r_in * l_in * 4),
+            flops=int((1 - inner_frac) * (cells * STEPS * 40 + d_in * r_in * l_in * 60)),
+            transcendentals=int((1 - inner_frac) * d_in * r_in * l_in * (MATERIALS + 1)),
+            bytes_accessed=int(cells * 4 // 4),
         ),
-    )(lim, prm, *pieces)
+    )(lim, prm, x, rband, cband, zlo, zhi, ex, part)
 
 
 def shards(phase_field, centres, widths, densities, colours):
     depth_cells, row_cells, col_cells = phase_field.shape
     groups = lax.axis_size("gz")
     h = 1.0 / (depth_cells * groups)
-    zblock = halo_stage(phase_field, ((0, "gz"),), STEPS)
-    zlo, zhi = zblock("lo"), zblock("hi")
-    deep = jnp.concatenate([zlo, phase_field, zhi], axis=0)
-    plane = halo_stage(deep, ((1, "gx"), (2, "gy")), STEPS)
+    plane = halo_stage(phase_field, ((1, "gx"), (2, "gy")), STEPS)
     rband = jnp.concatenate([plane("hi", "mid"), plane("lo", "mid")], axis=1)
     right = jnp.concatenate([plane("mid", "hi"), plane("hi", "hi"), plane("lo", "hi")], axis=1)
     left = jnp.concatenate([plane("mid", "lo"), plane("hi", "lo"), plane("lo", "lo")], axis=1)
     fill = jnp.zeros(right.shape[:2] + (LANES - col_cells - 2 * STEPS,), jnp.float32)
     cband = jnp.concatenate([right, fill, left], axis=2)
+    def face(lo, hi):
+        core = jnp.concatenate([phase_field[lo:hi], rband[lo:hi]], axis=1)
+        return jnp.concatenate([core, cband[lo:hi]], axis=2)
+
+    lo_face, hi_face = face(0, STEPS), face(depth_cells - STEPS, depth_cells)
+    zlo = jnp.zeros_like(lo_face)
+    zhi = jnp.zeros_like(hi_face)
+    for pairs, send_hi, land_lo in axis_moves("gz"):
+        got = lax.ppermute(pick(send_hi, hi_face, lo_face), "gz", pairs)
+        zlo = zlo + pick(land_lo, got, jnp.zeros_like(got))
+        zhi = zhi + pick(land_lo, jnp.zeros_like(got), got)
 
     z_lo = STEPS - lax.axis_index("gz") * depth_cells
     r_lo = -lax.axis_index("gx") * row_cells
@@ -235,7 +306,7 @@
     ).astype(jnp.int32)
     prm = jnp.concatenate([centres, widths, densities, colours.reshape(-1)]).astype(jnp.float32)
 
-    seg = render_block((phase_field, zlo, zhi, rband, cband), lim, prm, (depth_cells, row_cells, col_cells), h)
+    seg = render_block(phase_field, rband, cband, zlo, zhi, lim, prm, h)
 
     rows_part = row_cells // groups
     parts = seg.reshape(CHANNELS + 1, groups, rows_part, col_cells)

time: 64.4 us -> 66.8 us (1.037)
  waiting for transfers between devices: 6.35 us -> 1.62 us
  other arithmetic: 2.21 us -> 6.8 us
  Pallas kernels: 27.8 us -> 29.9 us
    ppermute x0 -> x2, starting transfers between devices: none -> 5.84 us  [shards(): got = lax.ppermute(pick(send_hi, hi_face, lo_face), 'gz', pairs)]
    ppermute x5 -> x3, starting transfers between devices: 8.53 us -> 3.28 us  [halo_stage(): got = lax.ppermute(piece, tuple((a for a, _, _ in used)), pairs)]
    ppermute x5 -> x3, waiting for transfers between devices: 6.35 us -> 1.62 us  [halo_stage(): got = lax.ppermute(piece, tuple((a for a, _, _ in used)), pairs)]
    select_n x3, other arithmetic: 0.1 us -> 2.41 us  [halo_stage(): val = got if cond is True else jnp.where(cond, got, 0.0)]
    pallas_call x1 -> x2, Pallas kernels: 27.8 us -> 29.9 us  [the longest x1 21.6 us: render_block(): pl.pallas_call(functools.partial(inner_kernel, h=h), out_shape=(jax.Shape...]
    concatenate x1, other arithmetic: 0.5 us -> 1.75 us  [shards(): cband = jnp.concatenate([right, fill, left], axis=2)]
    select_n x3, other arithmetic: 0.16 us -> 1.1 us  [pick(): return jnp.where(cond, a, b)]
    select_n x2, local copies, waits for them, and re-layouts: 0.94 us -> 1.8 us  [halo_stage(): val = got if cond is True else jnp.where(cond, got, 0.0)]
  transfers between devices with their start and end apart: 5 -> 5, of which waited for: 3 -> 1; matrix products, arithmetic and copies ran while one was open for 9% -> 15% of each run, Pallas kernels for 0% -> 32%
where the time goes in v8:
time: 66.8 us; the launch traced here: 66.4 us
  Pallas kernels  29.9 us (45%)
  blocking collectives  12.8 us (19%)
  starting transfers between devices  9.13 us (14%)
  other arithmetic  6.8 us (10%)
  local copies, waits for them, and re-layouts  5.9 us (9%)
  waiting for transfers between devices  1.62 us (2%)
    pallas_call x1, Pallas kernels, render_block(): pl.pallas_call(functools.partial(inner_kernel, h=h), out_shape=(jax.Shape...  21.6 us
    all_to_all x1, blocking collectives, shards(): got = lax.all_to_all(parts, 'gz', 1, 1, tiled=True)  12.8 us
    pallas_call x1, Pallas kernels, render_block(): pl.pallas_call(functools.partial(outer_kernel, h=h), out_shape=jax.ShapeD...  8.31 us
    ppermute x2, starting transfers between devices, shards(): got = lax.ppermute(pick(send_hi, hi_face, lo_face), 'gz', pairs)  5.84 us
    ppermute x3, starting transfers between devices, halo_stage(): got = lax.ppermute(piece, tuple((a for a, _, _ in used)), pairs)  3.28 us
    select_n x3, other arithmetic, halo_stage(): val = got if cond is True else jnp.where(cond, got, 0.0)  2.41 us
    slice x1, local copies, waits for them, and re-layouts, halo_stage(): lo = lax.slice_in_dim(piece, 0, width, axis=d)  2 us
    select_n x2, local copies, waits for them, and re-layouts, halo_stage(): val = got if cond is True else jnp.where(cond, got, 0.0)  1.8 us
  transfers between devices with their start and end apart: 5, of which 1 were waited for; matrix products, arithmetic and copies ran while one was open for 15% of the time, Pallas kernels for 32%

profile of v8, /device:TPU:0, one launch (start us, length us, event | category | flops | bytes accessed | tf_op | source)
XLA Modules:
  0.0 66.4 jit_solution(7555518777820641088)
XLA Ops:
  0.0 1.0 %slice_select_fusion.1 = f32[32,4,128]{2,1,0:T(4,128)S(1)} fusion(f32[32,64,128]{2,1,0:T(8,128)} %x_hbm.3, pred[]{:T(512)S(6)} %eq.13), kind=kLoop, calls=%fused_computation.9 | loop fusion | flops 16384 | bytes 196609 | tf_op jit(solution)/shard_map/jit(_where)/select_n | solution.py:24
  1.0 0.6 collective-permute-start
  1.6 0.1 slice_select_fusion
  1.7 2.7 %collective-permute-start.2 = (f32[32,4,4]{2,1,0:T(4,128)S(1)}, f32[32,4,4]{2,1,0:T(4,128)}, u32[]{:S(2)}, u32[]{:S(2)}) collective-permute-start(f32[32,4,4]{2,1,0:T(4,128)S(1)} %slice_select_fusion), channel_id=1, source_target_pairs={{0,24},{8,16},{16,8},{24,0},{1,25},{9,17},{17,9},{25,1},{2,26},{10... | collective-permute-start | bytes 6152 | tf_op jit(solution)/shard_map/ppermute | solution.py:62
  4.3 2.0 %fusion.22 = (f32[32,64,4]{2,1,0:T(8,128)S(1)}, f32[32,64,4]{2,1,0:T(8,128)S(1)}) fusion(f32[32,64,128]{2,1,0:T(8,128)} %x_hbm.3), kind=kLoop, calls=%fused_computation.65 | loop fusion | bytes 131072 | tf_op jit(solution)/shard_map/slice | solution.py:52
  6.3 0.0 copy-start
  6.3 0.4 copy.36
  6.7 0.4 copy.37
  7.1 0.1 collective-permute-start.1
  7.2 0.4 copy-done
  7.6 0.7 %fusion.21 = (f32[4,64,128]{2,1,0:T(8,128)}, f32[4,64,128]{2,1,0:T(8,128)S(1)}) fusion(f32[32,64,128]{2,1,0:T(8,128)S(1)} %copy-done), kind=kLoop, calls=%fused_computation.64 | loop fusion | bytes 524288 | tf_op jit(solution)/shard_map/slice | solution.py:283
  8.2 0.1 pad.11.clone
  8.3 1.5 %broadcast_select_fusion.3 = (f32[32,4,4]{2,1,0:T(4,128)S(1)}, f32[32,4,4]{2,1,0:T(4,128)}, f32[32,4,4]{2,1,0:T(4,128)}, f32[32,4,4]{2,1,0:T(4,128)}) fusion(f32[32,4,4]{2,1,0:T(4,128)} %collective-permute-done.2, pred[]{:T(512)S(6)} %and.15, pred[]{:T(512)S(6)} %and.18, pred[]{:T(512)S(6)} %and.17, pred[]{:T(512)S(6)} %and.16), kind=kLoop, calls=%fused_computation.13 | loop fusion | flops 2048 | bytes 10244 | tf_op jit(solution)/shard_map/jit(_where)/select_n | solution.py:82
  9.8 1.6 %collective-permute-done.1 = f32[32,64,4]{1,0,2:T(8,128)S(1)} collective-permute-done((f32[32,64,4]{1,0,2:T(8,128)S(1)}, f32[32,64,4]{1,0,2:T(8,128)S(1)}, u32[]{:S(2)}, u32[]{:S(2)}) %collective-permute-start.1) | collective-permute-done | bytes 32800 | tf_op jit(solution)/shard_map/ppermute | solution.py:62
  11.5 0.4 copy.33
  11.9 1.4 %copy.34 = f32[32,64,4]{2,1,0:T(8,128)} copy(f32[32,64,4]{1,0,2:T(8,128)S(1)} %get-tuple-element.28) | data formatting | bytes 65536 | tf_op jit(solution)/shard_map/jit(_where)/select_n | solution.py:82
  13.3 1.7 %maximum_maximum_fusion.cband_hbm = f32[32,72,128]{2,1,0:T(8,128)S(1)} fusion(f32[32,4,4]{2,1,0:T(4,128)} %get-tuple-element.30, f32[32,4,4]{2,1,0:T(4,128)} %get-tuple-element.31, f32[32,64,4]{2,1,0:T(8,128)} %copy.34, f32[32,4,4]{2,1,0:T(4,128)} %get-tuple-element.32, f32[32,4,4]{2,1,0:T(4,128)S(1)} %get-tuple-element.29, f32[32,64,4]{2,1,0:T(8,128)S(1)} %copy.33, ...), kind=kLoop, calls=%fused_computation | loop fusion | flops 1769472 | bytes 1253888 | tf_op jit(solution)/shard_map/concatenate | solution.py:281
  15.0 0.0 copy-start.2
  15.0 0.0 copy-start.3
  15.1 0.0 copy-start.4
  15.1 0.0 copy-start.5
  15.1 0.9 %broadcast_select_fusion.7 = (f32[32,4,128]{2,1,0:T(4,128)S(1)}, f32[32,4,128]{2,1,0:T(4,128)S(1)}) fusion(f32[32,4,128]{2,1,0:T(4,128)} %collective-permute-done, pred[]{:T(512)S(6)} %not.4, pred[]{:T(512)S(6)} %eq.12), kind=kLoop, calls=%fused_computation.17 | loop fusion | flops 32768 | bytes 196610 | tf_op jit(solution)/shard_map/jit(_where)/select_n | solution.py:82
  16.0 1.3 %collective-permute-start.4 = (f32[4,72,256]{2,1,0:T(8,128)S(1)}, f32[4,72,256]{2,1,0:T(8,128)S(1)}, u32[]{:S(2)}, u32[]{:S(2)}) collective-permute-start(f32[4,72,256]{2,1,0:T(8,128)S(1)} %pad_maximum_fusion.1), channel_id=1, source_target_pairs={{1,0},{2,1},{3,2},{4,3},{5,4},{6,5},{7,6},{9,8},{10,9},{11,10},{12... | collective-permute-start | bytes 884744 | tf_op jit(solution)/shard_map/ppermute | solution.py:290
  17.3 0.7 %pad_maximum_fusion = f32[4,72,256]{2,1,0:T(8,128)} fusion(f32[4,72,128]{2,1,0:T(8,128)S(1)} %get-tuple-element.14, f32[4,8,128]{2,1,0:T(8,128)S(1)} %get-tuple-element.26, f32[4,64,128]{2,1,0:T(8,128)S(1)} %get-tuple-element.16), kind=kLoop, calls=%fused_computation.1 | loop fusion | flops 147456 | bytes 589824 | tf_op jit(solution)/shard_map/concatenate | solution.py:284
  18.1 4.6 %collective-permute-start.3 = (f32[4,72,256]{2,1,0:T(8,128)}, f32[4,72,256]{2,1,0:T(8,128)S(1)}, u32[]{:S(2)}, u32[]{:S(2)}) collective-permute-start(f32[4,72,256]{2,1,0:T(8,128)} %pad_maximum_fusion), channel_id=1, source_target_pairs={{0,1},{1,2},{2,3},{3,4},{4,5},{5,6},{6,7},{8,9},{9,10},{10,11},{11... | collective-permute-start | bytes 884744 | tf_op jit(solution)/shard_map/ppermute | solution.py:290
  22.7 0.1 reshape.210
  22.7 0.1 stack.27.lim_ref
  22.8 0.1 pad_maximum_fusion.4.prm_ref
  23.0 21.6 %shard_map.55 = (f32[3,4,72,256]{3,2,1,0:T(8,128)S(1)}, f32[5,64,128]{2,1,0:T(8,128)S(1)}) custom-call(s32[6]{0:T(128)S(1)} %stack.27.lim_ref, f32[24]{0:T(128)S(1)} %pad_maximum_fusion.4.prm_ref, f32[32,64,128]{2,1,0:T(8,128)S(1)} %copy-done, f32[32,8,128]{2,1,0:T(8,128)S(1)} %pad_maximum_fusion.2.rband_hbm, f32[32,72,128]{2,1,0:T(8,128)S(1)} %maximum_maximum_fusion.cband_hbm), custom_call_target="tpu_custom_call" | custom-call | flops 100270080 | bytes 2949120 | tf_op jit(solution)/shard_map/pallas_call | solution.py:237
  44.6 8.3 %shard_map.56 = f32[4,64,128]{2,1,0:T(8,128)S(1)} custom-call(s32[6]{0:T(128)S(1)} %stack.27.lim_ref, f32[24]{0:T(128)S(1)} %pad_maximum_fusion.4.prm_ref, f32[32,64,128]{2,1,0:T(8,128)S(1)} %copy-done, f32[32,8,128]{2,1,0:T(8,128)S(1)} %pad_maximum_fusion.2.rband_hbm, f32[32,72,128]{2,1,0:T(8,128)S(1)} %maximum_maximum_fusion.cband_hbm, ...), custom_call_target="tpu_custom_call" | custom-call | flops 33423360 | bytes 737280 | tf_op jit(solution)/shard_map/pallas_call | solution.py:253
  52.9 12.8 %all_to_all.5 = f32[4,8,8,128]{3,2,0,1:T(8,128)S(1)} all-to-all(f32[4,8,8,128]{3,2,0,1:T(8,128)S(1)} %copy.35), channel_id=1, replica_groups=mesh['gx'=2,'gy'=2,'gz'=8] {'gz'}, dimensions={1} | all-to-all | bytes 262144 | tf_op jit(solution)/shard_map/all_to_all | solution.py:313
  65.8 0.6 pad_maximum_fusion.3
  (22 shorter events, 0.2 us)
Async XLA Ops:
  1.0 14.1 %collective-permute-start = (f32[32,4,128]{2,1,0:T(4,128)S(1)}, f32[32,4,128]{2,1,0:T(4,128)}, u32[]{:S(2)}, u32[]{:S(2)}) collective-permute-start(f32[32,4,128]{2,1,0:T(4,128)S(1)} %slice_select_fusion.1), channel_id=1, source_target_pairs={{0,16},{16,0},{1,17},{17,1},{2,18},{18,2},{3,19},{19,3},{4,20},{20... | collective-permute-start | bytes 196616 | tf_op jit(solution)/shard_map/ppermute | solution.py:62
  1.7 6.6 %collective-permute-start.2 = (f32[32,4,4]{2,1,0:T(4,128)S(1)}, f32[32,4,4]{2,1,0:T(4,128)}, u32[]{:S(2)}, u32[]{:S(2)}) collective-permute-start(f32[32,4,4]{2,1,0:T(4,128)S(1)} %slice_select_fusion), channel_id=1, source_target_pairs={{0,24},{8,16},{16,8},{24,0},{1,25},{9,17},{17,9},{25,1},{2,26},{10... | collective-permute-start | bytes 6152 | tf_op jit(solution)/shard_map/ppermute | solution.py:62
  6.3 1.2 %copy-start = (f32[32,64,128]{2,1,0:T(8,128)S(1)}, f32[32,64,128]{2,1,0:T(8,128)}, u32[]{:S(2)}) copy-start(f32[32,64,128]{2,1,0:T(8,128)} %x_hbm.3) | copy-start | bytes 3145732
  7.1 4.3 %collective-permute-start.1 = (f32[32,64,4]{1,0,2:T(8,128)S(1)}, f32[32,64,4]{1,0,2:T(8,128)S(1)}, u32[]{:S(2)}, u32[]{:S(2)}) collective-permute-start(f32[32,64,4]{1,0,2:T(8,128)S(1)} %broadcast_select_fusion.8), channel_id=1, source_target_pairs={{0,8},{8,0},{1,9},{9,1},{2,10},{10,2},{3,11},{11,3},{4,12},{12,4},... | collective-permute-start | bytes 98312 | tf_op jit(solution)/shard_map/ppermute | solution.py:62
  13.3 2.7 %copy-start.1 = (f32[4,64,128]{2,1,0:T(8,128)S(1)}, f32[4,64,128]{2,1,0:T(8,128)}, u32[]{:S(2)}) copy-start(f32[4,64,128]{2,1,0:T(8,128)} %get-tuple-element.15) | copy-start | bytes 393220
  15.0 7.6 %copy-start.2 = (f32[3,4]{1,0:T(4,128)S(1)}, f32[3,4]{1,0:T(4,128)}, u32[]{:S(2)}) copy-start(f32[3,4]{1,0:T(4,128)} %param.9) | copy-start | bytes 148
  15.0 7.8 %copy-start.3 = (f32[4]{0:T(128)S(1)}, f32[4]{0:T(128)}, u32[]{:S(2)}) copy-start(f32[4]{0:T(128)} %param.8) | copy-start | bytes 52
  15.1 7.8 %copy-start.4 = (f32[4]{0:T(128)S(1)}, f32[4]{0:T(128)}, u32[]{:S(2)}) copy-start(f32[4]{0:T(128)} %param.7) | copy-start | bytes 52
  15.1 7.8 %copy-start.5 = (f32[4]{0:T(128)S(1)}, f32[4]{0:T(128)}, u32[]{:S(2)}) copy-start(f32[4]{0:T(128)} %param.6) | copy-start | bytes 52
  16.0 28.5 %collective-permute-start.4 = (f32[4,72,256]{2,1,0:T(8,128)S(1)}, f32[4,72,256]{2,1,0:T(8,128)S(1)}, u32[]{:S(2)}, u32[]{:S(2)}) collective-permute-start(f32[4,72,256]{2,1,0:T(8,128)S(1)} %pad_maximum_fusion.1), channel_id=1, source_target_pairs={{1,0},{2,1},{3,2},{4,3},{5,4},{6,5},{7,6},{9,8},{10,9},{11,10},{12... | collective-permute-start | bytes 884744 | tf_op jit(solution)/shard_map/ppermute | solution.py:290
  18.1 26.5 %collective-permute-start.3 = (f32[4,72,256]{2,1,0:T(8,128)}, f32[4,72,256]{2,1,0:T(8,128)S(1)}, u32[]{:S(2)}, u32[]{:S(2)}) collective-permute-start(f32[4,72,256]{2,1,0:T(8,128)} %pad_maximum_fusion), channel_id=1, source_target_pairs={{0,1},{1,2},{2,3},{3,4},{4,5},{5,6},{6,7},{8,9},{9,10},{10,11},{11... | collective-permute-start | bytes 884744 | tf_op jit(solution)/shard_map/ppermute | solution.py:290

commit v9 on v8

--- a/solution.py
+++ b/solution.py
@@ -7,6 +7,7 @@
 from jax.experimental import pallas as pl
 from jax.experimental.pallas import tpu as pltpu
 from jax.sharding import PartitionSpec as P
+
 
 STEPS = 4
 MATERIALS = 4
@@ -234,7 +235,7 @@
     params = pltpu.CompilerParams(vmem_limit_bytes=48 * 1024 * 1024)
     planes = [pltpu.VMEM((depth, rows, lanes), jnp.float32)] * 2 + [pltpu.VMEM((rows, lanes), jnp.float32)]
     inner_frac = (d_in - 2 * STEPS) / d_in
-    ex, part = pl.pallas_call(
+    inner_call = pl.pallas_call(
         functools.partial(inner_kernel, h=h),
         out_shape=(
             jax.ShapeDtypeStruct((STEPS - 1, 4, rows, lanes), jnp.float32),
@@ -249,8 +250,8 @@
             transcendentals=int(inner_frac * d_in * r_in * l_in * (MATERIALS + 1)),
             bytes_accessed=int(cells * 4),
         ),
-    )(lim, prm, x, rband, cband)
-    return pl.pallas_call(
+    )
+    outer_call = pl.pallas_call(
         functools.partial(outer_kernel, h=h),
         out_shape=jax.ShapeDtypeStruct((CHANNELS + 1, r_in, l_in), jnp.float32),
         in_specs=[smem, smem] + [anyspace] * 6 + [vmem],
@@ -266,30 +267,34 @@
             transcendentals=int((1 - inner_frac) * d_in * r_in * l_in * (MATERIALS + 1)),
             bytes_accessed=int(cells * 4 // 4),
         ),
-    )(lim, prm, x, rband, cband, zlo, zhi, ex, part)
-
-
-def shards(phase_field, centres, widths, densities, colours):
+    )
+    ex, part = inner_call(lim, prm, x, rband, cband)
+    return outer_call(lim, prm, x, rband, cband, zlo, zhi, ex, part)
+
+
+def shards_body(phase_field, centres, widths, densities, colours):
     depth_cells, row_cells, col_cells = phase_field.shape
     groups = lax.axis_size("gz")
     h = 1.0 / (depth_cells * groups)
-    plane = halo_stage(phase_field, ((1, "gx"), (2, "gy")), STEPS)
-    rband = jnp.concatenate([plane("hi", "mid"), plane("lo", "mid")], axis=1)
-    right = jnp.concatenate([plane("mid", "hi"), plane("hi", "hi"), plane("lo", "hi")], axis=1)
-    left = jnp.concatenate([plane("mid", "lo"), plane("hi", "lo"), plane("lo", "lo")], axis=1)
-    fill = jnp.zeros(right.shape[:2] + (LANES - col_cells - 2 * STEPS,), jnp.float32)
-    cband = jnp.concatenate([right, fill, left], axis=2)
-    def face(lo, hi):
-        core = jnp.concatenate([phase_field[lo:hi], rband[lo:hi]], axis=1)
-        return jnp.concatenate([core, cband[lo:hi]], axis=2)
-
-    lo_face, hi_face = face(0, STEPS), face(depth_cells - STEPS, depth_cells)
-    zlo = jnp.zeros_like(lo_face)
-    zhi = jnp.zeros_like(hi_face)
-    for pairs, send_hi, land_lo in axis_moves("gz"):
-        got = lax.ppermute(pick(send_hi, hi_face, lo_face), "gz", pairs)
-        zlo = zlo + pick(land_lo, got, jnp.zeros_like(got))
-        zhi = zhi + pick(land_lo, jnp.zeros_like(got), got)
+
+    def bands(x):
+        plane = halo_stage(x, ((1, "gx"), (2, "gy")), STEPS)
+        rb = jnp.concatenate([plane("hi", "mid"), plane("lo", "mid")], axis=1)
+        right = jnp.concatenate([plane("mid", "hi"), plane("hi", "hi"), plane("lo", "hi")], axis=1)
+        left = jnp.concatenate([plane("mid", "lo"), plane("hi", "lo"), plane("lo", "lo")], axis=1)
+        fill = jnp.zeros(right.shape[:2] + (LANES - col_cells - 2 * STEPS,), jnp.float32)
+        return rb, jnp.concatenate([right, fill, left], axis=2)
+
+    rband, cband = bands(phase_field)
+    zcore = halo_stage(phase_field, ((0, "gz"),), STEPS)
+    zlo_c, zhi_c = zcore("lo"), zcore("hi")
+    rband_z, cband_z = bands(jnp.concatenate([zlo_c, zhi_c], axis=0))
+
+    def face(core, rb, cb):
+        return jnp.concatenate([jnp.concatenate([core, rb], axis=1), cb], axis=2)
+
+    zlo = face(zlo_c, rband_z[:STEPS], cband_z[:STEPS])
+    zhi = face(zhi_c, rband_z[STEPS:], cband_z[STEPS:])
 
     z_lo = STEPS - lax.axis_index("gz") * depth_cells
     r_lo = -lax.axis_index("gx") * row_cells
@@ -323,5 +328,5 @@
 def solution(mesh):
     placed = (P("gz", "gx", "gy"), P(), P(), P(), P())
     return jax.shard_map(
-        shards, mesh=mesh, in_specs=placed, out_specs=P(None, ("gx", "gz"), "gy"), check_vma=False
+        shards_body, mesh=mesh, in_specs=placed, out_specs=P(None, ("gx", "gz"), "gy"), check_vma=False
     )

time: 66.8 us -> 73.6 us (1.10)
  waiting for transfers between devices: 1.62 us -> 7.7 us
  blocking collectives: 12.8 us -> 14.1 us
  starting transfers between devices: 9.13 us -> 10.4 us
  local copies, waits for them, and re-layouts: 5.9 us -> 4.94 us
  other arithmetic: 6.8 us -> 5.94 us
    ppermute x3 -> x8, starting transfers between devices: 3.28 us -> 10.4 us  [halo_stage(): got = lax.ppermute(piece, tuple((a for a, _, _ in used)), pairs)]
    ppermute x3 -> x8, waiting for transfers between devices: 1.62 us -> 7.7 us  [halo_stage(): got = lax.ppermute(piece, tuple((a for a, _, _ in used)), pairs)]
    ppermute x2 -> x0, starting transfers between devices: 5.84 us -> none  [shards(): got = lax.ppermute(pick(send_hi, hi_face, lo_face), 'gz', pairs)]
    all_to_all x1, blocking collectives: 12.8 us -> 14.1 us  [shards_body(): got = lax.all_to_all(parts, 'gz', 1, 1, tiled=True)]
    select_n x2, local copies, waits for them, and re-layouts: 1.8 us -> 0.8 us  [halo_stage(): val = got if cond is True else jnp.where(cond, got, 0.0)]
    concatenate x7, other arithmetic: 3.24 us -> 2.27 us  [the longest x2 1.5 us: bands(): return (rb, jnp.concatenate([right, fill, left], axis=2))]
    select_n x3 -> x6, other arithmetic: 1.1 us -> 1.94 us  [pick(): return jnp.where(cond, a, b)]
    slice x1 -> x2, local copies, waits for them, and re-layouts: 2 us -> 2.73 us  [halo_stage(): lo = lax.slice_in_dim(piece, 0, width, axis=d)]
  transfers between devices with their start and end apart: 5 -> 8, of which waited for: 1 -> 2; matrix products, arithmetic and copies ran while one was open for 15% -> 12% of each run, Pallas kernels for 32% -> 29%
where the time goes in v9:
time: 73.6 us; the launch traced here: 73.3 us
  Pallas kernels  29.9 us (41%)
  blocking collectives  14.1 us (19%)
  starting transfers between devices  10.4 us (14%)
  waiting for transfers between devices  7.7 us (10%)
  other arithmetic  5.94 us (8%)
  local copies, waits for them, and re-layouts  4.94 us (7%)
    pallas_call x1, Pallas kernels, render_block(): ex, part = inner_call(lim, prm, x, rband, cband)  21.6 us
    all_to_all x1, blocking collectives, shards_body(): got = lax.all_to_all(parts, 'gz', 1, 1, tiled=True)  14.1 us
    ppermute x8, starting transfers between devices, halo_stage(): got = lax.ppermute(piece, tuple((a for a, _, _ in used)), pairs)  10.4 us
    pallas_call x1, Pallas kernels, render_block(): return outer_call(lim, prm, x, rband, cband, zlo, zhi, ex, part)  8.32 us
    ppermute x8, waiting for transfers between devices, halo_stage(): got = lax.ppermute(piece, tuple((a for a, _, _ in used)), pairs)  7.7 us
    slice x2, local copies, waits for them, and re-layouts, halo_stage(): lo = lax.slice_in_dim(piece, 0, width, axis=d)  2.73 us
    select_n x6, other arithmetic, pick(): return jnp.where(cond, a, b)  1.94 us
    select_n x6, other arithmetic, halo_stage(): val = got if cond is True else jnp.where(cond, got, 0.0)  1.69 us
  transfers between devices with their start and end apart: 8, of which 2 were waited for; matrix products, arithmetic and copies ran while one was open for 12% of the time, Pallas kernels for 29%

profile of v9, /device:TPU:0, one launch (start us, length us, event | category | flops | bytes accessed | tf_op | source)
XLA Modules:
  0.0 73.3 jit_solution(802729956487754839)
XLA Ops:
  0.0 1.0 %slice_select_fusion.2 = f32[32,4,128]{2,1,0:T(4,128)S(1)} fusion(f32[32,64,128]{2,1,0:T(8,128)} %x_hbm.3, pred[]{:T(512)S(6)} %eq.17), kind=kLoop, calls=%fused_computation.11 | loop fusion | flops 16384 | bytes 196609 | tf_op jit(solution)/shard_map/jit(_where)/select_n | solution.py:25
  1.0 0.6 collective-permute-start
  1.6 0.7 slice_select_fusion.1
  2.3 2.6 %collective-permute-start.2 = (f32[32,4,4]{2,1,0:T(4,128)}, f32[32,4,4]{2,1,0:T(4,128)S(1)}, u32[]{:S(2)}, u32[]{:S(2)}) collective-permute-start(f32[32,4,4]{2,1,0:T(4,128)} %slice_select_fusion.1), channel_id=1, source_target_pairs={{0,24},{8,16},{16,8},{24,0},{1,25},{9,17},{17,9},{25,1},{2,26},{10... | collective-permute-start | bytes 6152 | tf_op jit(solution)/shard_map/ppermute | solution.py:63
  4.9 2.0 %fusion.22 = (f32[32,64,4]{2,1,0:T(8,128)S(1)}, f32[32,64,4]{2,1,0:T(8,128)S(1)}) fusion(f32[32,64,128]{2,1,0:T(8,128)} %x_hbm.3), kind=kLoop, calls=%fused_computation.77 | loop fusion | bytes 131072 | tf_op jit(solution)/shard_map/slice | solution.py:53
  6.9 0.4 copy.44
  7.3 0.4 copy.45
  7.7 0.1 collective-permute-start.1
  7.8 0.3 copy-done
  8.1 0.7 fusion.21
  8.8 3.6 %collective-permute-start.3 = (f32[4,64,128]{2,1,0:T(8,128)}, f32[4,64,128]{2,1,0:T(8,128)S(1)}, u32[]{:S(2)}, u32[]{:S(2)}) collective-permute-start(f32[4,64,128]{2,1,0:T(8,128)} %get-tuple-element.14), channel_id=1, source_target_pairs={{0,1},{1,2},{2,3},{3,4},{4,5},{5,6},{6,7},{8,9},{9,10},{10,11},{11... | collective-permute-start | bytes 393224 | tf_op jit(solution)/shard_map/ppermute | solution.py:63
  12.5 1.3 %collective-permute-start.4 = (f32[4,64,128]{2,1,0:T(8,128)}, f32[4,64,128]{2,1,0:T(8,128)S(1)}, u32[]{:S(2)}, u32[]{:S(2)}) collective-permute-start(f32[4,64,128]{2,1,0:T(8,128)} %get-tuple-element.13), channel_id=1, source_target_pairs={{1,0},{2,1},{3,2},{4,3},{5,4},{6,5},{7,6},{9,8},{10,9},{11,10},{12... | collective-permute-start | bytes 393224 | tf_op jit(solution)/shard_map/ppermute | solution.py:63
  13.8 0.1 reshape.210
  13.9 0.1 pad_maximum_fusion.4.prm_ref
  13.9 0.1 pad.20.clone
  14.0 0.1 stack.27.lim_ref
  14.1 0.7 %broadcast_select_fusion.5 = (f32[32,4,4]{2,1,0:T(4,128)}, f32[32,4,4]{2,1,0:T(4,128)}, f32[32,4,4]{2,1,0:T(4,128)}, f32[32,4,4]{2,1,0:T(4,128)}) fusion(f32[32,4,4]{2,1,0:T(4,128)S(1)} %collective-permute-done.2, pred[]{:T(512)S(6)} %and.19, pred[]{:T(512)S(6)} %and.22, pred[]{:T(512)S(6)} %and.21, pred[]{:T(512)S(6)} %and.20), kind=kLoop, calls=%fused_computation.17 | loop fusion | flops 2048 | bytes 10244 | tf_op jit(solution)/shard_map/jit(_where)/select_n | solution.py:83
  14.9 0.4 copy.42
  15.3 0.4 copy.41
  15.7 1.3 %maximum_maximum_fusion.cband_hbm = f32[32,72,128]{2,1,0:T(8,128)S(1)} fusion(f32[32,4,4]{2,1,0:T(4,128)} %get-tuple-element.30, f32[32,4,4]{2,1,0:T(4,128)} %get-tuple-element.31, f32[32,64,4]{2,1,0:T(8,128)S(1)} %copy.42, f32[32,4,4]{2,1,0:T(4,128)} %get-tuple-element.32, f32[32,4,4]{2,1,0:T(4,128)} %get-tuple-element.29, f32[32,64,4]{2,1,0:T(8,128)S(1)} %copy.41, ...), kind=kLoop, calls=%fused_computation | loop fusion | flops 1769472 | bytes 1253888 | tf_op jit(solution)/shard_map/concatenate | solution.py:286
  17.0 0.9 %broadcast_select_fusion.9 = (f32[32,4,128]{2,1,0:T(4,128)S(1)}, f32[32,4,128]{2,1,0:T(4,128)S(1)}) fusion(f32[32,4,128]{2,1,0:T(4,128)} %collective-permute-done, pred[]{:T(512)S(6)} %not.4, pred[]{:T(512)S(6)} %eq.16), kind=kLoop, calls=%fused_computation.21 | loop fusion | flops 32768 | bytes 196610 | tf_op jit(solution)/shard_map/jit(_where)/select_n | solution.py:83
  18.0 21.6 %shard_map.55 = (f32[3,4,72,256]{3,2,1,0:T(8,128)S(1)}, f32[5,64,128]{2,1,0:T(8,128)S(1)}) custom-call(s32[6]{0:T(128)S(1)} %stack.27.lim_ref, f32[24]{0:T(128)S(1)} %pad_maximum_fusion.4.prm_ref, f32[32,64,128]{2,1,0:T(8,128)S(1)} %copy-done, f32[32,8,128]{2,1,0:T(8,128)S(1)} %pad_maximum_fusion.2.rband_hbm, f32[32,72,128]{2,1,0:T(8,128)S(1)} %maximum_maximum_fusion.cband_hbm), custom_call_target="tpu_custom_call" | custom-call | flops 100270080 | bytes 2949120 | tf_op jit(solution)/shard_map/pallas_call | solution.py:271
  39.7 0.1 slice_select_fusion.3
  39.8 1.6 %collective-permute-start.7 = (f32[8,4,4]{2,1,0:T(4,128)S(1)}, f32[8,4,4]{2,1,0:T(4,128)S(1)}, u32[]{:S(2)}, u32[]{:S(2)}) collective-permute-start(f32[8,4,4]{2,1,0:T(4,128)S(1)} %slice_select_fusion.3), channel_id=1, source_target_pairs={{0,24},{8,16},{16,8},{24,0},{1,25},{9,17},{17,9},{25,1},{2,26},{10... | collective-permute-start | bytes 1544 | tf_op jit(solution)/shard_map/ppermute | solution.py:63
  41.4 0.1 slice_select_fusion
  41.5 0.6 collective-permute-start.6
  42.1 0.8 %collective-permute-done.7 = f32[8,4,4]{2,1,0:T(4,128)S(1)} collective-permute-done((f32[8,4,4]{2,1,0:T(4,128)S(1)}, f32[8,4,4]{2,1,0:T(4,128)S(1)}, u32[]{:S(2)}, u32[]{:S(2)}) %collective-permute-start.7) | collective-permute-done | bytes 544 | tf_op jit(solution)/shard_map/ppermute | solution.py:63
  43.0 6.8 %collective-permute-done.6 = f32[8,64,4]{2,1,0:T(8,128)S(1)} collective-permute-done((f32[8,64,4]{2,1,0:T(8,128)S(1)}, f32[8,64,4]{2,1,0:T(8,128)S(1)}, u32[]{:S(2)}, u32[]{:S(2)}) %collective-permute-start.6) | collective-permute-done | bytes 8224 | tf_op jit(solution)/shard_map/ppermute | solution.py:63
  49.9 0.2 maximum_maximum_fusion.1
  50.1 8.3 %shard_map.56 = f32[4,64,128]{2,1,0:T(8,128)S(1)} custom-call(s32[6]{0:T(128)S(1)} %stack.27.lim_ref, f32[24]{0:T(128)S(1)} %pad_maximum_fusion.4.prm_ref, f32[32,64,128]{2,1,0:T(8,128)S(1)} %copy-done, f32[32,8,128]{2,1,0:T(8,128)S(1)} %pad_maximum_fusion.2.rband_hbm, f32[32,72,128]{2,1,0:T(8,128)S(1)} %maximum_maximum_fusion.cband_hbm, ...), custom_call_target="tpu_custom_call" | custom-call | flops 33423360 | bytes 737280 | tf_op jit(solution)/shard_map/pallas_call | solution.py:272
  58.5 14.1 %all_to_all.5 = f32[4,8,8,128]{3,2,0,1:T(8,128)S(1)} all-to-all(f32[4,8,8,128]{3,2,0,1:T(8,128)S(1)} %copy.43), channel_id=1, replica_groups=mesh['gx'=2,'gy'=2,'gz'=8] {'gz'}, dimensions={1} | all-to-all | bytes 262144 | tf_op jit(solution)/shard_map/all_to_all | solution.py:318
  72.6 0.6 pad_maximum_fusion.3
  (34 shorter events, 0.4 us)
Async XLA Ops:
  1.0 16.0 %collective-permute-start = (f32[32,4,128]{2,1,0:T(4,128)S(1)}, f32[32,4,128]{2,1,0:T(4,128)}, u32[]{:S(2)}, u32[]{:S(2)}) collective-permute-start(f32[32,4,128]{2,1,0:T(4,128)S(1)} %slice_select_fusion.2), channel_id=1, source_target_pairs={{0,16},{16,0},{1,17},{17,1},{2,18},{18,2},{3,19},{19,3},{4,20},{20... | collective-permute-start | bytes 196616 | tf_op jit(solution)/shard_map/ppermute | solution.py:63
  2.3 11.8 %collective-permute-start.2 = (f32[32,4,4]{2,1,0:T(4,128)}, f32[32,4,4]{2,1,0:T(4,128)S(1)}, u32[]{:S(2)}, u32[]{:S(2)}) collective-permute-start(f32[32,4,4]{2,1,0:T(4,128)} %slice_select_fusion.1), channel_id=1, source_target_pairs={{0,24},{8,16},{16,8},{24,0},{1,25},{9,17},{17,9},{25,1},{2,26},{10... | collective-permute-start | bytes 6152 | tf_op jit(solution)/shard_map/ppermute | solution.py:63
  6.9 1.2 %copy-start = (f32[32,64,128]{2,1,0:T(8,128)S(1)}, f32[32,64,128]{2,1,0:T(8,128)}, u32[]{:S(2)}) copy-start(f32[32,64,128]{2,1,0:T(8,128)} %x_hbm.3) | copy-start | bytes 3145732
  7.3 6.5 %copy-start.1 = (f32[3,4]{1,0:T(4,128)S(1)}, f32[3,4]{1,0:T(4,128)}, u32[]{:S(2)}) copy-start(f32[3,4]{1,0:T(4,128)} %param.9) | copy-start | bytes 148
  7.3 6.6 %copy-start.2 = (f32[4]{0:T(128)S(1)}, f32[4]{0:T(128)}, u32[]{:S(2)}) copy-start(f32[4]{0:T(128)} %param.8) | copy-start | bytes 52
  7.3 6.6 %copy-start.3 = (f32[4]{0:T(128)S(1)}, f32[4]{0:T(128)}, u32[]{:S(2)}) copy-start(f32[4]{0:T(128)} %param.7) | copy-start | bytes 52
  7.3 6.6 %copy-start.4 = (f32[4]{0:T(128)S(1)}, f32[4]{0:T(128)}, u32[]{:S(2)}) copy-start(f32[4]{0:T(128)} %param.6) | copy-start | bytes 52
  7.7 7.1 %collective-permute-start.1 = (f32[32,64,4]{1,0,2:T(8,128)S(1)}, f32[32,64,4]{1,0,2:T(8,128)S(1)}, u32[]{:S(2)}, u32[]{:S(2)}) collective-permute-start(f32[32,64,4]{1,0,2:T(8,128)S(1)} %broadcast_select_fusion.10), channel_id=1, source_target_pairs={{0,8},{8,0},{1,9},{9,1},{2,10},{10,2},{3,11},{11,3},{4,12},{12,4},... | collective-permute-start | bytes 98312 | tf_op jit(solution)/shard_map/ppermute | solution.py:63
  8.8 30.7 %collective-permute-start.3 = (f32[4,64,128]{2,1,0:T(8,128)}, f32[4,64,128]{2,1,0:T(8,128)S(1)}, u32[]{:S(2)}, u32[]{:S(2)}) collective-permute-start(f32[4,64,128]{2,1,0:T(8,128)} %get-tuple-element.14), channel_id=1, source_target_pairs={{0,1},{1,2},{2,3},{3,4},{4,5},{5,6},{6,7},{8,9},{9,10},{10,11},{11... | collective-permute-start | bytes 393224 | tf_op jit(solution)/shard_map/ppermute | solution.py:63
  12.5 27.1 %collective-permute-start.4 = (f32[4,64,128]{2,1,0:T(8,128)}, f32[4,64,128]{2,1,0:T(8,128)S(1)}, u32[]{:S(2)}, u32[]{:S(2)}) collective-permute-start(f32[4,64,128]{2,1,0:T(8,128)} %get-tuple-element.13), channel_id=1, source_target_pairs={{1,0},{2,1},{3,2},{4,3},{5,4},{6,5},{7,6},{9,8},{10,9},{11,10},{12... | collective-permute-start | bytes 393224 | tf_op jit(solution)/shard_map/ppermute | solution.py:63
  39.6 10.4 %collective-permute-start.5 = (f32[8,4,128]{2,1,0:T(4,128)S(1)}, f32[8,4,128]{2,1,0:T(4,128)S(1)}, u32[]{:S(2)}, u32[]{:S(2)}) collective-permute-start(f32[8,4,128]{2,1,0:T(4,128)S(1)} %slice_select_fusion.4), channel_id=1, source_target_pairs={{0,16},{16,0},{1,17},{17,1},{2,18},{18,2},{3,19},{19,3},{4,20},{20... | collective-permute-start | bytes 49160 | tf_op jit(solution)/shard_map/ppermute | solution.py:63
  39.8 3.2 %collective-permute-start.7 = (f32[8,4,4]{2,1,0:T(4,128)S(1)}, f32[8,4,4]{2,1,0:T(4,128)S(1)}, u32[]{:S(2)}, u32[]{:S(2)}) collective-permute-start(f32[8,4,4]{2,1,0:T(4,128)S(1)} %slice_select_fusion.3), channel_id=1, source_target_pairs={{0,24},{8,16},{16,8},{24,0},{1,25},{9,17},{17,9},{25,1},{2,26},{10... | collective-permute-start | bytes 1544 | tf_op jit(solution)/shard_map/ppermute | solution.py:63
  41.5 8.3 %collective-permute-start.6 = (f32[8,64,4]{2,1,0:T(8,128)S(1)}, f32[8,64,4]{2,1,0:T(8,128)S(1)}, u32[]{:S(2)}, u32[]{:S(2)}) collective-permute-start(f32[8,64,4]{2,1,0:T(8,128)S(1)} %slice_select_fusion), channel_id=1, source_target_pairs={{0,8},{8,0},{1,9},{9,1},{2,10},{10,2},{3,11},{11,3},{4,12},{12,4},... | collective-permute-start | bytes 24584 | tf_op jit(solution)/shard_map/ppermute | solution.py:63

commit v10 on v7

--- a/solution.py
+++ b/solution.py
@@ -59,7 +59,12 @@
             for (_, s, _), (p, q) in zip(used, parts):
                 src, dst = src * s + p, dst * s + q
             pairs.append((src, dst))
+        narrow = piece.ndim == 3 and piece.shape[2] == width and piece.shape[1] > width
+        if narrow:
+            piece = jnp.transpose(piece, (2, 0, 1))
         got = lax.ppermute(piece, tuple(a for a, _, _ in used), pairs)
+        if narrow:
+            got = jnp.transpose(got, (1, 2, 0))
         landing = [(d, m[2]) for d, m in zip(dims, combo) if m is not None]
         for sides in itertools.product(("lo", "hi"), repeat=len(landing)):
             cond = True

time: 64.4 us -> 63.8 us (level)
  local copies, waits for them, and re-layouts: 6.2 us -> 5.28 us
    slice x3 -> x1, local copies, waits for them, and re-layouts: 1.92 us -> 0.99 us  [halo_stage(): lo = lax.slice_in_dim(piece, 0, width, axis=d)]
  transfers between devices with their start and end apart: 5 -> 5, of which waited for: 3 -> 3; matrix products, arithmetic and copies ran while one was open for 9% -> 8% of each run, Pallas kernels for 0% -> 0%
where the time goes in v10:
time: 63.8 us; the launch traced here: 63.5 us
  Pallas kernels  27.8 us (44%)
  blocking collectives  12.9 us (20%)
  starting transfers between devices  8.51 us (13%)
  waiting for transfers between devices  6.33 us (10%)
  local copies, waits for them, and re-layouts  5.28 us (8%)
  other arithmetic  2.59 us (4%)
    pallas_call x1, Pallas kernels, render_block(): pl.pallas_call(kernel, out_shape=jax.ShapeDtypeStruct((CHANNELS + 1, r_in...  27.8 us
    all_to_all x1, blocking collectives, shards(): got = lax.all_to_all(parts, 'gz', 1, 1, tiled=True)  12.9 us
    ppermute x5, starting transfers between devices, halo_stage(): got = lax.ppermute(piece, tuple((a for a, _, _ in used)), pairs)  8.51 us
    ppermute x5, waiting for transfers between devices, halo_stage(): got = lax.ppermute(piece, tuple((a for a, _, _ in used)), pairs)  6.33 us
    unnamed x4, local copies, waits for them, and re-layouts  1.95 us
  transfers between devices with their start and end apart: 5, of which 3 were waited for; matrix products, arithmetic and copies ran while one was open for 8% of the time, Pallas kernels for 0%

profile of v10, /device:TPU:0, one launch (start us, length us, event | category | flops | bytes accessed | tf_op | source)
XLA Modules:
  0.0 63.5 jit_solution(9685829695523617813)
XLA Ops:
  0.0 1.0 %fusion.19 = (f32[4,64,128]{2,1,0:T(8,128)S(1)}, f32[4,64,128]{2,1,0:T(8,128)S(1)}) fusion(f32[32,64,128]{2,1,0:T(8,128)} %x_hbm.1), kind=kLoop, calls=%fused_computation.59 | loop fusion | bytes 524288 | tf_op jit(solution)/shard_map/slice | solution.py:52
  1.0 4.9 %collective-permute-start = (f32[4,64,128]{2,1,0:T(8,128)S(1)}, f32[4,64,128]{2,1,0:T(8,128)S(1)}, u32[]{:S(2)}, u32[]{:S(2)}) collective-permute-start(f32[4,64,128]{2,1,0:T(8,128)S(1)} %get-tuple-element.10), channel_id=1, source_target_pairs={{0,1},{1,2},{2,3},{3,4},{4,5},{5,6},{6,7},{8,9},{9,10},{10,11},{11... | collective-permute-start | bytes 393224 | tf_op jit(solution)/shard_map/ppermute | solution.py:65
  5.9 1.3 %collective-permute-start.1 = (f32[4,64,128]{2,1,0:T(8,128)S(1)}, f32[4,64,128]{2,1,0:T(8,128)S(1)}, u32[]{:S(2)}, u32[]{:S(2)}) collective-permute-start(f32[4,64,128]{2,1,0:T(8,128)S(1)} %get-tuple-element.9), channel_id=1, source_target_pairs={{1,0},{2,1},{3,2},{4,3},{5,4},{6,5},{7,6},{9,8},{10,9},{11,10},{12... | collective-permute-start | bytes 393224 | tf_op jit(solution)/shard_map/ppermute | solution.py:65
  7.3 0.8 %reshape.210 = f32[12]{0:T(128)S(1)} reshape(f32[3,4]{1,0:T(4,128)} %param.9) | data formatting | bytes 96 | tf_op jit(solution)/shard_map/reshape | solution.py:241
  8.0 0.1 pad.5.clone
  8.1 0.1 stack.27.lim_ref
  8.2 0.8 %pad_maximum_fusion.2.prm_ref = f32[24]{0:T(128)S(1)} fusion(f32[12]{0:T(128)S(1)} %reshape.210, f32[4]{0:T(128)} %param.8, f32[4]{0:T(128)} %param.7, f32[4]{0:T(128)} %param.6), kind=kLoop, calls=%fused_computation.58 | loop fusion | flops 72 | bytes 192 | tf_op jit(solution)/shard_map/concatenate | solution.py:241
  8.9 0.0 collective-permute-done.zlo_hbm
  9.0 1.3 %constant_dynamic-update-slice_fusion.1 = f32[40,64,128]{2,1,0:T(8,128)S(1)} fusion(f32[40,64,128]{2,1,0:T(8,128)S(1)} %constant_dynamic-update-slice_fusion.2, f32[32,64,128]{2,1,0:T(8,128)} %x_hbm.1), kind=kLoop, calls=%fused_computation.38 | loop fusion | bytes 2097152
  10.3 2.5 %collective-permute-done.1.zhi_hbm = f32[4,64,128]{2,1,0:T(8,128)S(1)} collective-permute-done((f32[4,64,128]{2,1,0:T(8,128)S(1)}, f32[4,64,128]{2,1,0:T(8,128)S(1)}, u32[]{:S(2)}, u32[]{:S(2)}) %collective-permute-start.1) | collective-permute-done | bytes 131104 | tf_op jit(solution)/shard_map/ppermute | solution.py:65
  12.8 0.1 slice_select_fusion.1
  12.9 0.1 collective-permute-start.4
  13.0 0.4 fusion
  13.4 1.7 %collective-permute-start.2 = (f32[40,4,128]{2,1,0:T(4,128)S(1)}, f32[40,4,128]{2,1,0:T(4,128)S(1)}, u32[]{:S(2)}, u32[]{:S(2)}) collective-permute-start(f32[40,4,128]{2,1,0:T(4,128)S(1)} %slice_select_fusion.2), channel_id=1, source_target_pairs={{0,16},{16,0},{1,17},{17,1},{2,18},{18,2},{3,19},{19,3},{4,20},{20... | collective-permute-start | bytes 245768 | tf_op jit(solution)/shard_map/ppermute | solution.py:65
  15.1 0.5 copy.29
  15.5 0.6 collective-permute-start.3
  16.1 1.6 %collective-permute-done.4 = f32[40,4,4]{2,1,0:T(4,128)S(1)} collective-permute-done((f32[40,4,4]{2,1,0:T(4,128)S(1)}, f32[40,4,4]{2,1,0:T(4,128)S(1)}, u32[]{:S(2)}, u32[]{:S(2)}) %collective-permute-start.4) | collective-permute-done | bytes 2592 | tf_op jit(solution)/shard_map/ppermute | solution.py:65
  17.7 0.1 broadcast_select_fusion.3
  17.7 2.3 %collective-permute-done.3 = f32[4,40,64]{2,1,0:T(8,128)S(1)} collective-permute-done((f32[4,40,64]{2,1,0:T(8,128)S(1)}, f32[4,40,64]{2,1,0:T(8,128)S(1)}, u32[]{:S(2)}, u32[]{:S(2)}) %collective-permute-start.3) | collective-permute-done | bytes 40992 | tf_op jit(solution)/shard_map/ppermute | solution.py:65
  20.0 0.5 copy.30
  20.5 0.5 copy.31
  21.0 0.0 copy-start
  21.0 0.5 maximum_maximum_fusion.cband_hbm
  21.5 0.0 collective-permute-done.2
  21.6 0.6 copy-done
  22.2 27.8 %shard_map.55 = f32[4,64,128]{2,1,0:T(8,128)S(1)} custom-call(s32[6]{0:T(128)S(1)} %stack.27.lim_ref, f32[24]{0:T(128)S(1)} %pad_maximum_fusion.2.prm_ref, f32[32,64,128]{2,1,0:T(8,128)S(1)} %copy-done, f32[4,64,128]{2,1,0:T(8,128)S(1)} %collective-permute-done.zlo_hbm, f32[4,64,128]{2,1,0:T(8,128)S(1)} %collective-permute-done.1.zhi_hbm, ...), custom_call_target="tpu_custom_call" | custom-call | flops 133693440 | bytes 3080192 | tf_op jit(solution)/shard_map/pallas_call | solution.py:193
  50.0 12.9 %all_to_all.5 = f32[4,8,8,128]{3,2,0,1:T(8,128)S(1)} all-to-all(f32[4,8,8,128]{3,2,0,1:T(8,128)S(1)} %copy.32), channel_id=1, replica_groups=mesh['gx'=2,'gy'=2,'gz'=8] {'gz'}, dimensions={1} | all-to-all | bytes 262144 | tf_op jit(solution)/shard_map/all_to_all | solution.py:247
  62.9 0.6 pad_maximum_fusion.1
  (12 shorter events, 0.2 us)
Async XLA Ops:
  1.0 8.0 %collective-permute-start = (f32[4,64,128]{2,1,0:T(8,128)S(1)}, f32[4,64,128]{2,1,0:T(8,128)S(1)}, u32[]{:S(2)}, u32[]{:S(2)}) collective-permute-start(f32[4,64,128]{2,1,0:T(8,128)S(1)} %get-tuple-element.10), channel_id=1, source_target_pairs={{0,1},{1,2},{2,3},{3,4},{4,5},{5,6},{6,7},{8,9},{9,10},{10,11},{11... | collective-permute-start | bytes 393224 | tf_op jit(solution)/shard_map/ppermute | solution.py:65
  5.9 6.9 %collective-permute-start.1 = (f32[4,64,128]{2,1,0:T(8,128)S(1)}, f32[4,64,128]{2,1,0:T(8,128)S(1)}, u32[]{:S(2)}, u32[]{:S(2)}) collective-permute-start(f32[4,64,128]{2,1,0:T(8,128)S(1)} %get-tuple-element.9), channel_id=1, source_target_pairs={{1,0},{2,1},{3,2},{4,3},{5,4},{6,5},{7,6},{9,8},{10,9},{11,10},{12... | collective-permute-start | bytes 393224 | tf_op jit(solution)/shard_map/ppermute | solution.py:65
  12.9 4.8 %collective-permute-start.4 = (f32[40,4,4]{2,1,0:T(4,128)S(1)}, f32[40,4,4]{2,1,0:T(4,128)S(1)}, u32[]{:S(2)}, u32[]{:S(2)}) collective-permute-start(f32[40,4,4]{2,1,0:T(4,128)S(1)} %slice_select_fusion.1), channel_id=1, source_target_pairs={{0,24},{8,16},{16,8},{24,0},{1,25},{9,17},{17,9},{25,1},{2,26},{10... | collective-permute-start | bytes 7688 | tf_op jit(solution)/shard_map/ppermute | solution.py:65
  13.4 8.1 %collective-permute-start.2 = (f32[40,4,128]{2,1,0:T(4,128)S(1)}, f32[40,4,128]{2,1,0:T(4,128)S(1)}, u32[]{:S(2)}, u32[]{:S(2)}) collective-permute-start(f32[40,4,128]{2,1,0:T(4,128)S(1)} %slice_select_fusion.2), channel_id=1, source_target_pairs={{0,16},{16,0},{1,17},{17,1},{2,18},{18,2},{3,19},{19,3},{4,20},{20... | collective-permute-start | bytes 245768 | tf_op jit(solution)/shard_map/ppermute | solution.py:65
  15.5 4.5 %collective-permute-start.3 = (f32[4,40,64]{2,1,0:T(8,128)S(1)}, f32[4,40,64]{2,1,0:T(8,128)S(1)}, u32[]{:S(2)}, u32[]{:S(2)}) collective-permute-start(f32[4,40,64]{2,1,0:T(8,128)S(1)} %copy.29), channel_id=1, source_target_pairs={{0,8},{8,0},{1,9},{9,1},{2,10},{10,2},{3,11},{11,3},{4,12},{12,4},... | collective-permute-start | bytes 122888 | tf_op jit(solution)/shard_map/ppermute | solution.py:65
  21.0 1.2 %copy-start = (f32[32,64,128]{2,1,0:T(8,128)S(1)}, f32[32,64,128]{2,1,0:T(8,128)}, u32[]{:S(2)}) copy-start(f32[32,64,128]{2,1,0:T(8,128)} %x_hbm.1) | copy-start | bytes 3145732

commit v11 on v10

--- a/solution.py
+++ b/solution.py
@@ -153,7 +153,7 @@
             dst[z] = new * (m_ref[...] * zf)
             return g
 
-        lax.fori_loop(z0, z1, body, g0)
+        lax.fori_loop(z0, z1, body, g0, unroll=4)
 
     smooth(b_ref, a_ref, 0)
     smooth(a_ref, b_ref, 1)
@@ -179,7 +179,7 @@
         out_ref[CHANNELS] = run + ext
         return g
 
-    lax.fori_loop(z0, z1, final, g0)
+    lax.fori_loop(z0, z1, final, g0, unroll=2)
     for ch in range(CHANNELS):
         emit = col[ch][0] * acc_ref[0] + col[ch][1] * acc_ref[1] + col[ch][2] * acc_ref[2] + col[ch][3] * acc_ref[3]
         out_ref[ch] = h * emit

time: 63.8 us -> 53.3 us (0.84)
  Pallas kernels: 27.8 us -> 17.2 us
    pallas_call x1, Pallas kernels: 27.8 us -> 17.2 us  [render_block(): pl.pallas_call(kernel, out_shape=jax.ShapeDtypeStruct((CHANNELS + 1, r_in...]
  transfers between devices with their start and end apart: 5 -> 5, of which waited for: 3 -> 3; matrix products, arithmetic and copies ran while one was open for 8% -> 10% of each run, Pallas kernels for 0% -> 0%
where the time goes in v11:
time: 53.3 us; the launch traced here: 53 us
  Pallas kernels  17.2 us (32%)
  blocking collectives  12.9 us (24%)
  starting transfers between devices  8.51 us (16%)
  waiting for transfers between devices  6.33 us (12%)
  local copies, waits for them, and re-layouts  5.28 us (10%)
  other arithmetic  2.59 us (5%)
    pallas_call x1, Pallas kernels, render_block(): pl.pallas_call(kernel, out_shape=jax.ShapeDtypeStruct((CHANNELS + 1, r_in...  17.2 us
    all_to_all x1, blocking collectives, shards(): got = lax.all_to_all(parts, 'gz', 1, 1, tiled=True)  12.9 us
    ppermute x5, starting transfers between devices, halo_stage(): got = lax.ppermute(piece, tuple((a for a, _, _ in used)), pairs)  8.51 us
    ppermute x5, waiting for transfers between devices, halo_stage(): got = lax.ppermute(piece, tuple((a for a, _, _ in used)), pairs)  6.33 us
    unnamed x4, local copies, waits for them, and re-layouts  1.95 us
  transfers between devices with their start and end apart: 5, of which 3 were waited for; matrix products, arithmetic and copies ran while one was open for 10% of the time, Pallas kernels for 0%

profile of v11, /device:TPU:0, one launch (start us, length us, event | category | flops | bytes accessed | tf_op | source)
XLA Modules:
  0.0 53.0 jit_solution(13675660717849033519)
XLA Ops:
  0.0 1.0 %fusion.19 = (f32[4,64,128]{2,1,0:T(8,128)S(1)}, f32[4,64,128]{2,1,0:T(8,128)S(1)}) fusion(f32[32,64,128]{2,1,0:T(8,128)} %x_hbm.1), kind=kLoop, calls=%fused_computation.59 | loop fusion | bytes 524288 | tf_op jit(solution)/shard_map/slice | solution.py:52
  1.0 4.9 %collective-permute-start = (f32[4,64,128]{2,1,0:T(8,128)S(1)}, f32[4,64,128]{2,1,0:T(8,128)S(1)}, u32[]{:S(2)}, u32[]{:S(2)}) collective-permute-start(f32[4,64,128]{2,1,0:T(8,128)S(1)} %get-tuple-element.10), channel_id=1, source_target_pairs={{0,1},{1,2},{2,3},{3,4},{4,5},{5,6},{6,7},{8,9},{9,10},{10,11},{11... | collective-permute-start | bytes 393224 | tf_op jit(solution)/shard_map/ppermute | solution.py:65
  5.9 1.3 %collective-permute-start.1 = (f32[4,64,128]{2,1,0:T(8,128)S(1)}, f32[4,64,128]{2,1,0:T(8,128)S(1)}, u32[]{:S(2)}, u32[]{:S(2)}) collective-permute-start(f32[4,64,128]{2,1,0:T(8,128)S(1)} %get-tuple-element.9), channel_id=1, source_target_pairs={{1,0},{2,1},{3,2},{4,3},{5,4},{6,5},{7,6},{9,8},{10,9},{11,10},{12... | collective-permute-start | bytes 393224 | tf_op jit(solution)/shard_map/ppermute | solution.py:65
  7.3 0.8 %reshape.210 = f32[12]{0:T(128)S(1)} reshape(f32[3,4]{1,0:T(4,128)} %param.9) | data formatting | bytes 96 | tf_op jit(solution)/shard_map/reshape | solution.py:241
  8.0 0.1 pad.5.clone
  8.1 0.1 stack.27.lim_ref
  8.2 0.8 %pad_maximum_fusion.2.prm_ref = f32[24]{0:T(128)S(1)} fusion(f32[12]{0:T(128)S(1)} %reshape.210, f32[4]{0:T(128)} %param.8, f32[4]{0:T(128)} %param.7, f32[4]{0:T(128)} %param.6), kind=kLoop, calls=%fused_computation.58 | loop fusion | flops 72 | bytes 192 | tf_op jit(solution)/shard_map/concatenate | solution.py:241
  8.9 0.0 collective-permute-done.zlo_hbm
  9.0 1.3 %constant_dynamic-update-slice_fusion.1 = f32[40,64,128]{2,1,0:T(8,128)S(1)} fusion(f32[40,64,128]{2,1,0:T(8,128)S(1)} %constant_dynamic-update-slice_fusion.2, f32[32,64,128]{2,1,0:T(8,128)} %x_hbm.1), kind=kLoop, calls=%fused_computation.38 | loop fusion | bytes 2097152
  10.3 2.5 %collective-permute-done.1.zhi_hbm = f32[4,64,128]{2,1,0:T(8,128)S(1)} collective-permute-done((f32[4,64,128]{2,1,0:T(8,128)S(1)}, f32[4,64,128]{2,1,0:T(8,128)S(1)}, u32[]{:S(2)}, u32[]{:S(2)}) %collective-permute-start.1) | collective-permute-done | bytes 131104 | tf_op jit(solution)/shard_map/ppermute | solution.py:65
  12.8 0.1 slice_select_fusion.1
  12.9 0.1 collective-permute-start.4
  13.0 0.4 fusion
  13.4 1.7 %collective-permute-start.2 = (f32[40,4,128]{2,1,0:T(4,128)S(1)}, f32[40,4,128]{2,1,0:T(4,128)S(1)}, u32[]{:S(2)}, u32[]{:S(2)}) collective-permute-start(f32[40,4,128]{2,1,0:T(4,128)S(1)} %slice_select_fusion.2), channel_id=1, source_target_pairs={{0,16},{16,0},{1,17},{17,1},{2,18},{18,2},{3,19},{19,3},{4,20},{20... | collective-permute-start | bytes 245768 | tf_op jit(solution)/shard_map/ppermute | solution.py:65
  15.1 0.5 copy.29
  15.5 0.6 %collective-permute-start.3 = (f32[4,40,64]{2,1,0:T(8,128)S(1)}, f32[4,40,64]{2,1,0:T(8,128)S(1)}, u32[]{:S(2)}, u32[]{:S(2)}) collective-permute-start(f32[4,40,64]{2,1,0:T(8,128)S(1)} %copy.29), channel_id=1, source_target_pairs={{0,8},{8,0},{1,9},{9,1},{2,10},{10,2},{3,11},{11,3},{4,12},{12,4},... | collective-permute-start | bytes 122888 | tf_op jit(solution)/shard_map/ppermute | solution.py:65
  16.1 1.6 %collective-permute-done.4 = f32[40,4,4]{2,1,0:T(4,128)S(1)} collective-permute-done((f32[40,4,4]{2,1,0:T(4,128)S(1)}, f32[40,4,4]{2,1,0:T(4,128)S(1)}, u32[]{:S(2)}, u32[]{:S(2)}) %collective-permute-start.4) | collective-permute-done | bytes 2592 | tf_op jit(solution)/shard_map/ppermute | solution.py:65
  17.7 0.1 broadcast_select_fusion.3
  17.7 2.3 %collective-permute-done.3 = f32[4,40,64]{2,1,0:T(8,128)S(1)} collective-permute-done((f32[4,40,64]{2,1,0:T(8,128)S(1)}, f32[4,40,64]{2,1,0:T(8,128)S(1)}, u32[]{:S(2)}, u32[]{:S(2)}) %collective-permute-start.3) | collective-permute-done | bytes 40992 | tf_op jit(solution)/shard_map/ppermute | solution.py:65
  20.0 0.5 copy.30
  20.5 0.5 copy.31
  21.0 0.0 copy-start
  21.0 0.5 maximum_maximum_fusion.cband_hbm
  21.5 0.0 collective-permute-done.2
  21.6 0.6 %copy-done = f32[32,64,128]{2,1,0:T(8,128)S(1)} copy-done((f32[32,64,128]{2,1,0:T(8,128)S(1)}, f32[32,64,128]{2,1,0:T(8,128)}, u32[]{:S(2)}) %copy-start) | copy-done | bytes 1048600
  22.2 17.2 %shard_map.55 = f32[4,64,128]{2,1,0:T(8,128)S(1)} custom-call(s32[6]{0:T(128)S(1)} %stack.27.lim_ref, f32[24]{0:T(128)S(1)} %pad_maximum_fusion.2.prm_ref, f32[32,64,128]{2,1,0:T(8,128)S(1)} %copy-done, f32[4,64,128]{2,1,0:T(8,128)S(1)} %collective-permute-done.zlo_hbm, f32[4,64,128]{2,1,0:T(8,128)S(1)} %collective-permute-done.1.zhi_hbm, ...), custom_call_target="tpu_custom_call" | custom-call | flops 133693440 | bytes 3080192 | tf_op jit(solution)/shard_map/pallas_call | solution.py:193
  39.5 12.9 %all_to_all.5 = f32[4,8,8,128]{3,2,0,1:T(8,128)S(1)} all-to-all(f32[4,8,8,128]{3,2,0,1:T(8,128)S(1)} %copy.32), channel_id=1, replica_groups=mesh['gx'=2,'gy'=2,'gz'=8] {'gz'}, dimensions={1} | all-to-all | bytes 262144 | tf_op jit(solution)/shard_map/all_to_all | solution.py:247
  52.4 0.6 %pad_maximum_fusion.1 = f32[4,8,128]{2,1,0:T(8,128)} fusion(f32[1,8,128]{2,1,0:T(8,128)S(1)} %get-tuple-element.13, f32[3,8,128]{2,1,0:T(8,128)S(1)} %fusion.2), kind=kLoop, calls=%fused_computation.14 | loop fusion | flops 4096 | bytes 32768 | tf_op jit(solution)/shard_map/concatenate | solution.py:254
  (12 shorter events, 0.2 us)
Async XLA Ops:
  1.0 8.0 %collective-permute-start = (f32[4,64,128]{2,1,0:T(8,128)S(1)}, f32[4,64,128]{2,1,0:T(8,128)S(1)}, u32[]{:S(2)}, u32[]{:S(2)}) collective-permute-start(f32[4,64,128]{2,1,0:T(8,128)S(1)} %get-tuple-element.10), channel_id=1, source_target_pairs={{0,1},{1,2},{2,3},{3,4},{4,5},{5,6},{6,7},{8,9},{9,10},{10,11},{11... | collective-permute-start | bytes 393224 | tf_op jit(solution)/shard_map/ppermute | solution.py:65
  5.9 6.9 %collective-permute-start.1 = (f32[4,64,128]{2,1,0:T(8,128)S(1)}, f32[4,64,128]{2,1,0:T(8,128)S(1)}, u32[]{:S(2)}, u32[]{:S(2)}) collective-permute-start(f32[4,64,128]{2,1,0:T(8,128)S(1)} %get-tuple-element.9), channel_id=1, source_target_pairs={{1,0},{2,1},{3,2},{4,3},{5,4},{6,5},{7,6},{9,8},{10,9},{11,10},{12... | collective-permute-start | bytes 393224 | tf_op jit(solution)/shard_map/ppermute | solution.py:65
  12.9 4.8 %collective-permute-start.4 = (f32[40,4,4]{2,1,0:T(4,128)S(1)}, f32[40,4,4]{2,1,0:T(4,128)S(1)}, u32[]{:S(2)}, u32[]{:S(2)}) collective-permute-start(f32[40,4,4]{2,1,0:T(4,128)S(1)} %slice_select_fusion.1), channel_id=1, source_target_pairs={{0,24},{8,16},{16,8},{24,0},{1,25},{9,17},{17,9},{25,1},{2,26},{10... | collective-permute-start | bytes 7688 | tf_op jit(solution)/shard_map/ppermute | solution.py:65
  13.4 8.1 %collective-permute-start.2 = (f32[40,4,128]{2,1,0:T(4,128)S(1)}, f32[40,4,128]{2,1,0:T(4,128)S(1)}, u32[]{:S(2)}, u32[]{:S(2)}) collective-permute-start(f32[40,4,128]{2,1,0:T(4,128)S(1)} %slice_select_fusion.2), channel_id=1, source_target_pairs={{0,16},{16,0},{1,17},{17,1},{2,18},{18,2},{3,19},{19,3},{4,20},{20... | collective-permute-start | bytes 245768 | tf_op jit(solution)/shard_map/ppermute | solution.py:65
  15.5 4.5 %collective-permute-start.3 = (f32[4,40,64]{2,1,0:T(8,128)S(1)}, f32[4,40,64]{2,1,0:T(8,128)S(1)}, u32[]{:S(2)}, u32[]{:S(2)}) collective-permute-start(f32[4,40,64]{2,1,0:T(8,128)S(1)} %copy.29), channel_id=1, source_target_pairs={{0,8},{8,0},{1,9},{9,1},{2,10},{10,2},{3,11},{11,3},{4,12},{12,4},... | collective-permute-start | bytes 122888 | tf_op jit(solution)/shard_map/ppermute | solution.py:65
  21.0 1.2 %copy-start = (f32[32,64,128]{2,1,0:T(8,128)S(1)}, f32[32,64,128]{2,1,0:T(8,128)}, u32[]{:S(2)}) copy-start(f32[32,64,128]{2,1,0:T(8,128)} %x_hbm.1) | copy-start | bytes 3145732

commit v12 on v11

--- a/solution.py
+++ b/solution.py
@@ -153,7 +153,7 @@
             dst[z] = new * (m_ref[...] * zf)
             return g
 
-        lax.fori_loop(z0, z1, body, g0, unroll=4)
+        lax.fori_loop(z0, z1, body, g0, unroll=8)
 
     smooth(b_ref, a_ref, 0)
     smooth(a_ref, b_ref, 1)
@@ -179,7 +179,7 @@
         out_ref[CHANNELS] = run + ext
         return g
 
-    lax.fori_loop(z0, z1, final, g0, unroll=2)
+    lax.fori_loop(z0, z1, final, g0, unroll=4)
     for ch in range(CHANNELS):
         emit = col[ch][0] * acc_ref[0] + col[ch][1] * acc_ref[1] + col[ch][2] * acc_ref[2] + col[ch][3] * acc_ref[3]
         out_ref[ch] = h * emit

time: 53.3 us -> 53.2 us (level)
  no operation moved by 1% of the time
where the time goes in v12:
time: 53.2 us; the launch traced here: 52.9 us
  Pallas kernels  17.1 us (32%)
  blocking collectives  12.9 us (24%)
  starting transfers between devices  8.51 us (16%)
  waiting for transfers between devices  6.33 us (12%)
  local copies, waits for them, and re-layouts  5.28 us (10%)
  other arithmetic  2.59 us (5%)
    pallas_call x1, Pallas kernels, render_block(): pl.pallas_call(kernel, out_shape=jax.ShapeDtypeStruct((CHANNELS + 1, r_in...  17.1 us
    all_to_all x1, blocking collectives, shards(): got = lax.all_to_all(parts, 'gz', 1, 1, tiled=True)  12.9 us
    ppermute x5, starting transfers between devices, halo_stage(): got = lax.ppermute(piece, tuple((a for a, _, _ in used)), pairs)  8.51 us
    ppermute x5, waiting for transfers between devices, halo_stage(): got = lax.ppermute(piece, tuple((a for a, _, _ in used)), pairs)  6.33 us
    unnamed x4, local copies, waits for them, and re-layouts  1.95 us
  transfers between devices with their start and end apart: 5, of which 3 were waited for; matrix products, arithmetic and copies ran while one was open for 10% of the time, Pallas kernels for 0%

profile of v12, /device:TPU:0, one launch (start us, length us, event | category | flops | bytes accessed | tf_op | source)
XLA Modules:
  0.0 52.9 jit_solution(5333429829550535743)
XLA Ops:
  0.0 1.0 %fusion.19 = (f32[4,64,128]{2,1,0:T(8,128)S(1)}, f32[4,64,128]{2,1,0:T(8,128)S(1)}) fusion(f32[32,64,128]{2,1,0:T(8,128)} %x_hbm.1), kind=kLoop, calls=%fused_computation.59 | loop fusion | bytes 524288 | tf_op jit(solution)/shard_map/slice | solution.py:52
  1.0 4.9 %collective-permute-start = (f32[4,64,128]{2,1,0:T(8,128)S(1)}, f32[4,64,128]{2,1,0:T(8,128)S(1)}, u32[]{:S(2)}, u32[]{:S(2)}) collective-permute-start(f32[4,64,128]{2,1,0:T(8,128)S(1)} %get-tuple-element.10), channel_id=1, source_target_pairs={{0,1},{1,2},{2,3},{3,4},{4,5},{5,6},{6,7},{8,9},{9,10},{10,11},{11... | collective-permute-start | bytes 393224 | tf_op jit(solution)/shard_map/ppermute | solution.py:65
  5.9 1.3 %collective-permute-start.1 = (f32[4,64,128]{2,1,0:T(8,128)S(1)}, f32[4,64,128]{2,1,0:T(8,128)S(1)}, u32[]{:S(2)}, u32[]{:S(2)}) collective-permute-start(f32[4,64,128]{2,1,0:T(8,128)S(1)} %get-tuple-element.9), channel_id=1, source_target_pairs={{1,0},{2,1},{3,2},{4,3},{5,4},{6,5},{7,6},{9,8},{10,9},{11,10},{12... | collective-permute-start | bytes 393224 | tf_op jit(solution)/shard_map/ppermute | solution.py:65
  7.3 0.8 %reshape.210 = f32[12]{0:T(128)S(1)} reshape(f32[3,4]{1,0:T(4,128)} %param.9) | data formatting | bytes 96 | tf_op jit(solution)/shard_map/reshape | solution.py:241
  8.0 0.1 pad.5.clone
  8.1 0.1 stack.27.lim_ref
  8.2 0.8 %pad_maximum_fusion.2.prm_ref = f32[24]{0:T(128)S(1)} fusion(f32[12]{0:T(128)S(1)} %reshape.210, f32[4]{0:T(128)} %param.8, f32[4]{0:T(128)} %param.7, f32[4]{0:T(128)} %param.6), kind=kLoop, calls=%fused_computation.58 | loop fusion | flops 72 | bytes 192 | tf_op jit(solution)/shard_map/concatenate | solution.py:241
  8.9 0.0 collective-permute-done.zlo_hbm
  9.0 1.3 %constant_dynamic-update-slice_fusion.1 = f32[40,64,128]{2,1,0:T(8,128)S(1)} fusion(f32[40,64,128]{2,1,0:T(8,128)S(1)} %constant_dynamic-update-slice_fusion.2, f32[32,64,128]{2,1,0:T(8,128)} %x_hbm.1), kind=kLoop, calls=%fused_computation.38 | loop fusion | bytes 2097152
  10.3 2.5 %collective-permute-done.1.zhi_hbm = f32[4,64,128]{2,1,0:T(8,128)S(1)} collective-permute-done((f32[4,64,128]{2,1,0:T(8,128)S(1)}, f32[4,64,128]{2,1,0:T(8,128)S(1)}, u32[]{:S(2)}, u32[]{:S(2)}) %collective-permute-start.1) | collective-permute-done | bytes 131104 | tf_op jit(solution)/shard_map/ppermute | solution.py:65
  12.8 0.1 slice_select_fusion.1
  12.9 0.1 collective-permute-start.4
  13.0 0.4 fusion
  13.4 1.7 %collective-permute-start.2 = (f32[40,4,128]{2,1,0:T(4,128)S(1)}, f32[40,4,128]{2,1,0:T(4,128)S(1)}, u32[]{:S(2)}, u32[]{:S(2)}) collective-permute-start(f32[40,4,128]{2,1,0:T(4,128)S(1)} %slice_select_fusion.2), channel_id=1, source_target_pairs={{0,16},{16,0},{1,17},{17,1},{2,18},{18,2},{3,19},{19,3},{4,20},{20... | collective-permute-start | bytes 245768 | tf_op jit(solution)/shard_map/ppermute | solution.py:65
  15.1 0.5 copy.29
  15.5 0.6 %collective-permute-start.3 = (f32[4,40,64]{2,1,0:T(8,128)S(1)}, f32[4,40,64]{2,1,0:T(8,128)S(1)}, u32[]{:S(2)}, u32[]{:S(2)}) collective-permute-start(f32[4,40,64]{2,1,0:T(8,128)S(1)} %copy.29), channel_id=1, source_target_pairs={{0,8},{8,0},{1,9},{9,1},{2,10},{10,2},{3,11},{11,3},{4,12},{12,4},... | collective-permute-start | bytes 122888 | tf_op jit(solution)/shard_map/ppermute | solution.py:65
  16.1 1.6 %collective-permute-done.4 = f32[40,4,4]{2,1,0:T(4,128)S(1)} collective-permute-done((f32[40,4,4]{2,1,0:T(4,128)S(1)}, f32[40,4,4]{2,1,0:T(4,128)S(1)}, u32[]{:S(2)}, u32[]{:S(2)}) %collective-permute-start.4) | collective-permute-done | bytes 2592 | tf_op jit(solution)/shard_map/ppermute | solution.py:65
  17.7 0.1 broadcast_select_fusion.3
  17.7 2.3 %collective-permute-done.3 = f32[4,40,64]{2,1,0:T(8,128)S(1)} collective-permute-done((f32[4,40,64]{2,1,0:T(8,128)S(1)}, f32[4,40,64]{2,1,0:T(8,128)S(1)}, u32[]{:S(2)}, u32[]{:S(2)}) %collective-permute-start.3) | collective-permute-done | bytes 40992 | tf_op jit(solution)/shard_map/ppermute | solution.py:65
  20.0 0.5 copy.30
  20.5 0.5 copy.31
  21.0 0.0 copy-start
  21.0 0.5 maximum_maximum_fusion.cband_hbm
  21.5 0.0 collective-permute-done.2
  21.6 0.6 %copy-done = f32[32,64,128]{2,1,0:T(8,128)S(1)} copy-done((f32[32,64,128]{2,1,0:T(8,128)S(1)}, f32[32,64,128]{2,1,0:T(8,128)}, u32[]{:S(2)}) %copy-start) | copy-done | bytes 1048600
  22.2 17.1 %shard_map.55 = f32[4,64,128]{2,1,0:T(8,128)S(1)} custom-call(s32[6]{0:T(128)S(1)} %stack.27.lim_ref, f32[24]{0:T(128)S(1)} %pad_maximum_fusion.2.prm_ref, f32[32,64,128]{2,1,0:T(8,128)S(1)} %copy-done, f32[4,64,128]{2,1,0:T(8,128)S(1)} %collective-permute-done.zlo_hbm, f32[4,64,128]{2,1,0:T(8,128)S(1)} %collective-permute-done.1.zhi_hbm, ...), custom_call_target="tpu_custom_call" | custom-call | flops 133693440 | bytes 3080192 | tf_op jit(solution)/shard_map/pallas_call | solution.py:193
  39.4 12.9 %all_to_all.5 = f32[4,8,8,128]{3,2,0,1:T(8,128)S(1)} all-to-all(f32[4,8,8,128]{3,2,0,1:T(8,128)S(1)} %copy.32), channel_id=1, replica_groups=mesh['gx'=2,'gy'=2,'gz'=8] {'gz'}, dimensions={1} | all-to-all | bytes 262144 | tf_op jit(solution)/shard_map/all_to_all | solution.py:247
  52.3 0.6 %pad_maximum_fusion.1 = f32[4,8,128]{2,1,0:T(8,128)} fusion(f32[1,8,128]{2,1,0:T(8,128)S(1)} %get-tuple-element.13, f32[3,8,128]{2,1,0:T(8,128)S(1)} %fusion.2), kind=kLoop, calls=%fused_computation.14 | loop fusion | flops 4096 | bytes 32768 | tf_op jit(solution)/shard_map/concatenate | solution.py:254
  (12 shorter events, 0.2 us)
Async XLA Ops:
  1.0 8.0 %collective-permute-start = (f32[4,64,128]{2,1,0:T(8,128)S(1)}, f32[4,64,128]{2,1,0:T(8,128)S(1)}, u32[]{:S(2)}, u32[]{:S(2)}) collective-permute-start(f32[4,64,128]{2,1,0:T(8,128)S(1)} %get-tuple-element.10), channel_id=1, source_target_pairs={{0,1},{1,2},{2,3},{3,4},{4,5},{5,6},{6,7},{8,9},{9,10},{10,11},{11... | collective-permute-start | bytes 393224 | tf_op jit(solution)/shard_map/ppermute | solution.py:65
  5.9 6.9 %collective-permute-start.1 = (f32[4,64,128]{2,1,0:T(8,128)S(1)}, f32[4,64,128]{2,1,0:T(8,128)S(1)}, u32[]{:S(2)}, u32[]{:S(2)}) collective-permute-start(f32[4,64,128]{2,1,0:T(8,128)S(1)} %get-tuple-element.9), channel_id=1, source_target_pairs={{1,0},{2,1},{3,2},{4,3},{5,4},{6,5},{7,6},{9,8},{10,9},{11,10},{12... | collective-permute-start | bytes 393224 | tf_op jit(solution)/shard_map/ppermute | solution.py:65
  12.9 4.8 %collective-permute-start.4 = (f32[40,4,4]{2,1,0:T(4,128)S(1)}, f32[40,4,4]{2,1,0:T(4,128)S(1)}, u32[]{:S(2)}, u32[]{:S(2)}) collective-permute-start(f32[40,4,4]{2,1,0:T(4,128)S(1)} %slice_select_fusion.1), channel_id=1, source_target_pairs={{0,24},{8,16},{16,8},{24,0},{1,25},{9,17},{17,9},{25,1},{2,26},{10... | collective-permute-start | bytes 7688 | tf_op jit(solution)/shard_map/ppermute | solution.py:65
  13.4 8.1 %collective-permute-start.2 = (f32[40,4,128]{2,1,0:T(4,128)S(1)}, f32[40,4,128]{2,1,0:T(4,128)S(1)}, u32[]{:S(2)}, u32[]{:S(2)}) collective-permute-start(f32[40,4,128]{2,1,0:T(4,128)S(1)} %slice_select_fusion.2), channel_id=1, source_target_pairs={{0,16},{16,0},{1,17},{17,1},{2,18},{18,2},{3,19},{19,3},{4,20},{20... | collective-permute-start | bytes 245768 | tf_op jit(solution)/shard_map/ppermute | solution.py:65
  15.5 4.5 %collective-permute-start.3 = (f32[4,40,64]{2,1,0:T(8,128)S(1)}, f32[4,40,64]{2,1,0:T(8,128)S(1)}, u32[]{:S(2)}, u32[]{:S(2)}) collective-permute-start(f32[4,40,64]{2,1,0:T(8,128)S(1)} %copy.29), channel_id=1, source_target_pairs={{0,8},{8,0},{1,9},{9,1},{2,10},{10,2},{3,11},{11,3},{4,12},{12,4},... | collective-permute-start | bytes 122888 | tf_op jit(solution)/shard_map/ppermute | solution.py:65
  21.0 1.2 %copy-start = (f32[32,64,128]{2,1,0:T(8,128)S(1)}, f32[32,64,128]{2,1,0:T(8,128)}, u32[]{:S(2)}) copy-start(f32[32,64,128]{2,1,0:T(8,128)} %x_hbm.1) | copy-start | bytes 3145732

commit v13 on v6

--- a/solution.py
+++ b/solution.py
@@ -59,7 +59,12 @@
             for (_, s, _), (p, q) in zip(used, parts):
                 src, dst = src * s + p, dst * s + q
             pairs.append((src, dst))
+        narrow = piece.ndim == 3 and piece.shape[2] == width and piece.shape[1] > width
+        if narrow:
+            piece = jnp.transpose(piece, (2, 0, 1))
         got = lax.ppermute(piece, tuple(a for a, _, _ in used), pairs)
+        if narrow:
+            got = jnp.transpose(got, (1, 2, 0))
         landing = [(d, m[2]) for d, m in zip(dims, combo) if m is not None]
         for sides in itertools.product(("lo", "hi"), repeat=len(landing)):
             cond = True
@@ -120,8 +125,7 @@
     row_at = jnp.where(row < r_in + halo, row, row - rows)
     lane_at = jnp.where(lane < (l_in + lanes) // 2, lane, lane - lanes)
     ok = (row_at >= lim_ref[2]) & (row_at < lim_ref[3]) & (lane_at >= lim_ref[4]) & (lane_at < lim_ref[5])
-    m_ref[0] = jnp.zeros((rows, lanes), jnp.float32)
-    m_ref[1] = jnp.where(ok, 1.0, 0.0).astype(jnp.float32)
+    m_ref[...] = jnp.where(ok, 1.0, 0.0).astype(jnp.float32)
 
     cen = [prm_ref[k] for k in range(MATERIALS)]
     wid = [prm_ref[MATERIALS + k] for k in range(MATERIALS)]
@@ -145,11 +149,21 @@
             fc = flux(pltpu.roll(c, lanes - 1, 1) - c)
             plane = (fr - pltpu.roll(fr, 1, 0)) + (fc - pltpu.roll(fc, 1, 1))
             new = c + RATE_DEPTH * (g - g_prev) + RATE_PLANE * plane
-            inside = ((z >= lim_ref[0]) & (z < lim_ref[1])).astype(jnp.int32)
-            dst[z] = new * m_ref[inside]
+            inside = (z >= lim_ref[0]) & (z < lim_ref[1])
+
+            @pl.when(inside)
+            def _():
+                dst[z, 0:r_in, 0:l_in] = new[0:r_in, 0:l_in]
+                dst[z, r_in:rows, :] = new[r_in:rows] * m_ref[r_in:rows, :]
+                dst[z, 0:r_in, l_in:lanes] = new[0:r_in, l_in:lanes] * m_ref[0:r_in, l_in:lanes]
+
+            @pl.when(jnp.logical_not(inside))
+            def _():
+                dst[z] = jnp.zeros((rows, lanes), jnp.float32)
+
             return g
 
-        lax.fori_loop(z0, z1, body, g0)
+        lax.fori_loop(z0, z1, body, g0, unroll=8)
 
     smooth(b_ref, a_ref, 0)
     smooth(a_ref, b_ref, 1)
@@ -176,7 +190,7 @@
         out_ref[CHANNELS] = run + ext
         return g
 
-    lax.fori_loop(z0, z1, final, g0)
+    lax.fori_loop(z0, z1, final, g0, unroll=4)
     for ch in range(CHANNELS):
         emit = col[ch][0] * acc_ref[0] + col[ch][1] * acc_ref[1] + col[ch][2] * acc_ref[2] + col[ch][3] * acc_ref[3]
         out_ref[ch] = h * emit
@@ -195,7 +209,7 @@
         scratch_shapes=[
             pltpu.VMEM((depth, rows, lanes), jnp.float32),
             pltpu.VMEM((depth, rows, lanes), jnp.float32),
-            pltpu.VMEM((2, rows, lanes), jnp.float32),
+            pltpu.VMEM((rows, lanes), jnp.float32),
             pltpu.VMEM((MATERIALS, r_in, l_in), jnp.float32),
             pltpu.SemaphoreType.DMA((5,)),
         ],

time: 65.6 us -> 60.9 us (0.928)
  Pallas kernels: 28.9 us -> 24.8 us
  local copies, waits for them, and re-layouts: 6.2 us -> 5.28 us
    pallas_call x1, Pallas kernels: 28.9 us -> 24.8 us  [render_block(): pl.pallas_call(kernel, out_shape=jax.ShapeDtypeStruct((CHANNELS + 1, r_in...]
    slice x3 -> x1, local copies, waits for them, and re-layouts: 1.92 us -> 0.99 us  [halo_stage(): lo = lax.slice_in_dim(piece, 0, width, axis=d)]
where the time goes in v13:
time: 60.9 us; the launch traced here: 60.6 us
  Pallas kernels  24.8 us (41%)
  blocking collectives  12.8 us (21%)
  starting transfers between devices  8.51 us (14%)
  waiting for transfers between devices  6.33 us (10%)
  local copies, waits for them, and re-layouts  5.28 us (9%)
  other arithmetic  2.59 us (4%)
    pallas_call x1, Pallas kernels, render_block(): pl.pallas_call(kernel, out_shape=jax.ShapeDtypeStruct((CHANNELS + 1, r_in...  24.8 us
    all_to_all x1, blocking collectives, shards(): got = lax.all_to_all(parts, 'gz', 1, 1, tiled=True)  12.8 us
    ppermute x5, starting transfers between devices, halo_stage(): got = lax.ppermute(piece, tuple((a for a, _, _ in used)), pairs)  8.51 us
    ppermute x5, waiting for transfers between devices, halo_stage(): got = lax.ppermute(piece, tuple((a for a, _, _ in used)), pairs)  6.33 us
    unnamed x4, local copies, waits for them, and re-layouts  1.95 us
  transfers between devices with their start and end apart: 5, of which 3 were waited for; matrix products, arithmetic and copies ran while one was open for 9% of the time, Pallas kernels for 0%

profile of v13, /device:TPU:0, one launch (start us, length us, event | category | flops | bytes accessed | tf_op | source)
XLA Modules:
  0.0 60.6 jit_solution(17352782418274140966)
XLA Ops:
  0.0 1.0 %fusion.19 = (f32[4,64,128]{2,1,0:T(8,128)S(1)}, f32[4,64,128]{2,1,0:T(8,128)S(1)}) fusion(f32[32,64,128]{2,1,0:T(8,128)} %x_hbm.1), kind=kLoop, calls=%fused_computation.59 | loop fusion | bytes 524288 | tf_op jit(solution)/shard_map/slice | solution.py:52
  1.0 4.9 %collective-permute-start = (f32[4,64,128]{2,1,0:T(8,128)S(1)}, f32[4,64,128]{2,1,0:T(8,128)S(1)}, u32[]{:S(2)}, u32[]{:S(2)}) collective-permute-start(f32[4,64,128]{2,1,0:T(8,128)S(1)} %get-tuple-element.10), channel_id=1, source_target_pairs={{0,1},{1,2},{2,3},{3,4},{4,5},{5,6},{6,7},{8,9},{9,10},{10,11},{11... | collective-permute-start | bytes 393224 | tf_op jit(solution)/shard_map/ppermute | solution.py:65
  5.9 1.3 %collective-permute-start.1 = (f32[4,64,128]{2,1,0:T(8,128)S(1)}, f32[4,64,128]{2,1,0:T(8,128)S(1)}, u32[]{:S(2)}, u32[]{:S(2)}) collective-permute-start(f32[4,64,128]{2,1,0:T(8,128)S(1)} %get-tuple-element.9), channel_id=1, source_target_pairs={{1,0},{2,1},{3,2},{4,3},{5,4},{6,5},{7,6},{9,8},{10,9},{11,10},{12... | collective-permute-start | bytes 393224 | tf_op jit(solution)/shard_map/ppermute | solution.py:65
  7.3 0.8 %reshape.210 = f32[12]{0:T(128)S(1)} reshape(f32[3,4]{1,0:T(4,128)} %param.9) | data formatting | bytes 96 | tf_op jit(solution)/shard_map/reshape | solution.py:252
  8.0 0.1 pad.5.clone
  8.1 0.1 stack.27.lim_ref
  8.2 0.8 %pad_maximum_fusion.2.prm_ref = f32[24]{0:T(128)S(1)} fusion(f32[12]{0:T(128)S(1)} %reshape.210, f32[4]{0:T(128)} %param.8, f32[4]{0:T(128)} %param.7, f32[4]{0:T(128)} %param.6), kind=kLoop, calls=%fused_computation.58 | loop fusion | flops 72 | bytes 192 | tf_op jit(solution)/shard_map/concatenate | solution.py:252
  8.9 0.0 collective-permute-done.zlo_hbm
  9.0 1.3 %constant_dynamic-update-slice_fusion.1 = f32[40,64,128]{2,1,0:T(8,128)S(1)} fusion(f32[40,64,128]{2,1,0:T(8,128)S(1)} %constant_dynamic-update-slice_fusion.2, f32[32,64,128]{2,1,0:T(8,128)} %x_hbm.1), kind=kLoop, calls=%fused_computation.38 | loop fusion | bytes 2097152
  10.3 2.5 %collective-permute-done.1.zhi_hbm = f32[4,64,128]{2,1,0:T(8,128)S(1)} collective-permute-done((f32[4,64,128]{2,1,0:T(8,128)S(1)}, f32[4,64,128]{2,1,0:T(8,128)S(1)}, u32[]{:S(2)}, u32[]{:S(2)}) %collective-permute-start.1) | collective-permute-done | bytes 131104 | tf_op jit(solution)/shard_map/ppermute | solution.py:65
  12.8 0.1 slice_select_fusion.1
  12.9 0.1 collective-permute-start.4
  13.0 0.4 fusion
  13.4 1.7 %collective-permute-start.2 = (f32[40,4,128]{2,1,0:T(4,128)S(1)}, f32[40,4,128]{2,1,0:T(4,128)S(1)}, u32[]{:S(2)}, u32[]{:S(2)}) collective-permute-start(f32[40,4,128]{2,1,0:T(4,128)S(1)} %slice_select_fusion.2), channel_id=1, source_target_pairs={{0,16},{16,0},{1,17},{17,1},{2,18},{18,2},{3,19},{19,3},{4,20},{20... | collective-permute-start | bytes 245768 | tf_op jit(solution)/shard_map/ppermute | solution.py:65
  15.1 0.5 copy.29
  15.5 0.6 collective-permute-start.3
  16.1 1.6 %collective-permute-done.4 = f32[40,4,4]{2,1,0:T(4,128)S(1)} collective-permute-done((f32[40,4,4]{2,1,0:T(4,128)S(1)}, f32[40,4,4]{2,1,0:T(4,128)S(1)}, u32[]{:S(2)}, u32[]{:S(2)}) %collective-permute-start.4) | collective-permute-done | bytes 2592 | tf_op jit(solution)/shard_map/ppermute | solution.py:65
  17.7 0.1 broadcast_select_fusion.3
  17.7 2.3 %collective-permute-done.3 = f32[4,40,64]{2,1,0:T(8,128)S(1)} collective-permute-done((f32[4,40,64]{2,1,0:T(8,128)S(1)}, f32[4,40,64]{2,1,0:T(8,128)S(1)}, u32[]{:S(2)}, u32[]{:S(2)}) %collective-permute-start.3) | collective-permute-done | bytes 40992 | tf_op jit(solution)/shard_map/ppermute | solution.py:65
  20.0 0.5 copy.30
  20.5 0.5 copy.31
  21.0 0.0 copy-start
  21.0 0.5 maximum_maximum_fusion.cband_hbm
  21.5 0.0 collective-permute-done.2
  21.6 0.6 %copy-done = f32[32,64,128]{2,1,0:T(8,128)S(1)} copy-done((f32[32,64,128]{2,1,0:T(8,128)S(1)}, f32[32,64,128]{2,1,0:T(8,128)}, u32[]{:S(2)}) %copy-start) | copy-done | bytes 1048600
  22.2 24.8 %shard_map.55 = f32[4,64,128]{2,1,0:T(8,128)S(1)} custom-call(s32[6]{0:T(128)S(1)} %stack.27.lim_ref, f32[24]{0:T(128)S(1)} %pad_maximum_fusion.2.prm_ref, f32[32,64,128]{2,1,0:T(8,128)S(1)} %copy-done, f32[4,64,128]{2,1,0:T(8,128)S(1)} %collective-permute-done.zlo_hbm, f32[4,64,128]{2,1,0:T(8,128)S(1)} %collective-permute-done.1.zhi_hbm, ...), custom_call_target="tpu_custom_call" | custom-call | flops 133693440 | bytes 3080192 | tf_op jit(solution)/shard_map/pallas_call | solution.py:204
  47.1 12.8 %all_to_all.5 = f32[4,8,8,128]{3,2,0,1:T(8,128)S(1)} all-to-all(f32[4,8,8,128]{3,2,0,1:T(8,128)S(1)} %copy.32), channel_id=1, replica_groups=mesh['gx'=2,'gy'=2,'gz'=8] {'gz'}, dimensions={1} | all-to-all | bytes 262144 | tf_op jit(solution)/shard_map/all_to_all | solution.py:258
  60.0 0.6 %pad_maximum_fusion.1 = f32[4,8,128]{2,1,0:T(8,128)} fusion(f32[1,8,128]{2,1,0:T(8,128)S(1)} %get-tuple-element.13, f32[3,8,128]{2,1,0:T(8,128)S(1)} %fusion.2), kind=kLoop, calls=%fused_computation.14 | loop fusion | flops 4096 | bytes 32768 | tf_op jit(solution)/shard_map/concatenate | solution.py:265
  (12 shorter events, 0.2 us)
Async XLA Ops:
  1.0 8.0 %collective-permute-start = (f32[4,64,128]{2,1,0:T(8,128)S(1)}, f32[4,64,128]{2,1,0:T(8,128)S(1)}, u32[]{:S(2)}, u32[]{:S(2)}) collective-permute-start(f32[4,64,128]{2,1,0:T(8,128)S(1)} %get-tuple-element.10), channel_id=1, source_target_pairs={{0,1},{1,2},{2,3},{3,4},{4,5},{5,6},{6,7},{8,9},{9,10},{10,11},{11... | collective-permute-start | bytes 393224 | tf_op jit(solution)/shard_map/ppermute | solution.py:65
  5.9 6.9 %collective-permute-start.1 = (f32[4,64,128]{2,1,0:T(8,128)S(1)}, f32[4,64,128]{2,1,0:T(8,128)S(1)}, u32[]{:S(2)}, u32[]{:S(2)}) collective-permute-start(f32[4,64,128]{2,1,0:T(8,128)S(1)} %get-tuple-element.9), channel_id=1, source_target_pairs={{1,0},{2,1},{3,2},{4,3},{5,4},{6,5},{7,6},{9,8},{10,9},{11,10},{12... | collective-permute-start | bytes 393224 | tf_op jit(solution)/shard_map/ppermute | solution.py:65
  12.9 4.8 %collective-permute-start.4 = (f32[40,4,4]{2,1,0:T(4,128)S(1)}, f32[40,4,4]{2,1,0:T(4,128)S(1)}, u32[]{:S(2)}, u32[]{:S(2)}) collective-permute-start(f32[40,4,4]{2,1,0:T(4,128)S(1)} %slice_select_fusion.1), channel_id=1, source_target_pairs={{0,24},{8,16},{16,8},{24,0},{1,25},{9,17},{17,9},{25,1},{2,26},{10... | collective-permute-start | bytes 7688 | tf_op jit(solution)/shard_map/ppermute | solution.py:65
  13.4 8.1 %collective-permute-start.2 = (f32[40,4,128]{2,1,0:T(4,128)S(1)}, f32[40,4,128]{2,1,0:T(4,128)S(1)}, u32[]{:S(2)}, u32[]{:S(2)}) collective-permute-start(f32[40,4,128]{2,1,0:T(4,128)S(1)} %slice_select_fusion.2), channel_id=1, source_target_pairs={{0,16},{16,0},{1,17},{17,1},{2,18},{18,2},{3,19},{19,3},{4,20},{20... | collective-permute-start | bytes 245768 | tf_op jit(solution)/shard_map/ppermute | solution.py:65
  15.5 4.5 %collective-permute-start.3 = (f32[4,40,64]{2,1,0:T(8,128)S(1)}, f32[4,40,64]{2,1,0:T(8,128)S(1)}, u32[]{:S(2)}, u32[]{:S(2)}) collective-permute-start(f32[4,40,64]{2,1,0:T(8,128)S(1)} %copy.29), channel_id=1, source_target_pairs={{0,8},{8,0},{1,9},{9,1},{2,10},{10,2},{3,11},{11,3},{4,12},{12,4},... | collective-permute-start | bytes 122888 | tf_op jit(solution)/shard_map/ppermute | solution.py:65
  21.0 1.2 %copy-start = (f32[32,64,128]{2,1,0:T(8,128)S(1)}, f32[32,64,128]{2,1,0:T(8,128)}, u32[]{:S(2)}) copy-start(f32[32,64,128]{2,1,0:T(8,128)} %x_hbm.1) | copy-start | bytes 3145732

commit v14 on v13

--- a/solution.py
+++ b/solution.py
@@ -150,17 +150,8 @@
             plane = (fr - pltpu.roll(fr, 1, 0)) + (fc - pltpu.roll(fc, 1, 1))
             new = c + RATE_DEPTH * (g - g_prev) + RATE_PLANE * plane
             inside = (z >= lim_ref[0]) & (z < lim_ref[1])
-
-            @pl.when(inside)
-            def _():
-                dst[z, 0:r_in, 0:l_in] = new[0:r_in, 0:l_in]
-                dst[z, r_in:rows, :] = new[r_in:rows] * m_ref[r_in:rows, :]
-                dst[z, 0:r_in, l_in:lanes] = new[0:r_in, l_in:lanes] * m_ref[0:r_in, l_in:lanes]
-
-            @pl.when(jnp.logical_not(inside))
-            def _():
-                dst[z] = jnp.zeros((rows, lanes), jnp.float32)
-
+            zf = jnp.where(inside, 1.0, 0.0).astype(jnp.float32)
+            dst[z] = new * (m_ref[...] * zf)
             return g
 
         lax.fori_loop(z0, z1, body, g0, unroll=8)

time: 60.9 us -> 53.7 us (0.88)
  Pallas kernels: 24.8 us -> 17.6 us
    pallas_call x1, Pallas kernels: 24.8 us -> 17.6 us  [render_block(): pl.pallas_call(kernel, out_shape=jax.ShapeDtypeStruct((CHANNELS + 1, r_in...]
  transfers between devices with their start and end apart: 5 -> 5, of which waited for: 3 -> 3; matrix products, arithmetic and copies ran while one was open for 9% -> 10% of each run, Pallas kernels for 0% -> 0%
where the time goes in v14:
time: 53.7 us; the launch traced here: 53.3 us
  Pallas kernels  17.6 us (33%)
  blocking collectives  12.9 us (24%)
  starting transfers between devices  8.51 us (16%)
  waiting for transfers between devices  6.33 us (12%)
  local copies, waits for them, and re-layouts  5.28 us (10%)
  other arithmetic  2.59 us (5%)
    pallas_call x1, Pallas kernels, render_block(): pl.pallas_call(kernel, out_shape=jax.ShapeDtypeStruct((CHANNELS + 1, r_in...  17.6 us
    all_to_all x1, blocking collectives, shards(): got = lax.all_to_all(parts, 'gz', 1, 1, tiled=True)  12.9 us
    ppermute x5, starting transfers between devices, halo_stage(): got = lax.ppermute(piece, tuple((a for a, _, _ in used)), pairs)  8.51 us
    ppermute x5, waiting for transfers between devices, halo_stage(): got = lax.ppermute(piece, tuple((a for a, _, _ in used)), pairs)  6.33 us
    unnamed x4, local copies, waits for them, and re-layouts  1.95 us
  transfers between devices with their start and end apart: 5, of which 3 were waited for; matrix products, arithmetic and copies ran while one was open for 10% of the time, Pallas kernels for 0%

profile of v14, /device:TPU:0, one launch (start us, length us, event | category | flops | bytes accessed | tf_op | source)
XLA Modules:
  0.0 53.3 jit_solution(12505632454809073837)
XLA Ops:
  0.0 1.0 %fusion.19 = (f32[4,64,128]{2,1,0:T(8,128)S(1)}, f32[4,64,128]{2,1,0:T(8,128)S(1)}) fusion(f32[32,64,128]{2,1,0:T(8,128)} %x_hbm.1), kind=kLoop, calls=%fused_computation.59 | loop fusion | bytes 524288 | tf_op jit(solution)/shard_map/slice | solution.py:52
  1.0 4.9 %collective-permute-start = (f32[4,64,128]{2,1,0:T(8,128)S(1)}, f32[4,64,128]{2,1,0:T(8,128)S(1)}, u32[]{:S(2)}, u32[]{:S(2)}) collective-permute-start(f32[4,64,128]{2,1,0:T(8,128)S(1)} %get-tuple-element.10), channel_id=1, source_target_pairs={{0,1},{1,2},{2,3},{3,4},{4,5},{5,6},{6,7},{8,9},{9,10},{10,11},{11... | collective-permute-start | bytes 393224 | tf_op jit(solution)/shard_map/ppermute | solution.py:65
  5.9 1.3 %collective-permute-start.1 = (f32[4,64,128]{2,1,0:T(8,128)S(1)}, f32[4,64,128]{2,1,0:T(8,128)S(1)}, u32[]{:S(2)}, u32[]{:S(2)}) collective-permute-start(f32[4,64,128]{2,1,0:T(8,128)S(1)} %get-tuple-element.9), channel_id=1, source_target_pairs={{1,0},{2,1},{3,2},{4,3},{5,4},{6,5},{7,6},{9,8},{10,9},{11,10},{12... | collective-permute-start | bytes 393224 | tf_op jit(solution)/shard_map/ppermute | solution.py:65
  7.3 0.8 %reshape.210 = f32[12]{0:T(128)S(1)} reshape(f32[3,4]{1,0:T(4,128)} %param.9) | data formatting | bytes 96 | tf_op jit(solution)/shard_map/reshape | solution.py:243
  8.0 0.1 pad.5.clone
  8.1 0.1 stack.27.lim_ref
  8.2 0.8 %pad_maximum_fusion.2.prm_ref = f32[24]{0:T(128)S(1)} fusion(f32[12]{0:T(128)S(1)} %reshape.210, f32[4]{0:T(128)} %param.8, f32[4]{0:T(128)} %param.7, f32[4]{0:T(128)} %param.6), kind=kLoop, calls=%fused_computation.58 | loop fusion | flops 72 | bytes 192 | tf_op jit(solution)/shard_map/concatenate | solution.py:243
  8.9 0.0 collective-permute-done.zlo_hbm
  9.0 1.3 %constant_dynamic-update-slice_fusion.1 = f32[40,64,128]{2,1,0:T(8,128)S(1)} fusion(f32[40,64,128]{2,1,0:T(8,128)S(1)} %constant_dynamic-update-slice_fusion.2, f32[32,64,128]{2,1,0:T(8,128)} %x_hbm.1), kind=kLoop, calls=%fused_computation.38 | loop fusion | bytes 2097152
  10.3 2.5 %collective-permute-done.1.zhi_hbm = f32[4,64,128]{2,1,0:T(8,128)S(1)} collective-permute-done((f32[4,64,128]{2,1,0:T(8,128)S(1)}, f32[4,64,128]{2,1,0:T(8,128)S(1)}, u32[]{:S(2)}, u32[]{:S(2)}) %collective-permute-start.1) | collective-permute-done | bytes 131104 | tf_op jit(solution)/shard_map/ppermute | solution.py:65
  12.8 0.1 slice_select_fusion.1
  12.9 0.1 collective-permute-start.4
  13.0 0.4 fusion
  13.4 1.7 %collective-permute-start.2 = (f32[40,4,128]{2,1,0:T(4,128)S(1)}, f32[40,4,128]{2,1,0:T(4,128)S(1)}, u32[]{:S(2)}, u32[]{:S(2)}) collective-permute-start(f32[40,4,128]{2,1,0:T(4,128)S(1)} %slice_select_fusion.2), channel_id=1, source_target_pairs={{0,16},{16,0},{1,17},{17,1},{2,18},{18,2},{3,19},{19,3},{4,20},{20... | collective-permute-start | bytes 245768 | tf_op jit(solution)/shard_map/ppermute | solution.py:65
  15.1 0.5 copy.29
  15.5 0.6 %collective-permute-start.3 = (f32[4,40,64]{2,1,0:T(8,128)S(1)}, f32[4,40,64]{2,1,0:T(8,128)S(1)}, u32[]{:S(2)}, u32[]{:S(2)}) collective-permute-start(f32[4,40,64]{2,1,0:T(8,128)S(1)} %copy.29), channel_id=1, source_target_pairs={{0,8},{8,0},{1,9},{9,1},{2,10},{10,2},{3,11},{11,3},{4,12},{12,4},... | collective-permute-start | bytes 122888 | tf_op jit(solution)/shard_map/ppermute | solution.py:65
  16.1 1.6 %collective-permute-done.4 = f32[40,4,4]{2,1,0:T(4,128)S(1)} collective-permute-done((f32[40,4,4]{2,1,0:T(4,128)S(1)}, f32[40,4,4]{2,1,0:T(4,128)S(1)}, u32[]{:S(2)}, u32[]{:S(2)}) %collective-permute-start.4) | collective-permute-done | bytes 2592 | tf_op jit(solution)/shard_map/ppermute | solution.py:65
  17.7 0.1 broadcast_select_fusion.3
  17.7 2.3 %collective-permute-done.3 = f32[4,40,64]{2,1,0:T(8,128)S(1)} collective-permute-done((f32[4,40,64]{2,1,0:T(8,128)S(1)}, f32[4,40,64]{2,1,0:T(8,128)S(1)}, u32[]{:S(2)}, u32[]{:S(2)}) %collective-permute-start.3) | collective-permute-done | bytes 40992 | tf_op jit(solution)/shard_map/ppermute | solution.py:65
  20.0 0.5 copy.30
  20.5 0.5 copy.31
  21.0 0.0 copy-start
  21.0 0.5 maximum_maximum_fusion.cband_hbm
  21.5 0.0 collective-permute-done.2
  21.6 0.6 %copy-done = f32[32,64,128]{2,1,0:T(8,128)S(1)} copy-done((f32[32,64,128]{2,1,0:T(8,128)S(1)}, f32[32,64,128]{2,1,0:T(8,128)}, u32[]{:S(2)}) %copy-start) | copy-done | bytes 1048600
  22.2 17.6 %shard_map.55 = f32[4,64,128]{2,1,0:T(8,128)S(1)} custom-call(s32[6]{0:T(128)S(1)} %stack.27.lim_ref, f32[24]{0:T(128)S(1)} %pad_maximum_fusion.2.prm_ref, f32[32,64,128]{2,1,0:T(8,128)S(1)} %copy-done, f32[4,64,128]{2,1,0:T(8,128)S(1)} %collective-permute-done.zlo_hbm, f32[4,64,128]{2,1,0:T(8,128)S(1)} %collective-permute-done.1.zhi_hbm, ...), custom_call_target="tpu_custom_call" | custom-call | flops 133693440 | bytes 3080192 | tf_op jit(solution)/shard_map/pallas_call | solution.py:195
  39.8 12.9 %all_to_all.5 = f32[4,8,8,128]{3,2,0,1:T(8,128)S(1)} all-to-all(f32[4,8,8,128]{3,2,0,1:T(8,128)S(1)} %copy.32), channel_id=1, replica_groups=mesh['gx'=2,'gy'=2,'gz'=8] {'gz'}, dimensions={1} | all-to-all | bytes 262144 | tf_op jit(solution)/shard_map/all_to_all | solution.py:249
  52.7 0.6 %pad_maximum_fusion.1 = f32[4,8,128]{2,1,0:T(8,128)} fusion(f32[1,8,128]{2,1,0:T(8,128)S(1)} %get-tuple-element.13, f32[3,8,128]{2,1,0:T(8,128)S(1)} %fusion.2), kind=kLoop, calls=%fused_computation.14 | loop fusion | flops 4096 | bytes 32768 | tf_op jit(solution)/shard_map/concatenate | solution.py:256
  (12 shorter events, 0.2 us)
Async XLA Ops:
  1.0 8.0 %collective-permute-start = (f32[4,64,128]{2,1,0:T(8,128)S(1)}, f32[4,64,128]{2,1,0:T(8,128)S(1)}, u32[]{:S(2)}, u32[]{:S(2)}) collective-permute-start(f32[4,64,128]{2,1,0:T(8,128)S(1)} %get-tuple-element.10), channel_id=1, source_target_pairs={{0,1},{1,2},{2,3},{3,4},{4,5},{5,6},{6,7},{8,9},{9,10},{10,11},{11... | collective-permute-start | bytes 393224 | tf_op jit(solution)/shard_map/ppermute | solution.py:65
  5.9 6.9 %collective-permute-start.1 = (f32[4,64,128]{2,1,0:T(8,128)S(1)}, f32[4,64,128]{2,1,0:T(8,128)S(1)}, u32[]{:S(2)}, u32[]{:S(2)}) collective-permute-start(f32[4,64,128]{2,1,0:T(8,128)S(1)} %get-tuple-element.9), channel_id=1, source_target_pairs={{1,0},{2,1},{3,2},{4,3},{5,4},{6,5},{7,6},{9,8},{10,9},{11,10},{12... | collective-permute-start | bytes 393224 | tf_op jit(solution)/shard_map/ppermute | solution.py:65
  12.9 4.8 %collective-permute-start.4 = (f32[40,4,4]{2,1,0:T(4,128)S(1)}, f32[40,4,4]{2,1,0:T(4,128)S(1)}, u32[]{:S(2)}, u32[]{:S(2)}) collective-permute-start(f32[40,4,4]{2,1,0:T(4,128)S(1)} %slice_select_fusion.1), channel_id=1, source_target_pairs={{0,24},{8,16},{16,8},{24,0},{1,25},{9,17},{17,9},{25,1},{2,26},{10... | collective-permute-start | bytes 7688 | tf_op jit(solution)/shard_map/ppermute | solution.py:65
  13.4 8.1 %collective-permute-start.2 = (f32[40,4,128]{2,1,0:T(4,128)S(1)}, f32[40,4,128]{2,1,0:T(4,128)S(1)}, u32[]{:S(2)}, u32[]{:S(2)}) collective-permute-start(f32[40,4,128]{2,1,0:T(4,128)S(1)} %slice_select_fusion.2), channel_id=1, source_target_pairs={{0,16},{16,0},{1,17},{17,1},{2,18},{18,2},{3,19},{19,3},{4,20},{20... | collective-permute-start | bytes 245768 | tf_op jit(solution)/shard_map/ppermute | solution.py:65
  15.5 4.5 %collective-permute-start.3 = (f32[4,40,64]{2,1,0:T(8,128)S(1)}, f32[4,40,64]{2,1,0:T(8,128)S(1)}, u32[]{:S(2)}, u32[]{:S(2)}) collective-permute-start(f32[4,40,64]{2,1,0:T(8,128)S(1)} %copy.29), channel_id=1, source_target_pairs={{0,8},{8,0},{1,9},{9,1},{2,10},{10,2},{3,11},{11,3},{4,12},{12,4},... | collective-permute-start | bytes 122888 | tf_op jit(solution)/shard_map/ppermute | solution.py:65
  21.0 1.2 %copy-start = (f32[32,64,128]{2,1,0:T(8,128)S(1)}, f32[32,64,128]{2,1,0:T(8,128)}, u32[]{:S(2)}) copy-start(f32[32,64,128]{2,1,0:T(8,128)} %x_hbm.1) | copy-start | bytes 3145732

commit v15 on v12

--- a/solution.py
+++ b/solution.py
@@ -202,7 +202,7 @@
             pltpu.VMEM((MATERIALS, r_in, l_in), jnp.float32),
             pltpu.SemaphoreType.DMA((5,)),
         ],
-        compiler_params=pltpu.CompilerParams(vmem_limit_bytes=48 * 1024 * 1024),
+        compiler_params=pltpu.CompilerParams(vmem_limit_bytes=67043328),
         cost_estimate=pl.CostEstimate(
             flops=int(cells * STEPS * 40 + d_in * r_in * l_in * 60),
             transcendentals=int(d_in * r_in * l_in * (MATERIALS + 1)),

time: 53.2 us -> 58 us (1.090)
  Pallas kernels: 17.1 us -> 19.4 us
  other arithmetic: 2.59 us -> 4.88 us
  local copies, waits for them, and re-layouts: 5.28 us -> 6.64 us
  waiting for transfers between devices: 6.33 us -> 5.2 us
    pallas_call x1, Pallas kernels: 17.1 us -> 19.4 us  [render_block(): pl.pallas_call(kernel, out_shape=jax.ShapeDtypeStruct((CHANNELS + 1, r_in...]
    ppermute x5, waiting for transfers between devices: 6.33 us -> 5.2 us  [halo_stage(): got = lax.ppermute(piece, tuple((a for a, _, _ in used)), pairs)]
    concatenate x1, other arithmetic: 0.5 us -> 1.62 us  [shards(): cband = jnp.concatenate([right, fill, left], axis=2)]
    reshape x1, local copies, waits for them, and re-layouts: 0.01 us -> 0.91 us  [shards(): parts = seg.reshape(CHANNELS + 1, groups, rows_part, col_cells)]
    concatenate x1, other arithmetic: 0.04 us -> 0.71 us  [shards(): rband = jnp.concatenate([plane('hi', 'mid'), plane('lo', 'mid')], axis=1)]
    unnamed x4 -> x6, local copies, waits for them, and re-layouts: 1.95 us -> 1.85 us
  transfers between devices with their start and end apart: 5 -> 5, of which waited for: 3 -> 3; matrix products, arithmetic and copies ran while one was open for 10% -> 13% of each run, Pallas kernels for 0% -> 0%
where the time goes in v15:
time: 58 us; the launch traced here: 57.7 us
  Pallas kernels  19.4 us (33%)
  blocking collectives  12.9 us (22%)
  starting transfers between devices  8.45 us (15%)
  local copies, waits for them, and re-layouts  6.64 us (11%)
  waiting for transfers between devices  5.2 us (9%)
  other arithmetic  4.88 us (8%)
    pallas_call x1, Pallas kernels, render_block(): pl.pallas_call(kernel, out_shape=jax.ShapeDtypeStruct((CHANNELS + 1, r_in...  19.4 us
    all_to_all x1, blocking collectives, shards(): got = lax.all_to_all(parts, 'gz', 1, 1, tiled=True)  12.9 us
    ppermute x5, starting transfers between devices, halo_stage(): got = lax.ppermute(piece, tuple((a for a, _, _ in used)), pairs)  8.45 us
    ppermute x5, waiting for transfers between devices, halo_stage(): got = lax.ppermute(piece, tuple((a for a, _, _ in used)), pairs)  5.2 us
    unnamed x6, local copies, waits for them, and re-layouts  1.85 us
    concatenate x1, other arithmetic, shards(): cband = jnp.concatenate([right, fill, left], axis=2)  1.62 us
    concatenate x1, other arithmetic, shards(): jnp.concatenate([centres, widths, densities, colours.reshape(-1)])  1.27 us
  transfers between devices with their start and end apart: 5, of which 3 were waited for; matrix products, arithmetic and copies ran while one was open for 13% of the time, Pallas kernels for 0%

profile of v15, /device:TPU:0, one launch (start us, length us, event | category | flops | bytes accessed | tf_op | source)
XLA Modules:
  0.0 57.7 jit_solution(1644061095746210269)
XLA Ops:
  0.0 1.0 %fusion.19 = (f32[4,64,128]{2,1,0:T(8,128)S(1)}, f32[4,64,128]{2,1,0:T(8,128)S(1)}) fusion(f32[32,64,128]{2,1,0:T(8,128)} %x_hbm.1), kind=kLoop, calls=%fused_computation.59 | loop fusion | bytes 524288 | tf_op jit(solution)/shard_map/slice | solution.py:52
  1.0 4.9 %collective-permute-start = (f32[4,64,128]{2,1,0:T(8,128)S(1)}, f32[4,64,128]{2,1,0:T(8,128)S(1)}, u32[]{:S(2)}, u32[]{:S(2)}) collective-permute-start(f32[4,64,128]{2,1,0:T(8,128)S(1)} %get-tuple-element.10), channel_id=1, source_target_pairs={{0,1},{1,2},{2,3},{3,4},{4,5},{5,6},{6,7},{8,9},{9,10},{10,11},{11... | collective-permute-start | bytes 393224 | tf_op jit(solution)/shard_map/ppermute | solution.py:65
  5.9 1.3 %collective-permute-start.1 = (f32[4,64,128]{2,1,0:T(8,128)S(1)}, f32[4,64,128]{2,1,0:T(8,128)S(1)}, u32[]{:S(2)}, u32[]{:S(2)}) collective-permute-start(f32[4,64,128]{2,1,0:T(8,128)S(1)} %get-tuple-element.9), channel_id=1, source_target_pairs={{1,0},{2,1},{3,2},{4,3},{5,4},{6,5},{7,6},{9,8},{10,9},{11,10},{12... | collective-permute-start | bytes 393224 | tf_op jit(solution)/shard_map/ppermute | solution.py:65
  7.3 0.8 %reshape.210 = f32[12]{0:T(128)S(1)} reshape(f32[3,4]{1,0:T(4,128)} %param.9) | data formatting | bytes 96 | tf_op jit(solution)/shard_map/reshape | solution.py:241
  8.0 0.1 pad.5.clone
  8.1 0.7 %stack.27.lim_ref = s32[6]{0:T(128)} concatenate(s32[1]{0:T(128)} %bitcast, s32[1]{0:T(128)} %bitcast.1, s32[1]{0:T(128)} %bitcast.2, s32[1]{0:T(128)} %bitcast.3, s32[1]{0:T(128)} %bitcast.4, s32[1]{0:T(128)} %bitcast.5), dimensions={0} | concatenate | bytes 48 | tf_op jit(solution)/shard_map/stack | solution.py:231
  8.8 1.3 %pad_maximum_fusion.2.prm_ref = f32[24]{0:T(128)} fusion(f32[12]{0:T(128)S(1)} %reshape.210, f32[4]{0:T(128)} %param.8, f32[4]{0:T(128)} %param.7, f32[4]{0:T(128)} %param.6), kind=kLoop, calls=%fused_computation.58 | loop fusion | flops 72 | bytes 192 | tf_op jit(solution)/shard_map/concatenate | solution.py:241
  10.0 0.0 collective-permute-done.zlo_hbm
  10.0 0.0 copy-start
  10.0 1.4 %constant_dynamic-update-slice_fusion.1 = f32[40,64,128]{2,1,0:T(8,128)S(1)} fusion(f32[40,64,128]{2,1,0:T(8,128)S(1)} %constant_dynamic-update-slice_fusion.2, f32[32,64,128]{2,1,0:T(8,128)} %x_hbm.1), kind=kLoop, calls=%fused_computation.38 | loop fusion | bytes 2097152
  11.4 1.3 %collective-permute-done.1.zhi_hbm = f32[4,64,128]{2,1,0:T(8,128)S(1)} collective-permute-done((f32[4,64,128]{2,1,0:T(8,128)S(1)}, f32[4,64,128]{2,1,0:T(8,128)S(1)}, u32[]{:S(2)}, u32[]{:S(2)}) %collective-permute-start.1) | collective-permute-done | bytes 131104 | tf_op jit(solution)/shard_map/ppermute | solution.py:65
  12.8 0.0 copy-start.1
  12.8 0.0 copy-done
  12.8 0.1 slice_select_fusion.1
  12.9 0.5 copy-done.1
  13.4 0.0 collective-permute-start.4
  13.4 0.4 fusion
  13.8 1.7 %collective-permute-start.2 = (f32[40,4,128]{2,1,0:T(4,128)S(1)}, f32[40,4,128]{2,1,0:T(4,128)S(1)}, u32[]{:S(2)}, u32[]{:S(2)}) collective-permute-start(f32[40,4,128]{2,1,0:T(4,128)S(1)} %slice_select_fusion.2), channel_id=1, source_target_pairs={{0,16},{16,0},{1,17},{17,1},{2,18},{18,2},{3,19},{19,3},{4,20},{20... | collective-permute-start | bytes 245768 | tf_op jit(solution)/shard_map/ppermute | solution.py:65
  15.5 0.4 copy.29
  15.9 0.6 %collective-permute-start.3 = (f32[4,40,64]{2,1,0:T(8,128)S(1)}, f32[4,40,64]{2,1,0:T(8,128)S(1)}, u32[]{:S(2)}, u32[]{:S(2)}) collective-permute-start(f32[4,40,64]{2,1,0:T(8,128)S(1)} %copy.29), channel_id=1, source_target_pairs={{0,8},{8,0},{1,9},{9,1},{2,10},{10,2},{3,11},{11,3},{4,12},{12,4},... | collective-permute-start | bytes 122888 | tf_op jit(solution)/shard_map/ppermute | solution.py:65
  16.5 1.6 %collective-permute-done.4 = f32[40,4,4]{2,1,0:T(4,128)S(1)} collective-permute-done((f32[40,4,4]{2,1,0:T(4,128)S(1)}, f32[40,4,4]{2,1,0:T(4,128)S(1)}, u32[]{:S(2)}, u32[]{:S(2)}) %collective-permute-start.4) | collective-permute-done | bytes 2592 | tf_op jit(solution)/shard_map/ppermute | solution.py:65
  18.1 0.1 broadcast_select_fusion.3
  18.2 2.3 %collective-permute-done.3 = f32[4,40,64]{2,1,0:T(8,128)S(1)} collective-permute-done((f32[4,40,64]{2,1,0:T(8,128)S(1)}, f32[4,40,64]{2,1,0:T(8,128)S(1)}, u32[]{:S(2)}, u32[]{:S(2)}) %collective-permute-start.3) | collective-permute-done | bytes 40992 | tf_op jit(solution)/shard_map/ppermute | solution.py:65
  20.4 0.5 copy.30
  20.9 0.5 copy.31
  21.4 1.6 %maximum_maximum_fusion.cband_hbm = f32[40,72,128]{2,1,0:T(8,128)} fusion(f32[40,4,4]{2,1,0:T(4,128)S(1)} %get-tuple-element.20, f32[40,4,4]{2,1,0:T(4,128)S(1)} %get-tuple-element.21, f32[40,64,4]{2,1,0:T(8,128)S(1)} %bitcast.86, f32[40,4,4]{2,1,0:T(4,128)S(1)} %get-tuple-element.22, f32[40,4,4]{2,1,0:T(4,128)S(1)} %get-tuple-element.19, ...), kind=kLoop, calls=%fused_computation | loop fusion | flops 2211840 | bytes 1567232 | tf_op jit(solution)/shard_map/concatenate | solution.py:226
  23.0 0.0 collective-permute-done.2
  23.1 0.7 %pad_maximum_fusion.rband_hbm = f32[40,8,128]{2,1,0:T(8,128)} fusion(f32[40,4,128]{2,1,0:T(4,128)S(1)} %get-tuple-element.24, f32[40,4,128]{2,1,0:T(4,128)S(1)} %get-tuple-element.23), kind=kLoop, calls=%fused_computation.3 | loop fusion | flops 40960 | bytes 327680 | tf_op jit(solution)/shard_map/concatenate | solution.py:222
  23.8 19.4 %shard_map.55 = f32[4,64,128]{2,1,0:T(8,128)} custom-call(s32[6]{0:T(128)} %stack.27.lim_ref, f32[24]{0:T(128)} %pad_maximum_fusion.2.prm_ref, f32[32,64,128]{2,1,0:T(8,128)} %x_hbm.1, f32[4,64,128]{2,1,0:T(8,128)} %copy-done, f32[4,64,128]{2,1,0:T(8,128)} %copy-done.1, f32[40,8,128]{2,1,0:T(8,128)} %pad_maximum_fusion.rband_hbm, ...), custom_call_target="tpu_custom_call" | custom-call | flops 133693440 | bytes 3080192 | tf_op jit(solution)/shard_map/pallas_call | solution.py:193
  43.2 0.9 %copy.32 = f32[4,8,8,128]{3,2,0,1:T(8,128)S(1)} copy(f32[4,8,8,128]{3,2,1,0:T(8,128)} %bitcast.87) | data formatting | bytes 262144 | tf_op jit(solution)/shard_map/reshape | solution.py:246
  44.1 12.9 %all_to_all.5 = f32[4,8,8,128]{3,2,0,1:T(8,128)S(1)} all-to-all(f32[4,8,8,128]{3,2,0,1:T(8,128)S(1)} %copy.32), channel_id=1, replica_groups=mesh['gx'=2,'gy'=2,'gz'=8] {'gz'}, dimensions={1} | all-to-all | bytes 262144 | tf_op jit(solution)/shard_map/all_to_all | solution.py:247
  57.0 0.6 %pad_maximum_fusion.1 = f32[4,8,128]{2,1,0:T(8,128)} fusion(f32[1,8,128]{2,1,0:T(8,128)S(1)} %get-tuple-element.13, f32[3,8,128]{2,1,0:T(8,128)S(1)} %fusion.2), kind=kLoop, calls=%fused_computation.14 | loop fusion | flops 4096 | bytes 32768 | tf_op jit(solution)/shard_map/concatenate | solution.py:254
  (10 shorter events, 0.1 us)
Async XLA Ops:
  1.0 9.0 %collective-permute-start = (f32[4,64,128]{2,1,0:T(8,128)S(1)}, f32[4,64,128]{2,1,0:T(8,128)S(1)}, u32[]{:S(2)}, u32[]{:S(2)}) collective-permute-start(f32[4,64,128]{2,1,0:T(8,128)S(1)} %get-tuple-element.10), channel_id=1, source_target_pairs={{0,1},{1,2},{2,3},{3,4},{4,5},{5,6},{6,7},{8,9},{9,10},{10,11},{11... | collective-permute-start | bytes 393224 | tf_op jit(solution)/shard_map/ppermute | solution.py:65
  5.9 6.9 %collective-permute-start.1 = (f32[4,64,128]{2,1,0:T(8,128)S(1)}, f32[4,64,128]{2,1,0:T(8,128)S(1)}, u32[]{:S(2)}, u32[]{:S(2)}) collective-permute-start(f32[4,64,128]{2,1,0:T(8,128)S(1)} %get-tuple-element.9), channel_id=1, source_target_pairs={{1,0},{2,1},{3,2},{4,3},{5,4},{6,5},{7,6},{9,8},{10,9},{11,10},{12... | collective-permute-start | bytes 393224 | tf_op jit(solution)/shard_map/ppermute | solution.py:65
  10.0 2.8 %copy-start = (f32[4,64,128]{2,1,0:T(8,128)}, f32[4,64,128]{2,1,0:T(8,128)S(1)}, u32[]{:S(2)}) copy-start(f32[4,64,128]{2,1,0:T(8,128)S(1)} %collective-permute-done.zlo_hbm) | copy-start | bytes 393220
  12.8 0.6 %copy-start.1 = (f32[4,64,128]{2,1,0:T(8,128)}, f32[4,64,128]{2,1,0:T(8,128)S(1)}, u32[]{:S(2)}) copy-start(f32[4,64,128]{2,1,0:T(8,128)S(1)} %collective-permute-done.1.zhi_hbm) | copy-start | bytes 393220
  13.4 4.7 %collective-permute-start.4 = (f32[40,4,4]{2,1,0:T(4,128)S(1)}, f32[40,4,4]{2,1,0:T(4,128)S(1)}, u32[]{:S(2)}, u32[]{:S(2)}) collective-permute-start(f32[40,4,4]{2,1,0:T(4,128)S(1)} %slice_select_fusion.1), channel_id=1, source_target_pairs={{0,24},{8,16},{16,8},{24,0},{1,25},{9,17},{17,9},{25,1},{2,26},{10... | collective-permute-start | bytes 7688 | tf_op jit(solution)/shard_map/ppermute | solution.py:65
  13.8 9.2 %collective-permute-start.2 = (f32[40,4,128]{2,1,0:T(4,128)S(1)}, f32[40,4,128]{2,1,0:T(4,128)S(1)}, u32[]{:S(2)}, u32[]{:S(2)}) collective-permute-start(f32[40,4,128]{2,1,0:T(4,128)S(1)} %slice_select_fusion.2), channel_id=1, source_target_pairs={{0,16},{16,0},{1,17},{17,1},{2,18},{18,2},{3,19},{19,3},{4,20},{20... | collective-permute-start | bytes 245768 | tf_op jit(solution)/shard_map/ppermute | solution.py:65
  15.9 4.5 %collective-permute-start.3 = (f32[4,40,64]{2,1,0:T(8,128)S(1)}, f32[4,40,64]{2,1,0:T(8,128)S(1)}, u32[]{:S(2)}, u32[]{:S(2)}) collective-permute-start(f32[4,40,64]{2,1,0:T(8,128)S(1)} %copy.29), channel_id=1, source_target_pairs={{0,8},{8,0},{1,9},{9,1},{2,10},{10,2},{3,11},{11,3},{4,12},{12,4},... | collective-permute-start | bytes 122888 | tf_op jit(solution)/shard_map/ppermute | solution.py:65

commit v16 on v12

--- a/solution.py
+++ b/solution.py
@@ -179,7 +179,7 @@
         out_ref[CHANNELS] = run + ext
         return g
 
-    lax.fori_loop(z0, z1, final, g0, unroll=4)
+    lax.fori_loop(z0, z1, final, g0, unroll=8)
     for ch in range(CHANNELS):
         emit = col[ch][0] * acc_ref[0] + col[ch][1] * acc_ref[1] + col[ch][2] * acc_ref[2] + col[ch][3] * acc_ref[3]
         out_ref[ch] = h * emit

time: 53.2 us -> 53 us (level)
  no operation moved by 1% of the time
where the time goes in v16:
time: 53 us; the launch traced here: 52.7 us
  Pallas kernels  16.9 us (32%)
  blocking collectives  12.9 us (24%)
  starting transfers between devices  8.51 us (16%)
  waiting for transfers between devices  6.33 us (12%)
  local copies, waits for them, and re-layouts  5.28 us (10%)
  other arithmetic  2.59 us (5%)
    pallas_call x1, Pallas kernels, render_block(): pl.pallas_call(kernel, out_shape=jax.ShapeDtypeStruct((CHANNELS + 1, r_in...  16.9 us
    all_to_all x1, blocking collectives, shards(): got = lax.all_to_all(parts, 'gz', 1, 1, tiled=True)  12.9 us
    ppermute x5, starting transfers between devices, halo_stage(): got = lax.ppermute(piece, tuple((a for a, _, _ in used)), pairs)  8.51 us
    ppermute x5, waiting for transfers between devices, halo_stage(): got = lax.ppermute(piece, tuple((a for a, _, _ in used)), pairs)  6.33 us
    unnamed x4, local copies, waits for them, and re-layouts  1.95 us
  transfers between devices with their start and end apart: 5, of which 3 were waited for; matrix products, arithmetic and copies ran while one was open for 10% of the time, Pallas kernels for 0%

profile of v16, /device:TPU:0, one launch (start us, length us, event | category | flops | bytes accessed | tf_op | source)
XLA Modules:
  0.0 52.7 jit_solution(15329178853153574770)
XLA Ops:
  0.0 1.0 %fusion.19 = (f32[4,64,128]{2,1,0:T(8,128)S(1)}, f32[4,64,128]{2,1,0:T(8,128)S(1)}) fusion(f32[32,64,128]{2,1,0:T(8,128)} %x_hbm.1), kind=kLoop, calls=%fused_computation.59 | loop fusion | bytes 524288 | tf_op jit(solution)/shard_map/slice | solution.py:52
  1.0 4.9 %collective-permute-start = (f32[4,64,128]{2,1,0:T(8,128)S(1)}, f32[4,64,128]{2,1,0:T(8,128)S(1)}, u32[]{:S(2)}, u32[]{:S(2)}) collective-permute-start(f32[4,64,128]{2,1,0:T(8,128)S(1)} %get-tuple-element.10), channel_id=1, source_target_pairs={{0,1},{1,2},{2,3},{3,4},{4,5},{5,6},{6,7},{8,9},{9,10},{10,11},{11... | collective-permute-start | bytes 393224 | tf_op jit(solution)/shard_map/ppermute | solution.py:65
  5.9 1.3 %collective-permute-start.1 = (f32[4,64,128]{2,1,0:T(8,128)S(1)}, f32[4,64,128]{2,1,0:T(8,128)S(1)}, u32[]{:S(2)}, u32[]{:S(2)}) collective-permute-start(f32[4,64,128]{2,1,0:T(8,128)S(1)} %get-tuple-element.9), channel_id=1, source_target_pairs={{1,0},{2,1},{3,2},{4,3},{5,4},{6,5},{7,6},{9,8},{10,9},{11,10},{12... | collective-permute-start | bytes 393224 | tf_op jit(solution)/shard_map/ppermute | solution.py:65
  7.3 0.8 %reshape.210 = f32[12]{0:T(128)S(1)} reshape(f32[3,4]{1,0:T(4,128)} %param.9) | data formatting | bytes 96 | tf_op jit(solution)/shard_map/reshape | solution.py:241
  8.0 0.1 pad.5.clone
  8.1 0.1 stack.27.lim_ref
  8.2 0.8 %pad_maximum_fusion.2.prm_ref = f32[24]{0:T(128)S(1)} fusion(f32[12]{0:T(128)S(1)} %reshape.210, f32[4]{0:T(128)} %param.8, f32[4]{0:T(128)} %param.7, f32[4]{0:T(128)} %param.6), kind=kLoop, calls=%fused_computation.58 | loop fusion | flops 72 | bytes 192 | tf_op jit(solution)/shard_map/concatenate | solution.py:241
  8.9 0.0 collective-permute-done.zlo_hbm
  9.0 1.3 %constant_dynamic-update-slice_fusion.1 = f32[40,64,128]{2,1,0:T(8,128)S(1)} fusion(f32[40,64,128]{2,1,0:T(8,128)S(1)} %constant_dynamic-update-slice_fusion.2, f32[32,64,128]{2,1,0:T(8,128)} %x_hbm.1), kind=kLoop, calls=%fused_computation.38 | loop fusion | bytes 2097152
  10.3 2.5 %collective-permute-done.1.zhi_hbm = f32[4,64,128]{2,1,0:T(8,128)S(1)} collective-permute-done((f32[4,64,128]{2,1,0:T(8,128)S(1)}, f32[4,64,128]{2,1,0:T(8,128)S(1)}, u32[]{:S(2)}, u32[]{:S(2)}) %collective-permute-start.1) | collective-permute-done | bytes 131104 | tf_op jit(solution)/shard_map/ppermute | solution.py:65
  12.8 0.1 slice_select_fusion.1
  12.9 0.1 collective-permute-start.4
  13.0 0.4 fusion
  13.4 1.7 %collective-permute-start.2 = (f32[40,4,128]{2,1,0:T(4,128)S(1)}, f32[40,4,128]{2,1,0:T(4,128)S(1)}, u32[]{:S(2)}, u32[]{:S(2)}) collective-permute-start(f32[40,4,128]{2,1,0:T(4,128)S(1)} %slice_select_fusion.2), channel_id=1, source_target_pairs={{0,16},{16,0},{1,17},{17,1},{2,18},{18,2},{3,19},{19,3},{4,20},{20... | collective-permute-start | bytes 245768 | tf_op jit(solution)/shard_map/ppermute | solution.py:65
  15.1 0.5 copy.29
  15.5 0.6 %collective-permute-start.3 = (f32[4,40,64]{2,1,0:T(8,128)S(1)}, f32[4,40,64]{2,1,0:T(8,128)S(1)}, u32[]{:S(2)}, u32[]{:S(2)}) collective-permute-start(f32[4,40,64]{2,1,0:T(8,128)S(1)} %copy.29), channel_id=1, source_target_pairs={{0,8},{8,0},{1,9},{9,1},{2,10},{10,2},{3,11},{11,3},{4,12},{12,4},... | collective-permute-start | bytes 122888 | tf_op jit(solution)/shard_map/ppermute | solution.py:65
  16.1 1.6 %collective-permute-done.4 = f32[40,4,4]{2,1,0:T(4,128)S(1)} collective-permute-done((f32[40,4,4]{2,1,0:T(4,128)S(1)}, f32[40,4,4]{2,1,0:T(4,128)S(1)}, u32[]{:S(2)}, u32[]{:S(2)}) %collective-permute-start.4) | collective-permute-done | bytes 2592 | tf_op jit(solution)/shard_map/ppermute | solution.py:65
  17.7 0.1 broadcast_select_fusion.3
  17.7 2.3 %collective-permute-done.3 = f32[4,40,64]{2,1,0:T(8,128)S(1)} collective-permute-done((f32[4,40,64]{2,1,0:T(8,128)S(1)}, f32[4,40,64]{2,1,0:T(8,128)S(1)}, u32[]{:S(2)}, u32[]{:S(2)}) %collective-permute-start.3) | collective-permute-done | bytes 40992 | tf_op jit(solution)/shard_map/ppermute | solution.py:65
  20.0 0.5 copy.30
  20.5 0.5 copy.31
  21.0 0.0 copy-start
  21.0 0.5 maximum_maximum_fusion.cband_hbm
  21.5 0.0 collective-permute-done.2
  21.6 0.6 %copy-done = f32[32,64,128]{2,1,0:T(8,128)S(1)} copy-done((f32[32,64,128]{2,1,0:T(8,128)S(1)}, f32[32,64,128]{2,1,0:T(8,128)}, u32[]{:S(2)}) %copy-start) | copy-done | bytes 1048600
  22.2 16.9 %shard_map.55 = f32[4,64,128]{2,1,0:T(8,128)S(1)} custom-call(s32[6]{0:T(128)S(1)} %stack.27.lim_ref, f32[24]{0:T(128)S(1)} %pad_maximum_fusion.2.prm_ref, f32[32,64,128]{2,1,0:T(8,128)S(1)} %copy-done, f32[4,64,128]{2,1,0:T(8,128)S(1)} %collective-permute-done.zlo_hbm, f32[4,64,128]{2,1,0:T(8,128)S(1)} %collective-permute-done.1.zhi_hbm, ...), custom_call_target="tpu_custom_call" | custom-call | flops 133693440 | bytes 3080192 | tf_op jit(solution)/shard_map/pallas_call | solution.py:193
  39.2 12.9 %all_to_all.5 = f32[4,8,8,128]{3,2,0,1:T(8,128)S(1)} all-to-all(f32[4,8,8,128]{3,2,0,1:T(8,128)S(1)} %copy.32), channel_id=1, replica_groups=mesh['gx'=2,'gy'=2,'gz'=8] {'gz'}, dimensions={1} | all-to-all | bytes 262144 | tf_op jit(solution)/shard_map/all_to_all | solution.py:247
  52.1 0.6 %pad_maximum_fusion.1 = f32[4,8,128]{2,1,0:T(8,128)} fusion(f32[1,8,128]{2,1,0:T(8,128)S(1)} %get-tuple-element.13, f32[3,8,128]{2,1,0:T(8,128)S(1)} %fusion.2), kind=kLoop, calls=%fused_computation.14 | loop fusion | flops 4096 | bytes 32768 | tf_op jit(solution)/shard_map/concatenate | solution.py:254
  (12 shorter events, 0.2 us)
Async XLA Ops:
  1.0 8.0 %collective-permute-start = (f32[4,64,128]{2,1,0:T(8,128)S(1)}, f32[4,64,128]{2,1,0:T(8,128)S(1)}, u32[]{:S(2)}, u32[]{:S(2)}) collective-permute-start(f32[4,64,128]{2,1,0:T(8,128)S(1)} %get-tuple-element.10), channel_id=1, source_target_pairs={{0,1},{1,2},{2,3},{3,4},{4,5},{5,6},{6,7},{8,9},{9,10},{10,11},{11... | collective-permute-start | bytes 393224 | tf_op jit(solution)/shard_map/ppermute | solution.py:65
  5.9 6.9 %collective-permute-start.1 = (f32[4,64,128]{2,1,0:T(8,128)S(1)}, f32[4,64,128]{2,1,0:T(8,128)S(1)}, u32[]{:S(2)}, u32[]{:S(2)}) collective-permute-start(f32[4,64,128]{2,1,0:T(8,128)S(1)} %get-tuple-element.9), channel_id=1, source_target_pairs={{1,0},{2,1},{3,2},{4,3},{5,4},{6,5},{7,6},{9,8},{10,9},{11,10},{12... | collective-permute-start | bytes 393224 | tf_op jit(solution)/shard_map/ppermute | solution.py:65
  12.9 4.8 %collective-permute-start.4 = (f32[40,4,4]{2,1,0:T(4,128)S(1)}, f32[40,4,4]{2,1,0:T(4,128)S(1)}, u32[]{:S(2)}, u32[]{:S(2)}) collective-permute-start(f32[40,4,4]{2,1,0:T(4,128)S(1)} %slice_select_fusion.1), channel_id=1, source_target_pairs={{0,24},{8,16},{16,8},{24,0},{1,25},{9,17},{17,9},{25,1},{2,26},{10... | collective-permute-start | bytes 7688 | tf_op jit(solution)/shard_map/ppermute | solution.py:65
  13.4 8.1 %collective-permute-start.2 = (f32[40,4,128]{2,1,0:T(4,128)S(1)}, f32[40,4,128]{2,1,0:T(4,128)S(1)}, u32[]{:S(2)}, u32[]{:S(2)}) collective-permute-start(f32[40,4,128]{2,1,0:T(4,128)S(1)} %slice_select_fusion.2), channel_id=1, source_target_pairs={{0,16},{16,0},{1,17},{17,1},{2,18},{18,2},{3,19},{19,3},{4,20},{20... | collective-permute-start | bytes 245768 | tf_op jit(solution)/shard_map/ppermute | solution.py:65
  15.5 4.5 %collective-permute-start.3 = (f32[4,40,64]{2,1,0:T(8,128)S(1)}, f32[4,40,64]{2,1,0:T(8,128)S(1)}, u32[]{:S(2)}, u32[]{:S(2)}) collective-permute-start(f32[4,40,64]{2,1,0:T(8,128)S(1)} %copy.29), channel_id=1, source_target_pairs={{0,8},{8,0},{1,9},{9,1},{2,10},{10,2},{3,11},{11,3},{4,12},{12,4},... | collective-permute-start | bytes 122888 | tf_op jit(solution)/shard_map/ppermute | solution.py:65
  21.0 1.2 %copy-start = (f32[32,64,128]{2,1,0:T(8,128)S(1)}, f32[32,64,128]{2,1,0:T(8,128)}, u32[]{:S(2)}) copy-start(f32[32,64,128]{2,1,0:T(8,128)} %x_hbm.1) | copy-start | bytes 3145732

commit v17 on v12

--- a/solution.py
+++ b/solution.py
@@ -125,7 +125,8 @@
     row_at = jnp.where(row < r_in + halo, row, row - rows)
     lane_at = jnp.where(lane < (l_in + lanes) // 2, lane, lane - lanes)
     ok = (row_at >= lim_ref[2]) & (row_at < lim_ref[3]) & (lane_at >= lim_ref[4]) & (lane_at < lim_ref[5])
-    m_ref[...] = jnp.where(ok, 1.0, 0.0).astype(jnp.float32)
+    m_ref[0] = jnp.zeros((rows, lanes), jnp.float32)
+    m_ref[1] = jnp.where(ok, 1.0, 0.0).astype(jnp.float32)
 
     cen = [prm_ref[k] for k in range(MATERIALS)]
     wid = [prm_ref[MATERIALS + k] for k in range(MATERIALS)]
@@ -148,9 +149,8 @@
             fr = flux(pltpu.roll(c, rows - 1, 0) - c, RATE_PLANE)
             fc = flux(pltpu.roll(c, lanes - 1, 1) - c, RATE_PLANE)
             new = c + (g - g_prev) + (fr - pltpu.roll(fr, 1, 0)) + (fc - pltpu.roll(fc, 1, 1))
-            inside = (z >= lim_ref[0]) & (z < lim_ref[1])
-            zf = jnp.where(inside, 1.0, 0.0).astype(jnp.float32)
-            dst[z] = new * (m_ref[...] * zf)
+            inside = ((z >= lim_ref[0]) & (z < lim_ref[1])).astype(jnp.int32)
+            dst[z] = new * m_ref[inside]
             return g
 
         lax.fori_loop(z0, z1, body, g0, unroll=8)
@@ -198,7 +198,7 @@
         scratch_shapes=[
             pltpu.VMEM((depth, rows, lanes), jnp.float32),
             pltpu.VMEM((depth, rows, lanes), jnp.float32),
-            pltpu.VMEM((rows, lanes), jnp.float32),
+            pltpu.VMEM((2, rows, lanes), jnp.float32),
             pltpu.VMEM((MATERIALS, r_in, l_in), jnp.float32),
             pltpu.SemaphoreType.DMA((5,)),
         ],

time: 53.2 us -> 53.2 us (level)
  no operation moved by 1% of the time
where the time goes in v17:
time: 53.2 us; the launch traced here: 52.9 us
  Pallas kernels  17.1 us (32%)
  blocking collectives  12.9 us (24%)
  starting transfers between devices  8.51 us (16%)
  waiting for transfers between devices  6.33 us (12%)
  local copies, waits for them, and re-layouts  5.28 us (10%)
  other arithmetic  2.59 us (5%)
    pallas_call x1, Pallas kernels, render_block(): pl.pallas_call(kernel, out_shape=jax.ShapeDtypeStruct((CHANNELS + 1, r_in...  17.1 us
    all_to_all x1, blocking collectives, shards(): got = lax.all_to_all(parts, 'gz', 1, 1, tiled=True)  12.9 us
    ppermute x5, starting transfers between devices, halo_stage(): got = lax.ppermute(piece, tuple((a for a, _, _ in used)), pairs)  8.51 us
    ppermute x5, waiting for transfers between devices, halo_stage(): got = lax.ppermute(piece, tuple((a for a, _, _ in used)), pairs)  6.33 us
    unnamed x4, local copies, waits for them, and re-layouts  1.95 us
  transfers between devices with their start and end apart: 5, of which 3 were waited for; matrix products, arithmetic and copies ran while one was open for 10% of the time, Pallas kernels for 0%

profile of v17, /device:TPU:0, one launch (start us, length us, event | category | flops | bytes accessed | tf_op | source)
XLA Modules:
  0.0 52.9 jit_solution(3794022469692401608)
XLA Ops:
  0.0 1.0 %fusion.19 = (f32[4,64,128]{2,1,0:T(8,128)S(1)}, f32[4,64,128]{2,1,0:T(8,128)S(1)}) fusion(f32[32,64,128]{2,1,0:T(8,128)} %x_hbm.1), kind=kLoop, calls=%fused_computation.59 | loop fusion | bytes 524288 | tf_op jit(solution)/shard_map/slice | solution.py:52
  1.0 4.9 %collective-permute-start = (f32[4,64,128]{2,1,0:T(8,128)S(1)}, f32[4,64,128]{2,1,0:T(8,128)S(1)}, u32[]{:S(2)}, u32[]{:S(2)}) collective-permute-start(f32[4,64,128]{2,1,0:T(8,128)S(1)} %get-tuple-element.10), channel_id=1, source_target_pairs={{0,1},{1,2},{2,3},{3,4},{4,5},{5,6},{6,7},{8,9},{9,10},{10,11},{11... | collective-permute-start | bytes 393224 | tf_op jit(solution)/shard_map/ppermute | solution.py:65
  5.9 1.3 %collective-permute-start.1 = (f32[4,64,128]{2,1,0:T(8,128)S(1)}, f32[4,64,128]{2,1,0:T(8,128)S(1)}, u32[]{:S(2)}, u32[]{:S(2)}) collective-permute-start(f32[4,64,128]{2,1,0:T(8,128)S(1)} %get-tuple-element.9), channel_id=1, source_target_pairs={{1,0},{2,1},{3,2},{4,3},{5,4},{6,5},{7,6},{9,8},{10,9},{11,10},{12... | collective-permute-start | bytes 393224 | tf_op jit(solution)/shard_map/ppermute | solution.py:65
  7.3 0.8 %reshape.210 = f32[12]{0:T(128)S(1)} reshape(f32[3,4]{1,0:T(4,128)} %param.9) | data formatting | bytes 96 | tf_op jit(solution)/shard_map/reshape | solution.py:241
  8.0 0.1 pad.5.clone
  8.1 0.1 stack.27.lim_ref
  8.2 0.8 %pad_maximum_fusion.2.prm_ref = f32[24]{0:T(128)S(1)} fusion(f32[12]{0:T(128)S(1)} %reshape.210, f32[4]{0:T(128)} %param.8, f32[4]{0:T(128)} %param.7, f32[4]{0:T(128)} %param.6), kind=kLoop, calls=%fused_computation.58 | loop fusion | flops 72 | bytes 192 | tf_op jit(solution)/shard_map/concatenate | solution.py:241
  8.9 0.0 collective-permute-done.zlo_hbm
  9.0 1.3 %constant_dynamic-update-slice_fusion.1 = f32[40,64,128]{2,1,0:T(8,128)S(1)} fusion(f32[40,64,128]{2,1,0:T(8,128)S(1)} %constant_dynamic-update-slice_fusion.2, f32[32,64,128]{2,1,0:T(8,128)} %x_hbm.1), kind=kLoop, calls=%fused_computation.38 | loop fusion | bytes 2097152
  10.3 2.5 %collective-permute-done.1.zhi_hbm = f32[4,64,128]{2,1,0:T(8,128)S(1)} collective-permute-done((f32[4,64,128]{2,1,0:T(8,128)S(1)}, f32[4,64,128]{2,1,0:T(8,128)S(1)}, u32[]{:S(2)}, u32[]{:S(2)}) %collective-permute-start.1) | collective-permute-done | bytes 131104 | tf_op jit(solution)/shard_map/ppermute | solution.py:65
  12.8 0.1 slice_select_fusion.1
  12.9 0.1 collective-permute-start.4
  13.0 0.4 fusion
  13.4 1.7 %collective-permute-start.2 = (f32[40,4,128]{2,1,0:T(4,128)S(1)}, f32[40,4,128]{2,1,0:T(4,128)S(1)}, u32[]{:S(2)}, u32[]{:S(2)}) collective-permute-start(f32[40,4,128]{2,1,0:T(4,128)S(1)} %slice_select_fusion.2), channel_id=1, source_target_pairs={{0,16},{16,0},{1,17},{17,1},{2,18},{18,2},{3,19},{19,3},{4,20},{20... | collective-permute-start | bytes 245768 | tf_op jit(solution)/shard_map/ppermute | solution.py:65
  15.1 0.5 copy.29
  15.5 0.6 %collective-permute-start.3 = (f32[4,40,64]{2,1,0:T(8,128)S(1)}, f32[4,40,64]{2,1,0:T(8,128)S(1)}, u32[]{:S(2)}, u32[]{:S(2)}) collective-permute-start(f32[4,40,64]{2,1,0:T(8,128)S(1)} %copy.29), channel_id=1, source_target_pairs={{0,8},{8,0},{1,9},{9,1},{2,10},{10,2},{3,11},{11,3},{4,12},{12,4},... | collective-permute-start | bytes 122888 | tf_op jit(solution)/shard_map/ppermute | solution.py:65
  16.1 1.6 %collective-permute-done.4 = f32[40,4,4]{2,1,0:T(4,128)S(1)} collective-permute-done((f32[40,4,4]{2,1,0:T(4,128)S(1)}, f32[40,4,4]{2,1,0:T(4,128)S(1)}, u32[]{:S(2)}, u32[]{:S(2)}) %collective-permute-start.4) | collective-permute-done | bytes 2592 | tf_op jit(solution)/shard_map/ppermute | solution.py:65
  17.7 0.1 broadcast_select_fusion.3
  17.7 2.3 %collective-permute-done.3 = f32[4,40,64]{2,1,0:T(8,128)S(1)} collective-permute-done((f32[4,40,64]{2,1,0:T(8,128)S(1)}, f32[4,40,64]{2,1,0:T(8,128)S(1)}, u32[]{:S(2)}, u32[]{:S(2)}) %collective-permute-start.3) | collective-permute-done | bytes 40992 | tf_op jit(solution)/shard_map/ppermute | solution.py:65
  20.0 0.5 copy.30
  20.5 0.5 copy.31
  21.0 0.0 copy-start
  21.0 0.5 maximum_maximum_fusion.cband_hbm
  21.5 0.0 collective-permute-done.2
  21.6 0.6 %copy-done = f32[32,64,128]{2,1,0:T(8,128)S(1)} copy-done((f32[32,64,128]{2,1,0:T(8,128)S(1)}, f32[32,64,128]{2,1,0:T(8,128)}, u32[]{:S(2)}) %copy-start) | copy-done | bytes 1048600
  22.2 17.1 %shard_map.55 = f32[4,64,128]{2,1,0:T(8,128)S(1)} custom-call(s32[6]{0:T(128)S(1)} %stack.27.lim_ref, f32[24]{0:T(128)S(1)} %pad_maximum_fusion.2.prm_ref, f32[32,64,128]{2,1,0:T(8,128)S(1)} %copy-done, f32[4,64,128]{2,1,0:T(8,128)S(1)} %collective-permute-done.zlo_hbm, f32[4,64,128]{2,1,0:T(8,128)S(1)} %collective-permute-done.1.zhi_hbm, ...), custom_call_target="tpu_custom_call" | custom-call | flops 133693440 | bytes 3080192 | tf_op jit(solution)/shard_map/pallas_call | solution.py:193
  39.4 12.9 %all_to_all.5 = f32[4,8,8,128]{3,2,0,1:T(8,128)S(1)} all-to-all(f32[4,8,8,128]{3,2,0,1:T(8,128)S(1)} %copy.32), channel_id=1, replica_groups=mesh['gx'=2,'gy'=2,'gz'=8] {'gz'}, dimensions={1} | all-to-all | bytes 262144 | tf_op jit(solution)/shard_map/all_to_all | solution.py:247
  52.3 0.6 %pad_maximum_fusion.1 = f32[4,8,128]{2,1,0:T(8,128)} fusion(f32[1,8,128]{2,1,0:T(8,128)S(1)} %get-tuple-element.13, f32[3,8,128]{2,1,0:T(8,128)S(1)} %fusion.2), kind=kLoop, calls=%fused_computation.14 | loop fusion | flops 4096 | bytes 32768 | tf_op jit(solution)/shard_map/concatenate | solution.py:254
  (12 shorter events, 0.2 us)
Async XLA Ops:
  1.0 8.0 %collective-permute-start = (f32[4,64,128]{2,1,0:T(8,128)S(1)}, f32[4,64,128]{2,1,0:T(8,128)S(1)}, u32[]{:S(2)}, u32[]{:S(2)}) collective-permute-start(f32[4,64,128]{2,1,0:T(8,128)S(1)} %get-tuple-element.10), channel_id=1, source_target_pairs={{0,1},{1,2},{2,3},{3,4},{4,5},{5,6},{6,7},{8,9},{9,10},{10,11},{11... | collective-permute-start | bytes 393224 | tf_op jit(solution)/shard_map/ppermute | solution.py:65
  5.9 6.9 %collective-permute-start.1 = (f32[4,64,128]{2,1,0:T(8,128)S(1)}, f32[4,64,128]{2,1,0:T(8,128)S(1)}, u32[]{:S(2)}, u32[]{:S(2)}) collective-permute-start(f32[4,64,128]{2,1,0:T(8,128)S(1)} %get-tuple-element.9), channel_id=1, source_target_pairs={{1,0},{2,1},{3,2},{4,3},{5,4},{6,5},{7,6},{9,8},{10,9},{11,10},{12... | collective-permute-start | bytes 393224 | tf_op jit(solution)/shard_map/ppermute | solution.py:65
  12.9 4.8 %collective-permute-start.4 = (f32[40,4,4]{2,1,0:T(4,128)S(1)}, f32[40,4,4]{2,1,0:T(4,128)S(1)}, u32[]{:S(2)}, u32[]{:S(2)}) collective-permute-start(f32[40,4,4]{2,1,0:T(4,128)S(1)} %slice_select_fusion.1), channel_id=1, source_target_pairs={{0,24},{8,16},{16,8},{24,0},{1,25},{9,17},{17,9},{25,1},{2,26},{10... | collective-permute-start | bytes 7688 | tf_op jit(solution)/shard_map/ppermute | solution.py:65
  13.4 8.1 %collective-permute-start.2 = (f32[40,4,128]{2,1,0:T(4,128)S(1)}, f32[40,4,128]{2,1,0:T(4,128)S(1)}, u32[]{:S(2)}, u32[]{:S(2)}) collective-permute-start(f32[40,4,128]{2,1,0:T(4,128)S(1)} %slice_select_fusion.2), channel_id=1, source_target_pairs={{0,16},{16,0},{1,17},{17,1},{2,18},{18,2},{3,19},{19,3},{4,20},{20... | collective-permute-start | bytes 245768 | tf_op jit(solution)/shard_map/ppermute | solution.py:65
  15.5 4.5 %collective-permute-start.3 = (f32[4,40,64]{2,1,0:T(8,128)S(1)}, f32[4,40,64]{2,1,0:T(8,128)S(1)}, u32[]{:S(2)}, u32[]{:S(2)}) collective-permute-start(f32[4,40,64]{2,1,0:T(8,128)S(1)} %copy.29), channel_id=1, source_target_pairs={{0,8},{8,0},{1,9},{9,1},{2,10},{10,2},{3,11},{11,3},{4,12},{12,4},... | collective-permute-start | bytes 122888 | tf_op jit(solution)/shard_map/ppermute | solution.py:65
  21.0 1.2 %copy-start = (f32[32,64,128]{2,1,0:T(8,128)S(1)}, f32[32,64,128]{2,1,0:T(8,128)}, u32[]{:S(2)}) copy-start(f32[32,64,128]{2,1,0:T(8,128)} %x_hbm.1) | copy-start | bytes 3145732

commit v18 on v12

--- a/solution.py
+++ b/solution.py
@@ -153,7 +153,7 @@
             dst[z] = new * (m_ref[...] * zf)
             return g
 
-        lax.fori_loop(z0, z1, body, g0, unroll=8)
+        lax.fori_loop(z0, z1, body, g0, unroll=16)
 
     smooth(b_ref, a_ref, 0)
     smooth(a_ref, b_ref, 1)

time: 53.2 us -> 53.3 us (level)
  no operation moved by 1% of the time
where the time goes in v18:
time: 53.3 us; the launch traced here: 53 us
  Pallas kernels  17.3 us (32%)
  blocking collectives  12.9 us (24%)
  starting transfers between devices  8.51 us (16%)
  waiting for transfers between devices  6.33 us (12%)
  local copies, waits for them, and re-layouts  5.28 us (10%)
  other arithmetic  2.59 us (5%)
    pallas_call x1, Pallas kernels, render_block(): pl.pallas_call(kernel, out_shape=jax.ShapeDtypeStruct((CHANNELS + 1, r_in...  17.3 us
    all_to_all x1, blocking collectives, shards(): got = lax.all_to_all(parts, 'gz', 1, 1, tiled=True)  12.9 us
    ppermute x5, starting transfers between devices, halo_stage(): got = lax.ppermute(piece, tuple((a for a, _, _ in used)), pairs)  8.51 us
    ppermute x5, waiting for transfers between devices, halo_stage(): got = lax.ppermute(piece, tuple((a for a, _, _ in used)), pairs)  6.33 us
    unnamed x4, local copies, waits for them, and re-layouts  1.95 us
  transfers between devices with their start and end apart: 5, of which 3 were waited for; matrix products, arithmetic and copies ran while one was open for 10% of the time, Pallas kernels for 0%

profile of v18, /device:TPU:0, one launch (start us, length us, event | category | flops | bytes accessed | tf_op | source)
XLA Modules:
  0.0 53.0 jit_solution(7203298077895244991)
XLA Ops:
  0.0 1.0 %fusion.19 = (f32[4,64,128]{2,1,0:T(8,128)S(1)}, f32[4,64,128]{2,1,0:T(8,128)S(1)}) fusion(f32[32,64,128]{2,1,0:T(8,128)} %x_hbm.1), kind=kLoop, calls=%fused_computation.59 | loop fusion | bytes 524288 | tf_op jit(solution)/shard_map/slice | solution.py:52
  1.0 4.9 %collective-permute-start = (f32[4,64,128]{2,1,0:T(8,128)S(1)}, f32[4,64,128]{2,1,0:T(8,128)S(1)}, u32[]{:S(2)}, u32[]{:S(2)}) collective-permute-start(f32[4,64,128]{2,1,0:T(8,128)S(1)} %get-tuple-element.10), channel_id=1, source_target_pairs={{0,1},{1,2},{2,3},{3,4},{4,5},{5,6},{6,7},{8,9},{9,10},{10,11},{11... | collective-permute-start | bytes 393224 | tf_op jit(solution)/shard_map/ppermute | solution.py:65
  5.9 1.3 %collective-permute-start.1 = (f32[4,64,128]{2,1,0:T(8,128)S(1)}, f32[4,64,128]{2,1,0:T(8,128)S(1)}, u32[]{:S(2)}, u32[]{:S(2)}) collective-permute-start(f32[4,64,128]{2,1,0:T(8,128)S(1)} %get-tuple-element.9), channel_id=1, source_target_pairs={{1,0},{2,1},{3,2},{4,3},{5,4},{6,5},{7,6},{9,8},{10,9},{11,10},{12... | collective-permute-start | bytes 393224 | tf_op jit(solution)/shard_map/ppermute | solution.py:65
  7.3 0.8 %reshape.210 = f32[12]{0:T(128)S(1)} reshape(f32[3,4]{1,0:T(4,128)} %param.9) | data formatting | bytes 96 | tf_op jit(solution)/shard_map/reshape | solution.py:241
  8.0 0.1 pad.5.clone
  8.1 0.1 stack.27.lim_ref
  8.2 0.8 %pad_maximum_fusion.2.prm_ref = f32[24]{0:T(128)S(1)} fusion(f32[12]{0:T(128)S(1)} %reshape.210, f32[4]{0:T(128)} %param.8, f32[4]{0:T(128)} %param.7, f32[4]{0:T(128)} %param.6), kind=kLoop, calls=%fused_computation.58 | loop fusion | flops 72 | bytes 192 | tf_op jit(solution)/shard_map/concatenate | solution.py:241
  8.9 0.0 collective-permute-done.zlo_hbm
  9.0 1.3 %constant_dynamic-update-slice_fusion.1 = f32[40,64,128]{2,1,0:T(8,128)S(1)} fusion(f32[40,64,128]{2,1,0:T(8,128)S(1)} %constant_dynamic-update-slice_fusion.2, f32[32,64,128]{2,1,0:T(8,128)} %x_hbm.1), kind=kLoop, calls=%fused_computation.38 | loop fusion | bytes 2097152
  10.3 2.5 %collective-permute-done.1.zhi_hbm = f32[4,64,128]{2,1,0:T(8,128)S(1)} collective-permute-done((f32[4,64,128]{2,1,0:T(8,128)S(1)}, f32[4,64,128]{2,1,0:T(8,128)S(1)}, u32[]{:S(2)}, u32[]{:S(2)}) %collective-permute-start.1) | collective-permute-done | bytes 131104 | tf_op jit(solution)/shard_map/ppermute | solution.py:65
  12.8 0.1 slice_select_fusion.1
  12.9 0.1 collective-permute-start.4
  13.0 0.4 fusion
  13.4 1.7 %collective-permute-start.2 = (f32[40,4,128]{2,1,0:T(4,128)S(1)}, f32[40,4,128]{2,1,0:T(4,128)S(1)}, u32[]{:S(2)}, u32[]{:S(2)}) collective-permute-start(f32[40,4,128]{2,1,0:T(4,128)S(1)} %slice_select_fusion.2), channel_id=1, source_target_pairs={{0,16},{16,0},{1,17},{17,1},{2,18},{18,2},{3,19},{19,3},{4,20},{20... | collective-permute-start | bytes 245768 | tf_op jit(solution)/shard_map/ppermute | solution.py:65
  15.1 0.5 copy.29
  15.5 0.6 %collective-permute-start.3 = (f32[4,40,64]{2,1,0:T(8,128)S(1)}, f32[4,40,64]{2,1,0:T(8,128)S(1)}, u32[]{:S(2)}, u32[]{:S(2)}) collective-permute-start(f32[4,40,64]{2,1,0:T(8,128)S(1)} %copy.29), channel_id=1, source_target_pairs={{0,8},{8,0},{1,9},{9,1},{2,10},{10,2},{3,11},{11,3},{4,12},{12,4},... | collective-permute-start | bytes 122888 | tf_op jit(solution)/shard_map/ppermute | solution.py:65
  16.1 1.6 %collective-permute-done.4 = f32[40,4,4]{2,1,0:T(4,128)S(1)} collective-permute-done((f32[40,4,4]{2,1,0:T(4,128)S(1)}, f32[40,4,4]{2,1,0:T(4,128)S(1)}, u32[]{:S(2)}, u32[]{:S(2)}) %collective-permute-start.4) | collective-permute-done | bytes 2592 | tf_op jit(solution)/shard_map/ppermute | solution.py:65
  17.7 0.1 broadcast_select_fusion.3
  17.7 2.3 %collective-permute-done.3 = f32[4,40,64]{2,1,0:T(8,128)S(1)} collective-permute-done((f32[4,40,64]{2,1,0:T(8,128)S(1)}, f32[4,40,64]{2,1,0:T(8,128)S(1)}, u32[]{:S(2)}, u32[]{:S(2)}) %collective-permute-start.3) | collective-permute-done | bytes 40992 | tf_op jit(solution)/shard_map/ppermute | solution.py:65
  20.0 0.5 copy.30
  20.5 0.5 copy.31
  21.0 0.0 copy-start
  21.0 0.5 maximum_maximum_fusion.cband_hbm
  21.5 0.0 collective-permute-done.2
  21.6 0.6 %copy-done = f32[32,64,128]{2,1,0:T(8,128)S(1)} copy-done((f32[32,64,128]{2,1,0:T(8,128)S(1)}, f32[32,64,128]{2,1,0:T(8,128)}, u32[]{:S(2)}) %copy-start) | copy-done | bytes 1048600
  22.2 17.3 %shard_map.55 = f32[4,64,128]{2,1,0:T(8,128)S(1)} custom-call(s32[6]{0:T(128)S(1)} %stack.27.lim_ref, f32[24]{0:T(128)S(1)} %pad_maximum_fusion.2.prm_ref, f32[32,64,128]{2,1,0:T(8,128)S(1)} %copy-done, f32[4,64,128]{2,1,0:T(8,128)S(1)} %collective-permute-done.zlo_hbm, f32[4,64,128]{2,1,0:T(8,128)S(1)} %collective-permute-done.1.zhi_hbm, ...), custom_call_target="tpu_custom_call" | custom-call | flops 133693440 | bytes 3080192 | tf_op jit(solution)/shard_map/pallas_call | solution.py:193
  39.5 12.9 %all_to_all.5 = f32[4,8,8,128]{3,2,0,1:T(8,128)S(1)} all-to-all(f32[4,8,8,128]{3,2,0,1:T(8,128)S(1)} %copy.32), channel_id=1, replica_groups=mesh['gx'=2,'gy'=2,'gz'=8] {'gz'}, dimensions={1} | all-to-all | bytes 262144 | tf_op jit(solution)/shard_map/all_to_all | solution.py:247
  52.4 0.6 %pad_maximum_fusion.1 = f32[4,8,128]{2,1,0:T(8,128)} fusion(f32[1,8,128]{2,1,0:T(8,128)S(1)} %get-tuple-element.13, f32[3,8,128]{2,1,0:T(8,128)S(1)} %fusion.2), kind=kLoop, calls=%fused_computation.14 | loop fusion | flops 4096 | bytes 32768 | tf_op jit(solution)/shard_map/concatenate | solution.py:254
  (12 shorter events, 0.2 us)
Async XLA Ops:
  1.0 8.0 %collective-permute-start = (f32[4,64,128]{2,1,0:T(8,128)S(1)}, f32[4,64,128]{2,1,0:T(8,128)S(1)}, u32[]{:S(2)}, u32[]{:S(2)}) collective-permute-start(f32[4,64,128]{2,1,0:T(8,128)S(1)} %get-tuple-element.10), channel_id=1, source_target_pairs={{0,1},{1,2},{2,3},{3,4},{4,5},{5,6},{6,7},{8,9},{9,10},{10,11},{11... | collective-permute-start | bytes 393224 | tf_op jit(solution)/shard_map/ppermute | solution.py:65
  5.9 6.9 %collective-permute-start.1 = (f32[4,64,128]{2,1,0:T(8,128)S(1)}, f32[4,64,128]{2,1,0:T(8,128)S(1)}, u32[]{:S(2)}, u32[]{:S(2)}) collective-permute-start(f32[4,64,128]{2,1,0:T(8,128)S(1)} %get-tuple-element.9), channel_id=1, source_target_pairs={{1,0},{2,1},{3,2},{4,3},{5,4},{6,5},{7,6},{9,8},{10,9},{11,10},{12... | collective-permute-start | bytes 393224 | tf_op jit(solution)/shard_map/ppermute | solution.py:65
  12.9 4.8 %collective-permute-start.4 = (f32[40,4,4]{2,1,0:T(4,128)S(1)}, f32[40,4,4]{2,1,0:T(4,128)S(1)}, u32[]{:S(2)}, u32[]{:S(2)}) collective-permute-start(f32[40,4,4]{2,1,0:T(4,128)S(1)} %slice_select_fusion.1), channel_id=1, source_target_pairs={{0,24},{8,16},{16,8},{24,0},{1,25},{9,17},{17,9},{25,1},{2,26},{10... | collective-permute-start | bytes 7688 | tf_op jit(solution)/shard_map/ppermute | solution.py:65
  13.4 8.1 %collective-permute-start.2 = (f32[40,4,128]{2,1,0:T(4,128)S(1)}, f32[40,4,128]{2,1,0:T(4,128)S(1)}, u32[]{:S(2)}, u32[]{:S(2)}) collective-permute-start(f32[40,4,128]{2,1,0:T(4,128)S(1)} %slice_select_fusion.2), channel_id=1, source_target_pairs={{0,16},{16,0},{1,17},{17,1},{2,18},{18,2},{3,19},{19,3},{4,20},{20... | collective-permute-start | bytes 245768 | tf_op jit(solution)/shard_map/ppermute | solution.py:65
  15.5 4.5 %collective-permute-start.3 = (f32[4,40,64]{2,1,0:T(8,128)S(1)}, f32[4,40,64]{2,1,0:T(8,128)S(1)}, u32[]{:S(2)}, u32[]{:S(2)}) collective-permute-start(f32[4,40,64]{2,1,0:T(8,128)S(1)} %copy.29), channel_id=1, source_target_pairs={{0,8},{8,0},{1,9},{9,1},{2,10},{10,2},{3,11},{11,3},{4,12},{12,4},... | collective-permute-start | bytes 122888 | tf_op jit(solution)/shard_map/ppermute | solution.py:65
  21.0 1.2 %copy-start = (f32[32,64,128]{2,1,0:T(8,128)S(1)}, f32[32,64,128]{2,1,0:T(8,128)}, u32[]{:S(2)}) copy-start(f32[32,64,128]{2,1,0:T(8,128)} %x_hbm.1) | copy-start | bytes 3145732
